TPU v7x, 256 devices: a whole 4x4x8 slice. The times are simulated.
256 devices in a mesh: seq: 16 (over x, y), tensor: 16 (over z, core).
Axes of the slice: x: 4, y: 4, z: 8, core: 2. Of those that a mesh axis runs over, the one named last changes fastest.
Arguments:
- queries: bfloat16 [16384, 4096], P(('seq', 'tensor')), may hold values from -6 to 6
- key_rows: bfloat16 [16384, 4096], P(('seq', 'tensor')), may hold values from -6 to 6
- values: bfloat16 [16384, 4096], P(('seq', 'tensor')), may hold values from -6 to 6
- input_gate: bfloat16 [16384, 4], P(('seq', 'tensor')), may hold values from -3 to 1
- forget_gate: bfloat16 [16384, 4], P(('seq', 'tensor')), may hold values from 0 to 16
- segment_ids: int32 [16384], P('seq'), may hold values from 0 to 3, never falling along the last dimension, each value on 1 to 8192 neighbouring positions
- output_gate: bfloat16 [16384, 4096], P(('seq', 'tensor')), may hold values from -6 to 6
- norm_gain: float32 [4096], replicated, may hold values from 0.5 to 1.5
Outputs:
- gated_out: bfloat16 [16384, 4096], P(('seq', 'tensor'))
Inputs may be any that keep to these rules, and one draw needn't show every extreme that they name: `segment_ids`: non-decreasing along the tokens; each of the 4 prompts holds 1 to 8192 consecutive tokens, one exactly 8192.
All inputs are finite; a program needn't handle non-finite values.
Results may differ from a plain program's by a relative error of at most 0.005.
Values may be sent and summed in bfloat16 or wider, within the bound.
No kernel may reach another device: no remote copies, remote signals or barrier semaphores. Data moves between devices by JAX's collectives and lax.ppermute only.
A program may use at most 64 MiB of HBM per device.

v0:
```python
import math

import jax
import jax.numpy as jnp
from jax import lax
from jax.sharding import PartitionSpec as P

BLOCK = 256


precise = lax.Precision.HIGHEST


def shifted(value, axis, steps):
    count = lax.axis_size(axis)
    initial, last = (max(0, -steps), min(count, count - steps))
    return lax.ppermute(value, axis, [(source, source + steps) for source in range(initial, last)])


def combine_states(earlier, later):
    e_decay, e_state, e_norm, e_first, e_last = earlier
    l_decay, l_state, l_norm, l_first, l_last = later
    linked = jnp.where((e_last == l_first) | (e_last <= 0.0) | (l_first <= 0.0), 1.0, 0.0)
    factor = jnp.where(l_first <= 0.0, 1.0, l_decay * linked)
    decay_part = jnp.where(e_first <= 0.0, l_decay, e_decay * factor)
    state_part = factor * e_state + l_state
    norm_part = factor * e_norm + l_norm
    first_seg = jnp.where(e_first <= 0.0, l_first, e_first)
    last_seg = jnp.where(l_last <= 0.0, e_last, l_last)
    return (decay_part, state_part, norm_part, first_seg, last_seg)


def on_device(
    queries, key_rows, values, input_gate, forget_gate, segment_ids, output_gate, norm_gain
):
    tensor_size = lax.axis_size("tensor")
    row_count, inner = queries.shape
    head_count = input_gate.shape[1]
    head_dim = inner // head_count
    group_size = tensor_size // head_count
    column_count = head_dim // group_size

    def spread_heads(array, width):
        shaped = array.reshape(row_count, head_count, 1, width)
        return jnp.broadcast_to(shaped, (row_count, head_count, group_size, width)).reshape(
            row_count, tensor_size, width
        )

    query_send = spread_heads(queries, head_dim)
    key_send = spread_heads(key_rows, head_dim)
    value_send = values.reshape(row_count, tensor_size, column_count)
    gate_send = spread_heads(jnp.stack([input_gate, forget_gate], axis=2), 2)
    query_all, key_all, value_all, gate_all = (
        lax.all_to_all(query_send, "tensor", split_axis=1, concat_axis=0, tiled=True),
        lax.all_to_all(key_send, "tensor", split_axis=1, concat_axis=0, tiled=True),
        lax.all_to_all(value_send, "tensor", split_axis=1, concat_axis=0, tiled=True),
        lax.all_to_all(gate_send, "tensor", split_axis=1, concat_axis=0, tiled=True),
    )
    token_count = query_all.shape[0]
    query_all = query_all.reshape(token_count, head_dim)
    key_all = key_all.reshape(token_count, head_dim)
    value_all = value_all.reshape(token_count, column_count)
    gate_f = gate_all.reshape(token_count, 2).astype(jnp.float32)
    gate_in = gate_f[:, 0]
    log_forget = jax.nn.log_sigmoid(gate_f[:, 1])
    block_count = token_count // BLOCK
    key_scale = 1.0 / math.sqrt(head_dim)
    first_seg = segment_ids[0]
    row_ids = jnp.arange(BLOCK, dtype=jnp.int32)
    causal = row_ids[:, None] >= row_ids[None, :]

    def span_step(carry, block_in):
        cell_state, norm_vec, prev_seg, total_log = carry
        query_b, key_b, value_b, gate_b, forget_b, seg_b = block_in
        cumulative = jnp.cumsum(forget_b)
        allowed = causal & (seg_b[:, None] == seg_b[None, :])
        exponent = cumulative[:, None] - cumulative[None, :] + gate_b[None, :]
        weights = jnp.where(allowed, jnp.exp(jnp.where(allowed, exponent, 0.0)), 0.0)
        scores = (
            jnp.einsum("id,jd->ij", query_b, key_b, preferred_element_type=jnp.float32) * key_scale
        )
        weighted = weights * scores
        query_float = query_b.astype(jnp.float32)
        key_f = key_b.astype(jnp.float32) * key_scale
        value_f = value_b.astype(jnp.float32)
        numerator = jnp.dot(weighted, value_f, precision=precise)
        carried = jnp.exp(cumulative) * (seg_b == prev_seg).astype(jnp.float32)
        numerator = numerator + carried[:, None] * jnp.dot(
            query_float, cell_state, precision=precise
        )
        q_norm = jnp.sum(weighted, axis=1) + carried * jnp.dot(
            query_float, norm_vec, precision=precise
        )
        entry_factor = jnp.exp(total_log + cumulative) * (seg_b == first_seg).astype(jnp.float32)
        last_seg = seg_b[BLOCK - 1]
        tail_weight = jnp.exp(cumulative[BLOCK - 1] - cumulative + gate_b) * (
            seg_b == last_seg
        ).astype(jnp.float32)
        keep_factor = jnp.exp(cumulative[BLOCK - 1]) * (last_seg == prev_seg).astype(jnp.float32)
        scaled_keys = key_f * tail_weight[:, None]
        cell_state = keep_factor * cell_state + jnp.dot(scaled_keys.T, value_f, precision=precise)
        norm_vec = keep_factor * norm_vec + jnp.sum(scaled_keys, axis=0)
        return (
            (cell_state, norm_vec, last_seg, total_log + cumulative[BLOCK - 1]),
            (numerator, q_norm, entry_factor),
        )

    initial = (
        jnp.zeros((head_dim, column_count), jnp.float32),
        jnp.zeros((head_dim,), jnp.float32),
        first_seg,
        jnp.zeros((), jnp.float32),
    )
    blocks_in = (
        query_all.reshape(block_count, BLOCK, head_dim),
        key_all.reshape(block_count, BLOCK, head_dim),
        value_all.reshape(block_count, BLOCK, column_count),
        gate_in.reshape(block_count, BLOCK),
        log_forget.reshape(block_count, BLOCK),
        segment_ids.reshape(block_count, BLOCK),
    )
    final_carry, outputs = lax.scan(span_step, initial, blocks_in)
    cell_state, norm_vec, last_seg, total_log = final_carry
    numerator = outputs[0].reshape(token_count, column_count)
    q_norm = outputs[1].reshape(token_count)
    entry_factor = outputs[2].reshape(token_count)
    summary = (
        jnp.reshape(jnp.exp(total_log) * (last_seg == first_seg).astype(jnp.float32), (1,)),
        cell_state,
        norm_vec,
        jnp.reshape((first_seg + 1).astype(jnp.float32), (1,)),
        jnp.reshape((last_seg + 1).astype(jnp.float32), (1,)),
    )
    empty = jax.tree.map(jnp.zeros_like, summary)

    def relay_step(index, incoming):
        return shifted(combine_states(incoming, summary), "seq", 1)

    incoming = lax.fori_loop(0, lax.axis_size("seq") - 1, relay_step, empty)
    in_decay, in_state, in_norm, in_first, in_last = incoming
    linked = (in_last == summary[3]).astype(jnp.float32)
    scale_rows = entry_factor * linked
    query_full = query_all.astype(jnp.float32)
    numerator = numerator + scale_rows[:, None] * jnp.dot(query_full, in_state, precision=precise)
    q_norm = q_norm + scale_rows * jnp.dot(query_full, in_norm, precision=precise)
    hidden = (numerator / jnp.maximum(jnp.abs(q_norm), 1.0)[:, None]).astype(jnp.bfloat16)
    returned = lax.all_to_all(
        hidden.reshape(token_count, 1, column_count),
        "tensor",
        split_axis=0,
        concat_axis=1,
        tiled=True,
    )
    hidden_f = returned.astype(jnp.float32).reshape(row_count, head_count, head_dim)
    mean_val = jnp.mean(hidden_f, axis=2, keepdims=True)
    centered = hidden_f - mean_val
    variance = jnp.mean(centered * centered, axis=2, keepdims=True)
    normed = (centered * lax.rsqrt(variance + 1e-05)).reshape(row_count, inner)
    return (normed * norm_gain * jax.nn.silu(output_gate.astype(jnp.float32))).astype(jnp.bfloat16)


def solution(mesh):
    in_specs = (
        P(("seq", "tensor"), None),
        P(("seq", "tensor"), None),
        P(("seq", "tensor"), None),
        P(("seq", "tensor"), None),
        P(("seq", "tensor"), None),
        P("seq"),
        P(("seq", "tensor"), None),
        P(),
    )
    out_specs = P(("seq", "tensor"), None)
    return jax.shard_map(
        on_device, mesh=mesh, in_specs=in_specs, out_specs=out_specs, check_vma=False
    )
```

profile of v0, /device:TPU:23, one launch (start us, length us, event | category | flops | bytes accessed | tf_op | source)
XLA Modules:
  0.0 642.9 jit_solution(15675003004694583517)
XLA Ops:
  1.4 9.2 %all-to-all-start = ((bf16[64,16,2]{0,2,1:T(2,128)(2,1)}), bf16[64,16,2]{0,2,1:T(2,128)(2,1)S(1)}, u32[]{:S(2)}, u32[]{:S(2)}) async-start(bf16[64,16,2]{0,2,1:T(2,128)(2,1)} %bitcast.4), calls=%async_computation | async-start | bytes 16384 | tf_op jit(solution)/shard_map/all_to_all | solution.py:57
  12.4 5.2 all-to-all-done
  21.6 17.3 %all-to-all-done.2 = bf16[64,16,256]{2,0,1:T(8,128)(2,1)S(1)} async-done(((bf16[64,16,256]{2,0,1:T(8,128)(2,1)}), bf16[64,16,256]{2,0,1:T(8,128)(2,1)S(1)}, u32[]{:S(2)}, u32[]{:S(2)}) %all-to-all-start.2) | async-done | bytes 524320 | tf_op jit(solution)/shard_map/all_to_all | solution.py:56
  44.3 48.2 %all-to-all-done.3 = bf16[64,16,1024]{2,0,1:T(8,128)(2,1)S(1)} async-done(((bf16[64,16,1024]{2,0,1:T(8,128)(2,1)}), bf16[64,16,1024]{2,0,1:T(8,128)(2,1)S(1)}, u32[]{:S(2)}, u32[]{:S(2)}) %all-to-all-start.3) | async-done | bytes 2097184 | tf_op jit(solution)/shard_map/all_to_all | solution.py:54
  101.2 47.2 %all-to-all-done.1 = bf16[64,16,1024]{2,0,1:T(8,128)(2,1)} async-done(((bf16[64,16,1024]{2,0,1:T(8,128)(2,1)}), bf16[64,16,1024]{2,0,1:T(8,128)(2,1)}, u32[]{:S(2)}, u32[]{:S(2)}) %all-to-all-start.1) | async-done | bytes 2097184 | tf_op jit(solution)/shard_map/all_to_all | solution.py:55
  148.3 58.8 %while.41 = (s32[]{:T(128)}, f32[1024,256]{1,0:T(8,128)S(1)}, f32[1024]{0:T(1024)S(1)}, s32[]{:T(128)}, f32[]{:T(128)}, /*index=5*/f32[4,256,256]{2,1,0:T(8,128)...) while((s32[]{:T(128)}, f32[1024,256]{1,0:T(8,128)S(1)}, ...), condition=%wide.region_5.6_spmd.clone.clone, body=%wide.region_0.5_spmd.clone.sunk.clone | while | flops 1952486144 | bytes 7930723 | solution.py:122
  208.9 381.5 %while.40 = (s32[]{:T(128)}, f32[1024,256]{1,0:T(8,128)}, f32[1024]{0:T(1024)S(1)}, f32[1]{0:T(128)}, f32[1]{0:T(128)}, /*index=5*/pred[1]{0:T(512)(128)(4,1)}, ...) while((s32[]{:T(128)}, f32[1024,256]{1,0:T(8,128)}, ...), condition=%wide.region_7.8_spmd.clone, body=%wide.region_6.7_spmd.sunk.clone | while | flops 526346 | bytes 7369048 | solution.py:139
  216.1 20.6 %collective-permute-start.2 = (f32[1]{0:T(128)}, f32[1]{0:T(128)}, u32[]{:S(2)}, u32[]{:S(2)}) collective-permute-start(f32[1]{0:T(128)} %select_n.44), channel_id=1, source_target_pairs={{0,16},{16,32},{32,48},{48,64},{64,80},{80,96},{96,112},{112,128},... | collective-permute-start | bytes 20 | tf_op jit(solution)/shard_map/while/body/eval_jaxpr/ppermute | solution.py:17
  245.8 19.7 %collective-permute-start.2 = (f32[1]{0:T(128)}, f32[1]{0:T(128)}, u32[]{:S(2)}, u32[]{:S(2)}) collective-permute-start(f32[1]{0:T(128)} %select_n.44), channel_id=1, source_target_pairs={{0,16},{16,32},{32,48},{48,64},{64,80},{80,96},{96,112},{112,128},... | collective-permute-start | bytes 20 | tf_op jit(solution)/shard_map/while/body/eval_jaxpr/ppermute | solution.py:17
  274.5 18.7 %collective-permute-start.2 = (f32[1]{0:T(128)}, f32[1]{0:T(128)}, u32[]{:S(2)}, u32[]{:S(2)}) collective-permute-start(f32[1]{0:T(128)} %select_n.44), channel_id=1, source_target_pairs={{0,16},{16,32},{32,48},{48,64},{64,80},{80,96},{96,112},{112,128},... | collective-permute-start | bytes 20 | tf_op jit(solution)/shard_map/while/body/eval_jaxpr/ppermute | solution.py:17
  302.3 17.8 %collective-permute-start.2 = (f32[1]{0:T(128)}, f32[1]{0:T(128)}, u32[]{:S(2)}, u32[]{:S(2)}) collective-permute-start(f32[1]{0:T(128)} %select_n.44), channel_id=1, source_target_pairs={{0,16},{16,32},{32,48},{48,64},{64,80},{80,96},{96,112},{112,128},... | collective-permute-start | bytes 20 | tf_op jit(solution)/shard_map/while/body/eval_jaxpr/ppermute | solution.py:17
  330.7 17.7 %collective-permute-start.2 = (f32[1]{0:T(128)}, f32[1]{0:T(128)}, u32[]{:S(2)}, u32[]{:S(2)}) collective-permute-start(f32[1]{0:T(128)} %select_n.44), channel_id=1, source_target_pairs={{0,16},{16,32},{32,48},{48,64},{64,80},{80,96},{96,112},{112,128},... | collective-permute-start | bytes 20 | tf_op jit(solution)/shard_map/while/body/eval_jaxpr/ppermute | solution.py:17
  358.7 16.7 %collective-permute-start.2 = (f32[1]{0:T(128)}, f32[1]{0:T(128)}, u32[]{:S(2)}, u32[]{:S(2)}) collective-permute-start(f32[1]{0:T(128)} %select_n.44), channel_id=1, source_target_pairs={{0,16},{16,32},{32,48},{48,64},{64,80},{80,96},{96,112},{112,128},... | collective-permute-start | bytes 20 | tf_op jit(solution)/shard_map/while/body/eval_jaxpr/ppermute | solution.py:17
  385.8 15.8 %collective-permute-start.2 = (f32[1]{0:T(128)}, f32[1]{0:T(128)}, u32[]{:S(2)}, u32[]{:S(2)}) collective-permute-start(f32[1]{0:T(128)} %select_n.44), channel_id=1, source_target_pairs={{0,16},{16,32},{32,48},{48,64},{64,80},{80,96},{96,112},{112,128},... | collective-permute-start | bytes 20 | tf_op jit(solution)/shard_map/while/body/eval_jaxpr/ppermute | solution.py:17
  412.0 14.8 %collective-permute-start.2 = (f32[1]{0:T(128)}, f32[1]{0:T(128)}, u32[]{:S(2)}, u32[]{:S(2)}) collective-permute-start(f32[1]{0:T(128)} %select_n.44), channel_id=1, source_target_pairs={{0,16},{16,32},{32,48},{48,64},{64,80},{80,96},{96,112},{112,128},... | collective-permute-start | bytes 20 | tf_op jit(solution)/shard_map/while/body/eval_jaxpr/ppermute | solution.py:17
  437.2 13.9 %collective-permute-start.2 = (f32[1]{0:T(128)}, f32[1]{0:T(128)}, u32[]{:S(2)}, u32[]{:S(2)}) collective-permute-start(f32[1]{0:T(128)} %select_n.44), channel_id=1, source_target_pairs={{0,16},{16,32},{32,48},{48,64},{64,80},{80,96},{96,112},{112,128},... | collective-permute-start | bytes 20 | tf_op jit(solution)/shard_map/while/body/eval_jaxpr/ppermute | solution.py:17
  461.4 12.9 %collective-permute-start.2 = (f32[1]{0:T(128)}, f32[1]{0:T(128)}, u32[]{:S(2)}, u32[]{:S(2)}) collective-permute-start(f32[1]{0:T(128)} %select_n.44), channel_id=1, source_target_pairs={{0,16},{16,32},{32,48},{48,64},{64,80},{80,96},{96,112},{112,128},... | collective-permute-start | bytes 20 | tf_op jit(solution)/shard_map/while/body/eval_jaxpr/ppermute | solution.py:17
  484.7 12.0 %collective-permute-start.2 = (f32[1]{0:T(128)}, f32[1]{0:T(128)}, u32[]{:S(2)}, u32[]{:S(2)}) collective-permute-start(f32[1]{0:T(128)} %select_n.44), channel_id=1, source_target_pairs={{0,16},{16,32},{32,48},{48,64},{64,80},{80,96},{96,112},{112,128},... | collective-permute-start | bytes 20 | tf_op jit(solution)/shard_map/while/body/eval_jaxpr/ppermute | solution.py:17
  507.1 11.4 %collective-permute-start.2 = (f32[1]{0:T(128)}, f32[1]{0:T(128)}, u32[]{:S(2)}, u32[]{:S(2)}) collective-permute-start(f32[1]{0:T(128)} %select_n.44), channel_id=1, source_target_pairs={{0,16},{16,32},{32,48},{48,64},{64,80},{80,96},{96,112},{112,128},... | collective-permute-start | bytes 20 | tf_op jit(solution)/shard_map/while/body/eval_jaxpr/ppermute | solution.py:17
  528.8 11.4 %collective-permute-start.2 = (f32[1]{0:T(128)}, f32[1]{0:T(128)}, u32[]{:S(2)}, u32[]{:S(2)}) collective-permute-start(f32[1]{0:T(128)} %select_n.44), channel_id=1, source_target_pairs={{0,16},{16,32},{32,48},{48,64},{64,80},{80,96},{96,112},{112,128},... | collective-permute-start | bytes 20 | tf_op jit(solution)/shard_map/while/body/eval_jaxpr/ppermute | solution.py:17
  550.2 12.3 %collective-permute-start.2 = (f32[1]{0:T(128)}, f32[1]{0:T(128)}, u32[]{:S(2)}, u32[]{:S(2)}) collective-permute-start(f32[1]{0:T(128)} %select_n.44), channel_id=1, source_target_pairs={{0,16},{16,32},{32,48},{48,64},{64,80},{80,96},{96,112},{112,128},... | collective-permute-start | bytes 20 | tf_op jit(solution)/shard_map/while/body/eval_jaxpr/ppermute | solution.py:17
  572.8 13.0 %collective-permute-start.2 = (f32[1]{0:T(128)}, f32[1]{0:T(128)}, u32[]{:S(2)}, u32[]{:S(2)}) collective-permute-start(f32[1]{0:T(128)} %select_n.44), channel_id=1, source_target_pairs={{0,16},{16,32},{32,48},{48,64},{64,80},{80,96},{96,112},{112,128},... | collective-permute-start | bytes 20 | tf_op jit(solution)/shard_map/while/body/eval_jaxpr/ppermute | solution.py:17
  593.7 5.5 fusion.40
  602.3 35.9 %all_to_all.63 = bf16[16,2,8192]{2,1,0:T(2,128)(2,1)S(1)} all-to-all(bf16[16,2,8192]{2,1,0:T(2,128)(2,1)S(1)} %reshape.234), channel_id=1, replica_groups=mesh['seq'=16,'tensor'=16] {'tensor'}, dimensions={0} | all-to-all | bytes 1048576 | tf_op jit(solution)/shard_map/all_to_all | solution.py:147
  (251 shorter events, 223.8 us)
Async XLA Ops:
  17.6 21.3 %all-to-all-start.2 = ((bf16[64,16,256]{2,0,1:T(8,128)(2,1)}), bf16[64,16,256]{2,0,1:T(8,128)(2,1)S(1)}, u32[]{:S(2)}, u32[]{:S(2)}) async-start(bf16[64,16,256]{2,0,1:T(8,128)(2,1)} %bitcast.132), calls=%async_computation.2 | async-start | bytes 1048576 | tf_op jit(solution)/shard_map/all_to_all | solution.py:56
  40.5 52.1 %all-to-all-start.3 = ((bf16[64,16,1024]{2,0,1:T(8,128)(2,1)}), bf16[64,16,1024]{2,0,1:T(8,128)(2,1)S(1)}, u32[]{:S(2)}, u32[]{:S(2)}) async-start(bf16[64,16,1024]{2,0,1:T(8,128)(2,1)} %bitcast.204), calls=%async_computation.3 | async-start | bytes 4194304 | tf_op jit(solution)/shard_map/all_to_all | solution.py:54
  94.1 54.2 %all-to-all-start.1 = ((bf16[64,16,1024]{2,0,1:T(8,128)(2,1)}), bf16[64,16,1024]{2,0,1:T(8,128)(2,1)}, u32[]{:S(2)}, u32[]{:S(2)}) async-start(bf16[64,16,1024]{2,0,1:T(8,128)(2,1)} %bitcast.203), calls=%async_computation.1 | async-start | bytes 4194304 | tf_op jit(solution)/shard_map/all_to_all | solution.py:55
  211.2 26.7 %collective-permute-start = (f32[1024,256]{1,0:T(8,128)}, f32[1024,256]{1,0:T(8,128)}, u32[]{:S(2)}, u32[]{:S(2)}) collective-permute-start(f32[1024,256]{1,0:T(8,128)} %multiply_add_fusion.12), channel_id=1, source_target_pairs={{0,16},{16,32},{32,48},{48,64},{64,80},{80,96},{96,112},{112,128},... | collective-permute-start | bytes 3145736 | tf_op jit(solution)/shard_map/while/body/eval_jaxpr/ppermute | solution.py:17
  214.2 23.8 %collective-permute-start.1 = (f32[1024]{0:T(1024)S(1)}, f32[1024]{0:T(1024)S(1)}, u32[]{:S(2)}, u32[]{:S(2)}) collective-permute-start(f32[1024]{0:T(1024)S(1)} %multiply_add_fusion.13), channel_id=1, source_target_pairs={{0,16},{16,32},{32,48},{48,64},{64,80},{80,96},{96,112},{112,128},... | collective-permute-start | bytes 12296 | tf_op jit(solution)/shard_map/while/body/eval_jaxpr/ppermute | solution.py:17
  216.1 21.9 %collective-permute-start.2 = (f32[1]{0:T(128)}, f32[1]{0:T(128)}, u32[]{:S(2)}, u32[]{:S(2)}) collective-permute-start(f32[1]{0:T(128)} %select_n.44), channel_id=1, source_target_pairs={{0,16},{16,32},{32,48},{48,64},{64,80},{80,96},{96,112},{112,128},... | collective-permute-start | bytes 20 | tf_op jit(solution)/shard_map/while/body/eval_jaxpr/ppermute | solution.py:17
  240.9 25.8 %collective-permute-start = (f32[1024,256]{1,0:T(8,128)}, f32[1024,256]{1,0:T(8,128)}, u32[]{:S(2)}, u32[]{:S(2)}) collective-permute-start(f32[1024,256]{1,0:T(8,128)} %multiply_add_fusion.12), channel_id=1, source_target_pairs={{0,16},{16,32},{32,48},{48,64},{64,80},{80,96},{96,112},{112,128},... | collective-permute-start | bytes 3145736 | tf_op jit(solution)/shard_map/while/body/eval_jaxpr/ppermute | solution.py:17
  243.9 22.9 %collective-permute-start.1 = (f32[1024]{0:T(1024)S(1)}, f32[1024]{0:T(1024)S(1)}, u32[]{:S(2)}, u32[]{:S(2)}) collective-permute-start(f32[1024]{0:T(1024)S(1)} %multiply_add_fusion.13), channel_id=1, source_target_pairs={{0,16},{16,32},{32,48},{48,64},{64,80},{80,96},{96,112},{112,128},... | collective-permute-start | bytes 12296 | tf_op jit(solution)/shard_map/while/body/eval_jaxpr/ppermute | solution.py:17
  245.8 20.9 %collective-permute-start.2 = (f32[1]{0:T(128)}, f32[1]{0:T(128)}, u32[]{:S(2)}, u32[]{:S(2)}) collective-permute-start(f32[1]{0:T(128)} %select_n.44), channel_id=1, source_target_pairs={{0,16},{16,32},{32,48},{48,64},{64,80},{80,96},{96,112},{112,128},... | collective-permute-start | bytes 20 | tf_op jit(solution)/shard_map/while/body/eval_jaxpr/ppermute | solution.py:17
  269.7 24.8 %collective-permute-start = (f32[1024,256]{1,0:T(8,128)}, f32[1024,256]{1,0:T(8,128)}, u32[]{:S(2)}, u32[]{:S(2)}) collective-permute-start(f32[1024,256]{1,0:T(8,128)} %multiply_add_fusion.12), channel_id=1, source_target_pairs={{0,16},{16,32},{32,48},{48,64},{64,80},{80,96},{96,112},{112,128},... | collective-permute-start | bytes 3145736 | tf_op jit(solution)/shard_map/while/body/eval_jaxpr/ppermute | solution.py:17
  272.6 21.9 %collective-permute-start.1 = (f32[1024]{0:T(1024)S(1)}, f32[1024]{0:T(1024)S(1)}, u32[]{:S(2)}, u32[]{:S(2)}) collective-permute-start(f32[1024]{0:T(1024)S(1)} %multiply_add_fusion.13), channel_id=1, source_target_pairs={{0,16},{16,32},{32,48},{48,64},{64,80},{80,96},{96,112},{112,128},... | collective-permute-start | bytes 12296 | tf_op jit(solution)/shard_map/while/body/eval_jaxpr/ppermute | solution.py:17
  297.5 26.4 %collective-permute-start = (f32[1024,256]{1,0:T(8,128)}, f32[1024,256]{1,0:T(8,128)}, u32[]{:S(2)}, u32[]{:S(2)}) collective-permute-start(f32[1024,256]{1,0:T(8,128)} %multiply_add_fusion.12), channel_id=1, source_target_pairs={{0,16},{16,32},{32,48},{48,64},{64,80},{80,96},{96,112},{112,128},... | collective-permute-start | bytes 3145736 | tf_op jit(solution)/shard_map/while/body/eval_jaxpr/ppermute | solution.py:17
  300.4 23.5 %collective-permute-start.1 = (f32[1024]{0:T(1024)S(1)}, f32[1024]{0:T(1024)S(1)}, u32[]{:S(2)}, u32[]{:S(2)}) collective-permute-start(f32[1024]{0:T(1024)S(1)} %multiply_add_fusion.13), channel_id=1, source_target_pairs={{0,16},{16,32},{32,48},{48,64},{64,80},{80,96},{96,112},{112,128},... | collective-permute-start | bytes 12296 | tf_op jit(solution)/shard_map/while/body/eval_jaxpr/ppermute | solution.py:17
  302.3 21.5 %collective-permute-start.2 = (f32[1]{0:T(128)}, f32[1]{0:T(128)}, u32[]{:S(2)}, u32[]{:S(2)}) collective-permute-start(f32[1]{0:T(128)} %select_n.44), channel_id=1, source_target_pairs={{0,16},{16,32},{32,48},{48,64},{64,80},{80,96},{96,112},{112,128},... | collective-permute-start | bytes 20 | tf_op jit(solution)/shard_map/while/body/eval_jaxpr/ppermute | solution.py:17
  326.8 25.1 %collective-permute-start = (f32[1024,256]{1,0:T(8,128)}, f32[1024,256]{1,0:T(8,128)}, u32[]{:S(2)}, u32[]{:S(2)}) collective-permute-start(f32[1024,256]{1,0:T(8,128)} %multiply_add_fusion.12), channel_id=1, source_target_pairs={{0,16},{16,32},{32,48},{48,64},{64,80},{80,96},{96,112},{112,128},... | collective-permute-start | bytes 3145736 | tf_op jit(solution)/shard_map/while/body/eval_jaxpr/ppermute | solution.py:17
  328.8 23.1 %collective-permute-start.1 = (f32[1024]{0:T(1024)S(1)}, f32[1024]{0:T(1024)S(1)}, u32[]{:S(2)}, u32[]{:S(2)}) collective-permute-start(f32[1024]{0:T(1024)S(1)} %multiply_add_fusion.13), channel_id=1, source_target_pairs={{0,16},{16,32},{32,48},{48,64},{64,80},{80,96},{96,112},{112,128},... | collective-permute-start | bytes 12296 | tf_op jit(solution)/shard_map/while/body/eval_jaxpr/ppermute | solution.py:17
  330.7 21.2 %collective-permute-start.2 = (f32[1]{0:T(128)}, f32[1]{0:T(128)}, u32[]{:S(2)}, u32[]{:S(2)}) collective-permute-start(f32[1]{0:T(128)} %select_n.44), channel_id=1, source_target_pairs={{0,16},{16,32},{32,48},{48,64},{64,80},{80,96},{96,112},{112,128},... | collective-permute-start | bytes 20 | tf_op jit(solution)/shard_map/while/body/eval_jaxpr/ppermute | solution.py:17
  354.9 24.1 %collective-permute-start = (f32[1024,256]{1,0:T(8,128)}, f32[1024,256]{1,0:T(8,128)}, u32[]{:S(2)}, u32[]{:S(2)}) collective-permute-start(f32[1024,256]{1,0:T(8,128)} %multiply_add_fusion.12), channel_id=1, source_target_pairs={{0,16},{16,32},{32,48},{48,64},{64,80},{80,96},{96,112},{112,128},... | collective-permute-start | bytes 3145736 | tf_op jit(solution)/shard_map/while/body/eval_jaxpr/ppermute | solution.py:17
  356.8 22.2 %collective-permute-start.1 = (f32[1024]{0:T(1024)S(1)}, f32[1024]{0:T(1024)S(1)}, u32[]{:S(2)}, u32[]{:S(2)}) collective-permute-start(f32[1024]{0:T(1024)S(1)} %multiply_add_fusion.13), channel_id=1, source_target_pairs={{0,16},{16,32},{32,48},{48,64},{64,80},{80,96},{96,112},{112,128},... | collective-permute-start | bytes 12296 | tf_op jit(solution)/shard_map/while/body/eval_jaxpr/ppermute | solution.py:17
  382.0 23.2 %collective-permute-start = (f32[1024,256]{1,0:T(8,128)}, f32[1024,256]{1,0:T(8,128)}, u32[]{:S(2)}, u32[]{:S(2)}) collective-permute-start(f32[1024,256]{1,0:T(8,128)} %multiply_add_fusion.12), channel_id=1, source_target_pairs={{0,16},{16,32},{32,48},{48,64},{64,80},{80,96},{96,112},{112,128},... | collective-permute-start | bytes 3145736 | tf_op jit(solution)/shard_map/while/body/eval_jaxpr/ppermute | solution.py:17
  383.9 21.2 %collective-permute-start.1 = (f32[1024]{0:T(1024)S(1)}, f32[1024]{0:T(1024)S(1)}, u32[]{:S(2)}, u32[]{:S(2)}) collective-permute-start(f32[1024]{0:T(1024)S(1)} %multiply_add_fusion.13), channel_id=1, source_target_pairs={{0,16},{16,32},{32,48},{48,64},{64,80},{80,96},{96,112},{112,128},... | collective-permute-start | bytes 12296 | tf_op jit(solution)/shard_map/while/body/eval_jaxpr/ppermute | solution.py:17
  408.1 22.2 %collective-permute-start = (f32[1024,256]{1,0:T(8,128)}, f32[1024,256]{1,0:T(8,128)}, u32[]{:S(2)}, u32[]{:S(2)}) collective-permute-start(f32[1024,256]{1,0:T(8,128)} %multiply_add_fusion.12), channel_id=1, source_target_pairs={{0,16},{16,32},{32,48},{48,64},{64,80},{80,96},{96,112},{112,128},... | collective-permute-start | bytes 3145736 | tf_op jit(solution)/shard_map/while/body/eval_jaxpr/ppermute | solution.py:17
  433.3 21.3 %collective-permute-start = (f32[1024,256]{1,0:T(8,128)}, f32[1024,256]{1,0:T(8,128)}, u32[]{:S(2)}, u32[]{:S(2)}) collective-permute-start(f32[1024,256]{1,0:T(8,128)} %multiply_add_fusion.12), channel_id=1, source_target_pairs={{0,16},{16,32},{32,48},{48,64},{64,80},{80,96},{96,112},{112,128},... | collective-permute-start | bytes 3145736 | tf_op jit(solution)/shard_map/while/body/eval_jaxpr/ppermute | solution.py:17
  569.0 20.9 %collective-permute-start = (f32[1024,256]{1,0:T(8,128)}, f32[1024,256]{1,0:T(8,128)}, u32[]{:S(2)}, u32[]{:S(2)}) collective-permute-start(f32[1024,256]{1,0:T(8,128)} %multiply_add_fusion.12), channel_id=1, source_target_pairs={{0,16},{16,32},{32,48},{48,64},{64,80},{80,96},{96,112},{112,128},... | collective-permute-start | bytes 3145736 | tf_op jit(solution)/shard_map/while/body/eval_jaxpr/ppermute | solution.py:17
  (31 other events, 482.1 us)
where the time goes:
time: 654 us; the launch traced here: 643 us
  starting transfers between devices  312 us (48%)
  waiting for transfers between devices  164 us (25%)
  other arithmetic  54.3 us (8%)
  blocking collectives  35.9 us (5%)
  matrix products  35.7 us (5%)
  loops' own time  20 us (3%)
  local copies, waits for them, and re-layouts  18.6 us (3%)
    ppermute x45, starting transfers between devices, shifted(): lax.ppermute(value, axis, [(source, source + steps) for source in range(i...  290 us
    all_to_all x1, waiting for transfers between devices, on_device(): lax.all_to_all(query_send, 'tensor', split_axis=1, concat_axis=0, tiled=T...  48.2 us
    all_to_all x1, waiting for transfers between devices, on_device(): lax.all_to_all(key_send, 'tensor', split_axis=1, concat_axis=0, tiled=True)  47.2 us
    ppermute x45, waiting for transfers between devices, shifted(): lax.ppermute(value, axis, [(source, source + steps) for source in range(i...  46.6 us
    all_to_all x1, blocking collectives, on_device(): lax.all_to_all(hidden.reshape(token_count, 1, column_count), 'tensor', sp...  35.9 us
    add x15, other arithmetic, combine_states(): state_part = factor * e_state + l_state  35.2 us
    all_to_all x1, waiting for transfers between devices, on_device(): lax.all_to_all(value_send, 'tensor', split_axis=1, concat_axis=0, tiled=T...  17.3 us
  transfers between devices with their start and end apart: 49, of which 19 were waited for; matrix products, arithmetic and copies ran while one was open for 0% of the time, Pallas kernels for 0%

commit v1 on v0

--- a/solution.py
+++ b/solution.py
@@ -17,17 +17,58 @@
     return lax.ppermute(value, axis, [(source, source + steps) for source in range(initial, last)])
 
 
-def combine_states(earlier, later):
-    e_decay, e_state, e_norm, e_first, e_last = earlier
-    l_decay, l_state, l_norm, l_first, l_last = later
+def meta_row(head_dim, column_count):
+    return head_dim + head_dim // column_count
+
+
+def pack_summary(query_all, key_all, value_all, gate_in, log_forget, segment_ids, key_scale):
+    head_dim = key_all.shape[1]
+    column_count = value_all.shape[1]
+    cumulative = jnp.cumsum(log_forget)
+    total_log = cumulative[-1]
+    first_seg = segment_ids[0]
+    last_seg = segment_ids[-1]
+    tail_weight = jnp.exp(total_log - cumulative + gate_in) * (segment_ids == last_seg).astype(
+        jnp.float32
+    )
+    scaled_keys = key_all.astype(jnp.float32) * (key_scale * tail_weight)[:, None]
+    state = jnp.dot(scaled_keys.T, value_all.astype(jnp.float32), precision=precise)
+    norm = jnp.sum(scaled_keys, axis=0)
+    decay = jnp.exp(total_log) * (last_seg == first_seg).astype(jnp.float32)
+    norm_rows = head_dim // column_count
+    rows = meta_row(head_dim, column_count) + 1
+    padded = -(-rows // 8) * 8
+    lane = jnp.arange(column_count)
+    meta = jnp.where(
+        lane == 0,
+        decay,
+        jnp.where(
+            lane == 1,
+            (first_seg + 1).astype(jnp.float32),
+            jnp.where(lane == 2, (last_seg + 1).astype(jnp.float32), 0.0),
+        ),
+    )
+    filler = jnp.zeros((padded - rows, column_count), jnp.float32)
+    return jnp.concatenate(
+        [state, norm.reshape(norm_rows, column_count), meta[None, :], filler], axis=0
+    )
+
+
+def combine_packed(earlier, later, head_dim):
+    column_count = earlier.shape[1]
+    row = meta_row(head_dim, column_count)
+    e_decay, e_first, e_last = earlier[row, 0], earlier[row, 1], earlier[row, 2]
+    l_decay, l_first, l_last = later[row, 0], later[row, 1], later[row, 2]
     linked = jnp.where((e_last == l_first) | (e_last <= 0.0) | (l_first <= 0.0), 1.0, 0.0)
     factor = jnp.where(l_first <= 0.0, 1.0, l_decay * linked)
     decay_part = jnp.where(e_first <= 0.0, l_decay, e_decay * factor)
-    state_part = factor * e_state + l_state
-    norm_part = factor * e_norm + l_norm
     first_seg = jnp.where(e_first <= 0.0, l_first, e_first)
     last_seg = jnp.where(l_last <= 0.0, e_last, l_last)
-    return (decay_part, state_part, norm_part, first_seg, last_seg)
+    body = factor * earlier + later
+    lane = jnp.arange(column_count)[None, :]
+    rows = jnp.arange(earlier.shape[0])[:, None]
+    meta = jnp.where(lane == 0, decay_part, jnp.where(lane == 1, first_seg, last_seg))
+    return jnp.where((rows == row) & (lane < 3), meta, body)
 
 
 def on_device(
@@ -66,6 +107,21 @@
     block_count = token_count // BLOCK
     key_scale = 1.0 / math.sqrt(head_dim)
     first_seg = segment_ids[0]
+
+    packed = pack_summary(
+        query_all, key_all, value_all, gate_in, log_forget, segment_ids, key_scale
+    )
+    scanned = packed
+    shift = 1
+    while shift < lax.axis_size("seq"):
+        scanned = combine_packed(shifted(scanned, "seq", shift), scanned, head_dim)
+        shift *= 2
+    incoming = shifted(scanned, "seq", 1)
+    in_row = meta_row(head_dim, column_count)
+    in_state = incoming[:head_dim]
+    in_norm = incoming[head_dim:in_row].reshape(head_dim)
+    in_last = incoming[in_row, 2]
+
     row_ids = jnp.arange(BLOCK, dtype=jnp.int32)
     causal = row_ids[:, None] >= row_ids[None, :]
 
@@ -119,26 +175,12 @@
         log_forget.reshape(block_count, BLOCK),
         segment_ids.reshape(block_count, BLOCK),
     )
-    final_carry, outputs = lax.scan(span_step, initial, blocks_in)
-    cell_state, norm_vec, last_seg, total_log = final_carry
+    unused, outputs = lax.scan(span_step, initial, blocks_in, unroll=True)
     numerator = outputs[0].reshape(token_count, column_count)
     q_norm = outputs[1].reshape(token_count)
     entry_factor = outputs[2].reshape(token_count)
-    summary = (
-        jnp.reshape(jnp.exp(total_log) * (last_seg == first_seg).astype(jnp.float32), (1,)),
-        cell_state,
-        norm_vec,
-        jnp.reshape((first_seg + 1).astype(jnp.float32), (1,)),
-        jnp.reshape((last_seg + 1).astype(jnp.float32), (1,)),
-    )
-    empty = jax.tree.map(jnp.zeros_like, summary)
-
-    def relay_step(index, incoming):
-        return shifted(combine_states(incoming, summary), "seq", 1)
-
-    incoming = lax.fori_loop(0, lax.axis_size("seq") - 1, relay_step, empty)
-    in_decay, in_state, in_norm, in_first, in_last = incoming
-    linked = (in_last == summary[3]).astype(jnp.float32)
+
+    linked = (in_last == (first_seg + 1).astype(jnp.float32)).astype(jnp.float32)
     scale_rows = entry_factor * linked
     query_full = query_all.astype(jnp.float32)
     numerator = numerator + scale_rows[:, None] * jnp.dot(query_full, in_state, precision=precise)

time: 654 us -> 355 us (0.54)
  starting transfers between devices: 312 us -> 31.9 us
  between operations: 2.15 us -> 44.5 us
  other arithmetic: 54.3 us -> 29.7 us
  loops' own time: 20 us -> 0 us
  local copies, waits for them, and re-layouts: 18.6 us -> 38.3 us
  waiting for transfers between devices: 164 us -> 147 us
  blocking collectives: 35.9 us -> 24 us
    ppermute x45 -> x5, starting transfers between devices: 290 us -> 9.95 us  [shifted(): lax.ppermute(value, axis, [(source, source + steps) for source in range(i...]
    add x30 -> x0, other arithmetic: 35.3 us -> none  [the longest x15 35.2 us: combine_states(): state_part = factor * e_state + l_state]
    all_to_all x1, waiting for transfers between devices: 48.2 us -> 17.4 us  [on_device(): lax.all_to_all(query_send, 'tensor', split_axis=1, concat_axis=0, tiled=T...]
    ppermute x45 -> x5, waiting for transfers between devices: 46.6 us -> 69.5 us  [shifted(): lax.ppermute(value, axis, [(source, source + steps) for source in range(i...]
    another operation x2 -> x0, loops' own time: 20 us -> none  [the longest x1 10.4 us: on_device(): final_carry, outputs = lax.scan(span_step, initial, blocks_in)]
    slice x9 -> x18, local copies, waits for them, and re-layouts: 3.21 us -> 17.8 us  [the longest x4 5.73 us: combine_packed(): earlier[row, 0]]
    all_to_all x1, blocking collectives: 35.9 us -> 24 us  [on_device(): lax.all_to_all(hidden.reshape(token_count, 1, column_count), 'tensor', sp...]
    select_n x0 -> x9, other arithmetic: none -> 11.3 us  [the longest x4 11.3 us: combine_packed(): return jnp.where((rows == row) & (lane < 3), meta, body)]
  transfers between devices with their start and end apart: 49 -> 9, of which waited for: 19 -> 8; matrix products, arithmetic and copies ran while one was open for 0% -> 17% of each run, Pallas kernels for 0% -> 0%
where the time goes in v1:
time: 355 us; the launch traced here: 348 us
  waiting for transfers between devices  147 us (41%)
  between operations  44.5 us (13%)
  local copies, waits for them, and re-layouts  38.3 us (11%)
  matrix products  32.3 us (9%)
  starting transfers between devices  31.9 us (9%)
  other arithmetic  29.7 us (8%)
  blocking collectives  24 us (7%)
    ppermute x5, waiting for transfers between devices, shifted(): lax.ppermute(value, axis, [(source, source + steps) for source in range(i...  69.5 us
    all_to_all x1, waiting for transfers between devices, on_device(): lax.all_to_all(key_send, 'tensor', split_axis=1, concat_axis=0, tiled=True)  38.1 us
    all_to_all x1, blocking collectives, on_device(): lax.all_to_all(hidden.reshape(token_count, 1, column_count), 'tensor', sp...  24 us
    all_to_all x1, waiting for transfers between devices, on_device(): lax.all_to_all(query_send, 'tensor', split_axis=1, concat_axis=0, tiled=T...  17.4 us
    all_to_all x1, waiting for transfers between devices, on_device(): lax.all_to_all(value_send, 'tensor', split_axis=1, concat_axis=0, tiled=T...  17.3 us
    select_n x4, other arithmetic, combine_packed(): return jnp.where((rows == row) & (lane < 3), meta, body)  11.3 us
    ppermute x5, starting transfers between devices, shifted(): lax.ppermute(value, axis, [(source, source + steps) for source in range(i...  9.95 us
    all_to_all x1, starting transfers between devices, on_device(): lax.all_to_all(gate_send, 'tensor', split_axis=1, concat_axis=0, tiled=True)  9.28 us
  transfers between devices with their start and end apart: 9, of which 8 were waited for; matrix products, arithmetic and copies ran while one was open for 17% of the time, Pallas kernels for 0%

profile of v1, /device:TPU:23, one launch (start us, length us, event | category | flops | bytes accessed | tf_op | source)
XLA Modules:
  0.0 348.1 jit_solution(8789657355587252517)
XLA Ops:
  1.3 9.3 %all-to-all-start = ((bf16[64,16,2]{0,2,1:T(2,128)(2,1)}), bf16[64,16,2]{0,2,1:T(2,128)(2,1)S(1)}, u32[]{:S(2)}, u32[]{:S(2)}) async-start(bf16[64,16,2]{0,2,1:T(2,128)(2,1)} %bitcast.2), calls=%async_computation | async-start | bytes 16384 | tf_op jit(solution)/shard_map/all_to_all | solution.py:98
  12.5 5.2 %all-to-all-done = bf16[64,16,2]{0,2,1:T(2,128)(2,1)S(1)} async-done(((bf16[64,16,2]{0,2,1:T(2,128)(2,1)}), bf16[64,16,2]{0,2,1:T(2,128)(2,1)S(1)}, u32[]{:S(2)}, u32[]{:S(2)}) %all-to-all-start) | async-done | bytes 4128 | tf_op jit(solution)/shard_map/all_to_all | solution.py:98
  17.7 4.0 %all-to-all-start.3 = ((bf16[64,16,256]{2,0,1:T(8,128)(2,1)}), bf16[64,16,256]{2,0,1:T(8,128)(2,1)S(1)}, u32[]{:S(2)}, u32[]{:S(2)}) async-start(bf16[64,16,256]{2,0,1:T(8,128)(2,1)} %bitcast.255), calls=%async_computation.3 | async-start | bytes 1048576 | tf_op jit(solution)/shard_map/all_to_all | solution.py:97
  21.7 17.3 %all-to-all-done.3 = bf16[64,16,256]{2,0,1:T(8,128)(2,1)S(1)} async-done(((bf16[64,16,256]{2,0,1:T(8,128)(2,1)}), bf16[64,16,256]{2,0,1:T(8,128)(2,1)S(1)}, u32[]{:S(2)}, u32[]{:S(2)}) %all-to-all-start.3) | async-done | bytes 524320 | tf_op jit(solution)/shard_map/all_to_all | solution.py:97
  40.6 3.7 %all-to-all-start.2 = ((bf16[64,16,1024]{2,0,1:T(8,128)(2,1)}), bf16[64,16,1024]{2,0,1:T(8,128)(2,1)S(1)}, u32[]{:S(2)}, u32[]{:S(2)}) async-start(bf16[64,16,1024]{2,0,1:T(8,128)(2,1)} %bitcast.264), calls=%async_computation.2 | async-start | bytes 4194304 | tf_op jit(solution)/shard_map/all_to_all | solution.py:96
  54.5 38.1 %all-to-all-done.2 = bf16[64,16,1024]{2,0,1:T(8,128)(2,1)S(1)} async-done(((bf16[64,16,1024]{2,0,1:T(8,128)(2,1)}), bf16[64,16,1024]{2,0,1:T(8,128)(2,1)S(1)}, u32[]{:S(2)}, u32[]{:S(2)}) %all-to-all-start.2) | async-done | bytes 2097184 | tf_op jit(solution)/shard_map/all_to_all | solution.py:96
  94.2 4.9 %all-to-all-start.1 = ((bf16[64,16,1024]{2,0,1:T(8,128)(2,1)}), bf16[64,16,1024]{2,0,1:T(8,128)(2,1)}, u32[]{:S(2)}, u32[]{:S(2)}) async-start(bf16[64,16,1024]{2,0,1:T(8,128)(2,1)} %bitcast.263), calls=%async_computation.1 | async-start | bytes 4194304 | tf_op jit(solution)/shard_map/all_to_all | solution.py:95
  119.4 4.6 %fusion.6 = f32[1024,256]{1,0:T(8,128)} fusion(f32[16,64]{1,0:T(8,128)S(1)} %mul.373, bf16[64,16,256]{2,0,1:T(8,128)(2,1)S(1)} %all-to-all-done.3, bf16[64,16,1024]{2,0,1:T(8,128)(2,1)S(1)} %all-to-all-done.2), kind=kOutput, calls=%fused_computation.15 | convolution fusion | flops 3223322624 | bytes 3674112 | tf_op jit(solution)/shard_map/dot_general | solution.py:35
  124.0 4.0 %concatenate.14 = f32[1032,256]{1,0:T(8,128)} concatenate(f32[1024,256]{1,0:T(8,128)} %fusion.6, f32[4,256]{1,0:T(4,128)S(1)} %reshape.550, f32[1,256]{1,0:T(1,128)S(1)} %compare_select_fusion.3, f32[3,256]{1,0:T(4,128)S(1)} %broadcast_in_dim.204), dimensions={0} | concatenate | bytes 2113536 | tf_op jit(solution)/shard_map/concatenate | solution.py:52
  128.0 2.9 collective-permute-start
  130.9 17.4 %all-to-all-done.1 = bf16[64,16,1024]{2,0,1:T(8,128)(2,1)} async-done(((bf16[64,16,1024]{2,0,1:T(8,128)(2,1)}), bf16[64,16,1024]{2,0,1:T(8,128)(2,1)}, u32[]{:S(2)}, u32[]{:S(2)}) %all-to-all-start.1) | async-done | bytes 2097184 | tf_op jit(solution)/shard_map/all_to_all | solution.py:95
  163.7 2.8 and_select_fusion.3
  175.8 19.1 %collective-permute-done.1 = f32[1032,256]{1,0:T(8,128)} collective-permute-done((f32[1032,256]{1,0:T(8,128)}, f32[1032,256]{1,0:T(8,128)}, u32[]{:S(2)}, u32[]{:S(2)}) %collective-permute-start.1) | collective-permute-done | bytes 1056800 | tf_op jit(solution)/shard_map/ppermute | solution.py:17
  203.3 2.8 and_select_fusion.2
  209.8 3.0 fusion.10
  215.5 16.5 %collective-permute-done.2 = f32[1032,256]{1,0:T(8,128)} collective-permute-done((f32[1032,256]{1,0:T(8,128)}, f32[1032,256]{1,0:T(8,128)}, u32[]{:S(2)}, u32[]{:S(2)}) %collective-permute-start.2) | collective-permute-done | bytes 1056800 | tf_op jit(solution)/shard_map/ppermute | solution.py:17
  240.4 2.8 and_select_fusion.1
  252.5 17.3 %collective-permute-done.3 = f32[1032,256]{1,0:T(8,128)} collective-permute-done((f32[1032,256]{1,0:T(8,128)}, f32[1032,256]{1,0:T(8,128)}, u32[]{:S(2)}, u32[]{:S(2)}) %collective-permute-start.3) | collective-permute-done | bytes 1056800 | tf_op jit(solution)/shard_map/ppermute | solution.py:17
  278.2 2.8 and_select_fusion
  281.0 3.0 collective-permute-start.4
  288.8 16.6 %collective-permute-done.4 = f32[1032,256]{1,0:T(8,128)} collective-permute-done((f32[1032,256]{1,0:T(8,128)}, f32[1032,256]{1,0:T(8,128)}, u32[]{:S(2)}, u32[]{:S(2)}) %collective-permute-start.4) | collective-permute-done | bytes 1056800 | tf_op jit(solution)/shard_map/ppermute | solution.py:17
  308.1 3.3 fusion.87
  311.4 5.4 %fusion.14 = bf16[1024,1,256]{0,2,1:T(8,128)(2,1)S(1)} fusion(f32[1024,256]{0,1:T(8,128)S(1)} %copy.41, bf16[1024,1024]{1,0:T(8,128)(2,1)} %bitcast.98, f32[1032,256]{1,0:T(8,128)} %collective-permute-done.4, f32[1024]{0:T(1024)S(1)} %abs_maximum_fusion, f32[1024]{0:T(1024)S(1)} %bitcast.314), kind=kOutput, calls=%fused_computation.23 | convolution fusion | flops 3222274048 | bytes 4726784 | tf_op jit(solution)/shard_map/dot_general | solution.py:186
  318.7 24.0 %all_to_all.63 = bf16[16,2,8192]{2,1,0:T(2,128)(2,1)S(1)} all-to-all(bf16[16,2,8192]{2,1,0:T(2,128)(2,1)S(1)} %reshape.597), channel_id=1, replica_groups=mesh['seq'=16,'tensor'=16] {'tensor'}, dimensions={0} | all-to-all | bytes 1048576 | tf_op jit(solution)/shard_map/all_to_all | solution.py:189
  (207 shorter events, 72.8 us)
Async XLA Ops:
  1.3 20.3 %copy-start.10 = (bf16[64,4096]{1,0:T(8,128)(2,1)S(1)}, bf16[64,4096]{1,0:T(8,128)(2,1)}, u32[]{:S(2)}) copy-start(bf16[64,4096]{1,0:T(8,128)(2,1)} %param.9) | copy-start | bytes 1572868
  1.3 16.3 %all-to-all-start = ((bf16[64,16,2]{0,2,1:T(2,128)(2,1)}), bf16[64,16,2]{0,2,1:T(2,128)(2,1)S(1)}, u32[]{:S(2)}, u32[]{:S(2)}) async-start(bf16[64,16,2]{0,2,1:T(2,128)(2,1)} %bitcast.2), calls=%async_computation | async-start | bytes 16384 | tf_op jit(solution)/shard_map/all_to_all | solution.py:98
  17.7 21.3 %all-to-all-start.3 = ((bf16[64,16,256]{2,0,1:T(8,128)(2,1)}), bf16[64,16,256]{2,0,1:T(8,128)(2,1)S(1)}, u32[]{:S(2)}, u32[]{:S(2)}) async-start(bf16[64,16,256]{2,0,1:T(8,128)(2,1)} %bitcast.255), calls=%async_computation.3 | async-start | bytes 1048576 | tf_op jit(solution)/shard_map/all_to_all | solution.py:97
  39.0 80.5 %copy-start.5 = (bf16[64,16,256]{2,0,1:T(8,128)(2,1)}, bf16[64,16,256]{2,0,1:T(8,128)(2,1)S(1)}, u32[]{:S(2)}) copy-start(bf16[64,16,256]{2,0,1:T(8,128)(2,1)S(1)} %all-to-all-done.3) | copy-start | bytes 1572868
  40.6 52.1 %all-to-all-start.2 = ((bf16[64,16,1024]{2,0,1:T(8,128)(2,1)}), bf16[64,16,1024]{2,0,1:T(8,128)(2,1)S(1)}, u32[]{:S(2)}, u32[]{:S(2)}) async-start(bf16[64,16,1024]{2,0,1:T(8,128)(2,1)} %bitcast.264), calls=%async_computation.2 | async-start | bytes 4194304 | tf_op jit(solution)/shard_map/all_to_all | solution.py:96
  54.4 186.0 %copy-start.22 = (pred[256]{0:T(512)(128)(4,1)}, pred[256]{0:T(512)(128)(4,1)S(1)}, u32[]{:S(2)}) copy-start(pred[256]{0:T(512)(128)(4,1)S(1)} %iota_compare_fusion.4) | copy-start | bytes 772
  94.2 54.1 %all-to-all-start.1 = ((bf16[64,16,1024]{2,0,1:T(8,128)(2,1)}), bf16[64,16,1024]{2,0,1:T(8,128)(2,1)}, u32[]{:S(2)}, u32[]{:S(2)}) async-start(bf16[64,16,1024]{2,0,1:T(8,128)(2,1)} %bitcast.263), calls=%async_computation.1 | async-start | bytes 4194304 | tf_op jit(solution)/shard_map/all_to_all | solution.py:95
  128.0 27.7 %collective-permute-start = (f32[1032,256]{1,0:T(8,128)}, f32[1032,256]{1,0:T(8,128)}, u32[]{:S(2)}, u32[]{:S(2)}) collective-permute-start(f32[1032,256]{1,0:T(8,128)} %concatenate.14), channel_id=1, source_target_pairs={{0,16},{16,32},{32,48},{48,64},{64,80},{80,96},{96,112},{112,128},... | collective-permute-start | bytes 3170312 | tf_op jit(solution)/shard_map/ppermute | solution.py:17
  150.8 56.7 %copy-start = (bf16[4,64,1,1024]{3,1,0,2:T(8,128)(2,1)}, bf16[4,64,1,1024]{3,1,0,2:T(8,128)(2,1)S(1)}, u32[]{:S(2)}) copy-start(bf16[4,64,1,1024]{3,1,0,2:T(8,128)(2,1)S(1)} %get-tuple-element.35) | copy-start | bytes 1572868
  166.5 28.3 %collective-permute-start.1 = (f32[1032,256]{1,0:T(8,128)}, f32[1032,256]{1,0:T(8,128)}, u32[]{:S(2)}, u32[]{:S(2)}) collective-permute-start(f32[1032,256]{1,0:T(8,128)} %and_select_fusion.3), channel_id=1, source_target_pairs={{0,32},{16,48},{32,64},{48,80},{64,96},{80,112},{96,128},{112,144}... | collective-permute-start | bytes 3170312 | tf_op jit(solution)/shard_map/ppermute | solution.py:17
  171.9 37.3 %copy-start.27 = (f32[256]{0:T(256)}, f32[256]{0:T(256)S(1)}, u32[]{:S(2)}) copy-start(f32[256]{0:T(256)S(1)} %get-tuple-element.20) | copy-start | bytes 3076
  203.3 6.0 %copy-start.7 = (bf16[4,64,1,1024]{3,1,0,2:T(8,128)(2,1)S(1)}, bf16[4,64,1,1024]{3,1,0,2:T(8,128)(2,1)}, u32[]{:S(2)}) copy-start(bf16[4,64,1,1024]{3,1,0,2:T(8,128)(2,1)} %get-tuple-element.34) | copy-start | bytes 1572868
  206.1 25.9 %collective-permute-start.2 = (f32[1032,256]{1,0:T(8,128)}, f32[1032,256]{1,0:T(8,128)}, u32[]{:S(2)}, u32[]{:S(2)}) collective-permute-start(f32[1032,256]{1,0:T(8,128)} %and_select_fusion.2), channel_id=1, source_target_pairs={{0,64},{16,80},{32,96},{48,112},{64,128},{80,144},{96,160},{112,17... | collective-permute-start | bytes 3170312 | tf_op jit(solution)/shard_map/ppermute | solution.py:17
  240.4 5.3 %copy-start.4 = (f32[1024,256]{1,0:T(8,128)S(1)}, f32[1024,256]{1,0:T(8,128)}, u32[]{:S(2)}) copy-start(f32[1024,256]{1,0:T(8,128)} %fusion.10) | copy-start | bytes 3145732
  243.2 26.6 %collective-permute-start.3 = (f32[1032,256]{1,0:T(8,128)}, f32[1032,256]{1,0:T(8,128)}, u32[]{:S(2)}, u32[]{:S(2)}) collective-permute-start(f32[1032,256]{1,0:T(8,128)} %and_select_fusion.1), channel_id=1, source_target_pairs={{0,128},{16,144},{32,160},{48,176},{64,192},{80,208},{96,224},{112... | collective-permute-start | bytes 3170312 | tf_op jit(solution)/shard_map/ppermute | solution.py:17
  248.4 29.8 %copy-start.23 = (pred[256]{0:T(512)(128)(4,1)S(1)}, pred[256]{0:T(512)(128)(4,1)}, u32[]{:S(2)}) copy-start(pred[256]{0:T(512)(128)(4,1)} %copy-done.22) | copy-start | bytes 772
  278.2 5.9 %copy-start.12 = (bf16[4,64,1,256]{3,1,0,2:T(8,128)(2,1)S(1)}, bf16[4,64,1,256]{3,1,0,2:T(8,128)(2,1)}, u32[]{:S(2)}) copy-start(bf16[4,64,1,256]{3,1,0,2:T(8,128)(2,1)} %get-tuple-element.62) | copy-start | bytes 393220
  278.2 5.9 %copy-start.17 = (f32[256,256]{0,1:T(8,128)S(1)}, f32[256,256]{0,1:T(8,128)}, u32[]{:S(2)}) copy-start(f32[256,256]{0,1:T(8,128)} %get-tuple-element.97) | copy-start | bytes 786436
  278.2 6.3 %copy-start.11 = (bf16[4,64,1,256]{3,1,0,2:T(8,128)(2,1)S(1)}, bf16[4,64,1,256]{3,1,0,2:T(8,128)(2,1)}, u32[]{:S(2)}) copy-start(bf16[4,64,1,256]{3,1,0,2:T(8,128)(2,1)} %get-tuple-element.61) | copy-start | bytes 393220
  281.0 24.4 %collective-permute-start.4 = (f32[1032,256]{1,0:T(8,128)}, f32[1032,256]{1,0:T(8,128)}, u32[]{:S(2)}, u32[]{:S(2)}) collective-permute-start(f32[1032,256]{1,0:T(8,128)} %and_select_fusion), channel_id=1, source_target_pairs={{0,16},{16,32},{32,48},{48,64},{64,80},{80,96},{96,112},{112,128},... | collective-permute-start | bytes 3170312 | tf_op jit(solution)/shard_map/ppermute | solution.py:17
  288.4 19.6 %copy-start.28 = (f32[256]{0:T(256)S(1)}, f32[256]{0:T(256)}, u32[]{:S(2)}) copy-start(f32[256]{0:T(256)} %copy-done.27) | copy-start | bytes 3076
  288.4 19.6 %copy-start.29 = (f32[256]{0:T(256)S(1)}, f32[256]{0:T(256)}, u32[]{:S(2)}) copy-start(f32[256]{0:T(256)} %get-tuple-element.78) | copy-start | bytes 3076
  288.4 19.6 %copy-start.30 = (f32[256]{0:T(256)S(1)}, f32[256]{0:T(256)}, u32[]{:S(2)}) copy-start(f32[256]{0:T(256)} %get-tuple-element.13) | copy-start | bytes 3076
  288.4 19.6 %copy-start.31 = (f32[256]{0:T(256)S(1)}, f32[256]{0:T(256)}, u32[]{:S(2)}) copy-start(f32[256]{0:T(256)} %get-tuple-element.15) | copy-start | bytes 3076
  (17 other events, 47.9 us)

commit v2 on v1

--- a/solution.py
+++ b/solution.py
@@ -15,6 +15,10 @@
     count = lax.axis_size(axis)
     initial, last = (max(0, -steps), min(count, count - steps))
     return lax.ppermute(value, axis, [(source, source + steps) for source in range(initial, last)])
+
+
+def shifted_narrow(value, axis, steps):
+    return shifted(value.astype(jnp.bfloat16), axis, steps).astype(jnp.float32)
 
 
 def meta_row(head_dim, column_count):
@@ -87,20 +91,31 @@
             row_count, tensor_size, width
         )
 
-    query_send = spread_heads(queries, head_dim)
-    key_send = spread_heads(key_rows, head_dim)
+    pair_q_k = jnp.stack(
+        [
+            queries.reshape(row_count, head_count, head_dim),
+            key_rows.reshape(row_count, head_count, head_dim),
+        ],
+        axis=2,
+    )
+    pair_send = jnp.broadcast_to(
+        pair_q_k[:, :, None], (row_count, head_count, group_size // 2, 2, head_dim)
+    ).reshape(row_count, tensor_size, head_dim)
     value_send = values.reshape(row_count, tensor_size, column_count)
+    both_send = jnp.concatenate([pair_send, value_send], axis=2)
     gate_send = spread_heads(jnp.stack([input_gate, forget_gate], axis=2), 2)
-    query_all, key_all, value_all, gate_all = (
-        lax.all_to_all(query_send, "tensor", split_axis=1, concat_axis=0, tiled=True),
-        lax.all_to_all(key_send, "tensor", split_axis=1, concat_axis=0, tiled=True),
-        lax.all_to_all(value_send, "tensor", split_axis=1, concat_axis=0, tiled=True),
-        lax.all_to_all(gate_send, "tensor", split_axis=1, concat_axis=0, tiled=True),
-    )
+    both_all = lax.all_to_all(both_send, "tensor", split_axis=1, concat_axis=0, tiled=True)
+    gate_all = lax.all_to_all(gate_send, "tensor", split_axis=1, concat_axis=0, tiled=True)
+    both_all = both_all.reshape(-1, head_dim + column_count)
+    own_part = both_all[:, :head_dim]
+    value_all = both_all[:, head_dim:]
+    other_part = lax.ppermute(
+        own_part, "tensor", [(index, index ^ 1) for index in range(tensor_size)]
+    )
+    is_even = lax.axis_index("tensor") % 2 == 0
+    query_all = jnp.where(is_even, own_part, other_part)
+    key_all = jnp.where(is_even, other_part, own_part)
     token_count = query_all.shape[0]
-    query_all = query_all.reshape(token_count, head_dim)
-    key_all = key_all.reshape(token_count, head_dim)
-    value_all = value_all.reshape(token_count, column_count)
     gate_f = gate_all.reshape(token_count, 2).astype(jnp.float32)
     gate_in = gate_f[:, 0]
     log_forget = jax.nn.log_sigmoid(gate_f[:, 1])
@@ -114,9 +129,9 @@
     scanned = packed
     shift = 1
     while shift < lax.axis_size("seq"):
-        scanned = combine_packed(shifted(scanned, "seq", shift), scanned, head_dim)
+        scanned = combine_packed(shifted_narrow(scanned, "seq", shift), scanned, head_dim)
         shift *= 2
-    incoming = shifted(scanned, "seq", 1)
+    incoming = shifted_narrow(scanned, "seq", 1)
     in_row = meta_row(head_dim, column_count)
     in_state = incoming[:head_dim]
     in_norm = incoming[head_dim:in_row].reshape(head_dim)

time: 355 us -> 292 us (0.82)
  waiting for transfers between devices: 147 us -> 81.6 us
  other arithmetic: 29.7 us -> 50.9 us
  local copies, waits for them, and re-layouts: 38.3 us -> 28.7 us
  starting transfers between devices: 31.9 us -> 26 us
    ppermute x5, waiting for transfers between devices: 69.5 us -> 29.1 us  [shifted(): lax.ppermute(value, axis, [(source, source + steps) for source in range(i...]
    all_to_all x3 -> x1, waiting for transfers between devices: 72.8 us -> 51.5 us  [on_device(): lax.all_to_all(both_send, 'tensor', split_axis=1, concat_axis=0, tiled=True)]
    reduce_sum x2, other arithmetic: 0.42 us -> 15.2 us  [on_device(): variance = jnp.mean(centered * centered, axis=2, keepdims=True)]
    convert_element_type x0 -> x5, other arithmetic: none -> 10.4 us  [shifted_narrow(): return shifted(value.astype(jnp.bfloat16), axis, steps).astype(jnp.float32)]
    select_n x4 -> x1, other arithmetic: 11.3 us -> 1.81 us  [on_device(): query_all = jnp.where(is_even, own_part, other_part)]
    all_to_all x3 -> x1, starting transfers between devices: 12.6 us -> 6.41 us  [on_device(): lax.all_to_all(both_send, 'tensor', split_axis=1, concat_axis=0, tiled=True)]
    slice x6 -> x3, local copies, waits for them, and re-layouts: 4.56 us -> 0.01 us  [on_device(): unused, outputs = lax.scan(span_step, initial, blocks_in, unroll=True)]
    broadcast_in_dim x5 -> x1, local copies, waits for them, and re-layouts: 4.9 us -> 0.61 us  [spread_heads(): jnp.broadcast_to(shaped, (row_count, head_count, group_size, width))]
  transfers between devices with their start and end apart: 9 -> 8, of which waited for: 8 -> 6; matrix products, arithmetic and copies ran while one was open for 17% -> 18% of each run, Pallas kernels for 0% -> 0%
where the time goes in v2:
time: 292 us; the launch traced here: 287 us
  waiting for transfers between devices  81.6 us (28%)
  other arithmetic  50.9 us (17%)
  between operations  45.2 us (15%)
  matrix products  29.8 us (10%)
  local copies, waits for them, and re-layouts  28.7 us (10%)
  starting transfers between devices  26 us (9%)
  blocking collectives  25.2 us (9%)
    all_to_all x1, waiting for transfers between devices, on_device(): lax.all_to_all(both_send, 'tensor', split_axis=1, concat_axis=0, tiled=True)  51.5 us
    ppermute x5, waiting for transfers between devices, shifted(): lax.ppermute(value, axis, [(source, source + steps) for source in range(i...  29.1 us
    all_to_all x1, blocking collectives, on_device(): lax.all_to_all(hidden.reshape(token_count, 1, column_count), 'tensor', sp...  25.2 us
    reduce_sum x2, other arithmetic, on_device(): variance = jnp.mean(centered * centered, axis=2, keepdims=True)  15.2 us
    convert_element_type x5, other arithmetic, shifted_narrow(): return shifted(value.astype(jnp.bfloat16), axis, steps).astype(jnp.float32)  10.4 us
    ppermute x5, starting transfers between devices, shifted(): lax.ppermute(value, axis, [(source, source + steps) for source in range(i...  9.37 us
    dot_general x3, matrix products, span_step(): jnp.dot(scaled_keys.T, value_f, precision=precise)  9.34 us
    all_to_all x1, starting transfers between devices, on_device(): lax.all_to_all(gate_send, 'tensor', split_axis=1, concat_axis=0, tiled=True)  9.15 us
  transfers between devices with their start and end apart: 8, of which 6 were waited for; matrix products, arithmetic and copies ran while one was open for 18% of the time, Pallas kernels for 0%

profile of v2, /device:TPU:23, one launch (start us, length us, event | category | flops | bytes accessed | tf_op | source)
XLA Modules:
  0.0 287.4 jit_solution(2255803454818502155)
XLA Ops:
  1.3 9.2 %all-to-all-start = ((bf16[64,16,2]{0,2,1:T(2,128)(2,1)}), bf16[64,16,2]{0,2,1:T(2,128)(2,1)S(1)}, u32[]{:S(2)}, u32[]{:S(2)}) async-start(bf16[64,16,2]{0,2,1:T(2,128)(2,1)} %bitcast.2), calls=%async_computation | async-start | bytes 16384 | tf_op jit(solution)/shard_map/all_to_all | solution.py:108
  17.4 6.4 %all-to-all-start.1 = ((bf16[64,16,1280]{2,0,1:T(8,128)(2,1)}), bf16[64,16,1280]{2,0,1:T(8,128)(2,1)S(1)}, u32[]{:S(2)}, u32[]{:S(2)}) async-start(bf16[64,16,1280]{2,0,1:T(8,128)(2,1)} %pad_maximum_fusion), calls=%async_computation.1 | async-start | bytes 5242880 | tf_op jit(solution)/shard_map/all_to_all | solution.py:107
  31.9 51.5 %all-to-all-done.1 = bf16[64,16,1280]{2,0,1:T(8,128)(2,1)S(1)} async-done(((bf16[64,16,1280]{2,0,1:T(8,128)(2,1)}), bf16[64,16,1280]{2,0,1:T(8,128)(2,1)S(1)}, u32[]{:S(2)}, u32[]{:S(2)}) %all-to-all-start.1) | async-done | bytes 2621472 | tf_op jit(solution)/shard_map/all_to_all | solution.py:107
  101.5 4.6 %fusion.1 = f32[1024,256]{1,0:T(8,128)} fusion(bf16[1024,1024]{1,0:T(8,128)(2,1)S(1)} %get-tuple-element.32, f32[1024]{0:T(1024)S(1)} %select_multiply_fusion, bf16[1024,1280]{1,0:T(8,128)(2,1)S(1)} %bitcast.149), kind=kOutput, calls=%fused_computation.2 | convolution fusion | flops 3223322624 | bytes 3674112 | tf_op jit(solution)/shard_map/dot_general | solution.py:39
  106.1 4.0 %concatenate.18 = f32[1032,256]{1,0:T(8,128)} concatenate(f32[1024,256]{1,0:T(8,128)} %fusion.1, f32[4,256]{1,0:T(4,128)S(1)} %reshape.401, f32[1,256]{1,0:T(1,128)S(1)} %compare_select_fusion.3, f32[3,256]{1,0:T(4,128)S(1)} %broadcast_in_dim.193), dimensions={0} | concatenate | bytes 2113536 | tf_op jit(solution)/shard_map/concatenate | solution.py:56
  111.4 3.2 %collective-permute-start.1 = (bf16[1032,256]{1,0:T(8,128)(2,1)S(1)}, bf16[1032,256]{1,0:T(8,128)(2,1)S(1)}, u32[]{:S(2)}, u32[]{:S(2)}) collective-permute-start(bf16[1032,256]{1,0:T(8,128)(2,1)S(1)} %convert_element_type.127), channel_id=1, source_target_pairs={{0,16},{16,32},{32,48},{48,64},{64,80},{80,96},{96,112},{112,128},... | collective-permute-start | bytes 1585160 | tf_op jit(solution)/shard_map/ppermute | solution.py:17
  117.3 4.4 %multiply_add_fusion.5 = (f32[256]{0:T(256)S(1)}, f32[256]{0:T(256)S(1)}, f32[256]{0:T(256)S(1)}, f32[256]{0:T(256)S(1)}, f32[256]{0:T(256)S(1)}) fusion(f32[256]{0:T(256)S(1)} %get-tuple-element.85, f32[256]{0:T(256)S(1)} %bitcast.185, f32[256]{0:T(256)S(1)} %add_bitcast_fusion.4, s32[]{:T(128)} %bitcast.14, s32[1024]{0:T(1024)S(1)} %copy-done.17, ...), kind=kLoop, calls=%fused_computation.142 | loop fusion | flops 4864 | bytes 16412 | tf_op jit(solution)/shard_map/eval_jaxpr/add | solution.py:162
  137.8 2.4 fusion.83
  142.1 3.1 %convolution_add_fusion.2 = f32[1024,256]{1,0:T(8,128)} fusion(f32[256]{0:T(256)S(1)} %get-tuple-element.60, f32[]{:T(128)S(6)} %mul.307, bf16[1024,1024]{1,0:T(8,128)(2,1)} %copy-done.2, bf16[1024,1280]{1,0:T(8,128)(2,1)S(1)} %bitcast.155), kind=kOutput, calls=%fused_computation.13 | convolution fusion | flops 806092800 | bytes 1704964 | tf_op jit(solution)/shard_map/eval_jaxpr/dot_general | solution.py:172
  147.1 10.1 %collective-permute-done.2 = bf16[1032,256]{1,0:T(8,128)(2,1)} collective-permute-done((bf16[1032,256]{1,0:T(8,128)(2,1)}, bf16[1032,256]{1,0:T(8,128)(2,1)}, u32[]{:S(2)}, u32[]{:S(2)}) %collective-permute-start.2) | collective-permute-done | bytes 528416 | tf_op jit(solution)/shard_map/ppermute | solution.py:17
  165.6 2.5 fusion.82
  169.4 2.4 fusion.16
  171.8 3.1 %convolution_add_fusion.1 = f32[1024,256]{1,0:T(8,128)} fusion(f32[1024,256]{1,0:T(8,128)S(1)} %copy-done.5, f32[256]{0:T(256)S(1)} %get-tuple-element.61, f32[]{:T(128)S(6)} %mul.318, bf16[1024,1024]{1,0:T(8,128)(2,1)} %copy-done.2, bf16[1024,1280]{1,0:T(8,128)(2,1)S(1)} %bitcast.156), kind=kOutput, calls=%fused_computation.12 | convolution fusion | flops 806354944 | bytes 2753540 | tf_op jit(solution)/shard_map/eval_jaxpr/dot_general | solution.py:172
  176.8 5.9 %collective-permute-done.3 = bf16[1032,256]{1,0:T(8,128)(2,1)} collective-permute-done((bf16[1032,256]{1,0:T(8,128)(2,1)}, bf16[1032,256]{1,0:T(8,128)(2,1)}, u32[]{:S(2)}, u32[]{:S(2)}) %collective-permute-start.3) | collective-permute-done | bytes 528416 | tf_op jit(solution)/shard_map/ppermute | solution.py:17
  191.1 2.5 fusion.81
  195.0 2.3 fusion.15
  197.2 3.1 %convolution_add_fusion = f32[1024,256]{1,0:T(8,128)} fusion(f32[1024,256]{1,0:T(8,128)S(1)} %copy-done.4, f32[256]{0:T(256)S(1)} %get-tuple-element.62, f32[]{:T(128)S(6)} %mul.330, bf16[1024,1024]{1,0:T(8,128)(2,1)} %copy-done.2, bf16[1024,1280]{1,0:T(8,128)(2,1)S(1)} %bitcast.157), kind=kOutput, calls=%fused_computation.11 | convolution fusion | flops 806354944 | bytes 2753540 | tf_op jit(solution)/shard_map/eval_jaxpr/dot_general | solution.py:172
  202.3 6.7 %collective-permute-done.4 = bf16[1032,256]{1,0:T(8,128)(2,1)} collective-permute-done((bf16[1032,256]{1,0:T(8,128)(2,1)}, bf16[1032,256]{1,0:T(8,128)(2,1)}, u32[]{:S(2)}, u32[]{:S(2)}) %collective-permute-start.4) | collective-permute-done | bytes 528416 | tf_op jit(solution)/shard_map/ppermute | solution.py:17
  218.7 2.3 collective-permute-start.5
  224.8 6.5 %collective-permute-done.5 = bf16[1032,256]{1,0:T(8,128)(2,1)S(1)} collective-permute-done((bf16[1032,256]{1,0:T(8,128)(2,1)S(1)}, bf16[1032,256]{1,0:T(8,128)(2,1)S(1)}, u32[]{:S(2)}, u32[]{:S(2)}) %collective-permute-start.5) | collective-permute-done | bytes 528416 | tf_op jit(solution)/shard_map/ppermute | solution.py:17
  233.4 2.1 fusion.6
  237.2 25.2 %all_to_all.33 = bf16[16,2,8192]{2,1,0:T(2,128)(2,1)S(1)} all-to-all(bf16[16,2,8192]{2,1,0:T(2,128)(2,1)S(1)} %reshape.427), channel_id=1, replica_groups=mesh['seq'=16,'tensor'=16] {'tensor'}, dimensions={0} | all-to-all | bytes 1048576 | tf_op jit(solution)/shard_map/all_to_all | solution.py:204
  266.2 2.4 fusion.78
  268.7 15.2 %multiply_reduce_fusion = f32[64,16]{0,1:T(8,128)S(1)} fusion(f32[64,16]{0,1:T(8,128)S(1)} %bitcast.170, bf16[16,64,1,256]{3,2,1,0:T(2,128)(2,1)S(1)} %bitcast.159), kind=kLoop, calls=%fused_computation.49 | loop fusion | flops 1047552 | bytes 532480 | tf_op jit(solution)/shard_map/reduce_sum | solution.py:214
  (164 shorter events, 61.1 us)
Async XLA Ops:
  1.3 16.1 %all-to-all-start = ((bf16[64,16,2]{0,2,1:T(2,128)(2,1)}), bf16[64,16,2]{0,2,1:T(2,128)(2,1)S(1)}, u32[]{:S(2)}, u32[]{:S(2)}) async-start(bf16[64,16,2]{0,2,1:T(2,128)(2,1)} %bitcast.2), calls=%async_computation | async-start | bytes 16384 | tf_op jit(solution)/shard_map/all_to_all | solution.py:108
  16.5 7.4 %copy-start.17 = (s32[1024]{0:T(1024)S(1)}, s32[1024]{0:T(1024)}, u32[]{:S(2)}) copy-start(s32[1024]{0:T(1024)} %param.13) | copy-start | bytes 12292
  17.4 66.0 %all-to-all-start.1 = ((bf16[64,16,1280]{2,0,1:T(8,128)(2,1)}), bf16[64,16,1280]{2,0,1:T(8,128)(2,1)S(1)}, u32[]{:S(2)}, u32[]{:S(2)}) async-start(bf16[64,16,1280]{2,0,1:T(8,128)(2,1)} %pad_maximum_fusion), calls=%async_computation.1 | async-start | bytes 5242880 | tf_op jit(solution)/shard_map/all_to_all | solution.py:107
  85.1 15.6 %collective-permute-start = (bf16[1024,1024]{1,0:T(8,128)(2,1)}, bf16[1024,1024]{1,0:T(8,128)(2,1)}, u32[]{:S(2)}, u32[]{:S(2)}) collective-permute-start(bf16[1024,1024]{1,0:T(8,128)(2,1)} %slice.350), channel_id=1, source_target_pairs={{0,1},{1,0},{2,3},{3,2},{4,5},{5,4},{6,7},{7,6},{8,9},{9,8},{10,11... | collective-permute-start | bytes 6291464 | tf_op jit(solution)/shard_map/ppermute | solution.py:112
  101.5 4.6 %copy-start.2 = (bf16[1024,1024]{1,0:T(8,128)(2,1)}, bf16[1024,1024]{1,0:T(8,128)(2,1)S(1)}, u32[]{:S(2)}) copy-start(bf16[1024,1024]{1,0:T(8,128)(2,1)S(1)} %get-tuple-element.32) | copy-start | bytes 6291460
  111.4 5.6 %copy-start.3 = (bf16[1024,1024]{1,0:T(8,128)(2,1)S(1)}, bf16[1024,1024]{1,0:T(8,128)(2,1)}, u32[]{:S(2)}) copy-start(bf16[1024,1024]{1,0:T(8,128)(2,1)} %copy-done.2) | copy-start | bytes 6291460
  111.4 17.8 %collective-permute-start.1 = (bf16[1032,256]{1,0:T(8,128)(2,1)S(1)}, bf16[1032,256]{1,0:T(8,128)(2,1)S(1)}, u32[]{:S(2)}, u32[]{:S(2)}) collective-permute-start(bf16[1032,256]{1,0:T(8,128)(2,1)S(1)} %convert_element_type.127), channel_id=1, source_target_pairs={{0,16},{16,32},{32,48},{48,64},{64,80},{80,96},{96,112},{112,128},... | collective-permute-start | bytes 1585160 | tf_op jit(solution)/shard_map/ppermute | solution.py:17
  116.4 11.9 %copy-start = (bf16[1024,1024]{1,0:T(8,128)(2,1)}, bf16[1024,1024]{1,0:T(8,128)(2,1)S(1)}, u32[]{:S(2)}) copy-start(bf16[1024,1024]{1,0:T(8,128)(2,1)S(1)} %broadcast_select_fusion.1) | copy-start | bytes 6291460
  140.2 5.0 %copy-start.7 = (f32[1032,256]{1,0:T(8,128)}, f32[1032,256]{1,0:T(8,128)S(1)}, u32[]{:S(2)}) copy-start(f32[1032,256]{1,0:T(8,128)S(1)} %get-tuple-element.30) | copy-start | bytes 3170308
  140.2 17.0 %collective-permute-start.2 = (bf16[1032,256]{1,0:T(8,128)(2,1)}, bf16[1032,256]{1,0:T(8,128)(2,1)}, u32[]{:S(2)}, u32[]{:S(2)}) collective-permute-start(bf16[1032,256]{1,0:T(8,128)(2,1)} %get-tuple-element.29), channel_id=1, source_target_pairs={{0,32},{16,48},{32,64},{48,80},{64,96},{80,112},{96,128},{112,144}... | collective-permute-start | bytes 1585160 | tf_op jit(solution)/shard_map/ppermute | solution.py:17
  165.6 3.8 %copy-start.5 = (f32[1024,256]{1,0:T(8,128)S(1)}, f32[1024,256]{1,0:T(8,128)}, u32[]{:S(2)}) copy-start(f32[1024,256]{1,0:T(8,128)} %convolution_add_fusion.2) | copy-start | bytes 3145732
  168.1 6.9 %copy-start.8 = (f32[1032,256]{1,0:T(8,128)}, f32[1032,256]{1,0:T(8,128)S(1)}, u32[]{:S(2)}) copy-start(f32[1032,256]{1,0:T(8,128)S(1)} %get-tuple-element.28) | copy-start | bytes 3170308
  168.1 14.6 %collective-permute-start.3 = (bf16[1032,256]{1,0:T(8,128)(2,1)}, bf16[1032,256]{1,0:T(8,128)(2,1)}, u32[]{:S(2)}, u32[]{:S(2)}) collective-permute-start(bf16[1032,256]{1,0:T(8,128)(2,1)} %get-tuple-element.27), channel_id=1, source_target_pairs={{0,64},{16,80},{32,96},{48,112},{64,128},{80,144},{96,160},{112,17... | collective-permute-start | bytes 1585160 | tf_op jit(solution)/shard_map/ppermute | solution.py:17
  174.9 20.0 %copy-start.15 = (f32[256,256]{1,0:T(8,128)S(1)}, f32[256,256]{1,0:T(8,128)}, u32[]{:S(2)}) copy-start(f32[256,256]{1,0:T(8,128)} %fusion.70) | copy-start | bytes 786436
  191.1 6.1 %copy-start.4 = (f32[1024,256]{1,0:T(8,128)S(1)}, f32[1024,256]{1,0:T(8,128)}, u32[]{:S(2)}) copy-start(f32[1024,256]{1,0:T(8,128)} %convolution_add_fusion.1) | copy-start | bytes 3145732
  193.7 6.7 %copy-start.6 = (f32[1032,256]{1,0:T(8,128)}, f32[1032,256]{1,0:T(8,128)S(1)}, u32[]{:S(2)}) copy-start(f32[1032,256]{1,0:T(8,128)S(1)} %get-tuple-element.26) | copy-start | bytes 3170308
  193.7 15.3 %collective-permute-start.4 = (bf16[1032,256]{1,0:T(8,128)(2,1)}, bf16[1032,256]{1,0:T(8,128)(2,1)}, u32[]{:S(2)}, u32[]{:S(2)}) collective-permute-start(bf16[1032,256]{1,0:T(8,128)(2,1)} %get-tuple-element.25), channel_id=1, source_target_pairs={{0,128},{16,144},{32,160},{48,176},{64,192},{80,208},{96,224},{112... | collective-permute-start | bytes 1585160 | tf_op jit(solution)/shard_map/ppermute | solution.py:17
  200.4 20.6 %copy-start.1 = (bf16[1024,1024]{1,0:T(8,128)(2,1)S(1)}, bf16[1024,1024]{1,0:T(8,128)(2,1)}, u32[]{:S(2)}) copy-start(bf16[1024,1024]{1,0:T(8,128)(2,1)} %copy-done) | copy-start | bytes 6291460
  216.9 6.1 %copy-start.9 = (f32[1024,256]{1,0:T(8,128)S(1)}, f32[1024,256]{1,0:T(8,128)}, u32[]{:S(2)}) copy-start(f32[1024,256]{1,0:T(8,128)} %convolution_add_fusion) | copy-start | bytes 3145732
  218.7 12.6 %collective-permute-start.5 = (bf16[1032,256]{1,0:T(8,128)(2,1)S(1)}, bf16[1032,256]{1,0:T(8,128)(2,1)S(1)}, u32[]{:S(2)}, u32[]{:S(2)}) collective-permute-start(bf16[1032,256]{1,0:T(8,128)(2,1)S(1)} %fusion.19), channel_id=1, source_target_pairs={{0,16},{16,32},{32,48},{48,64},{64,80},{80,96},{96,112},{112,128},... | collective-permute-start | bytes 1585160 | tf_op jit(solution)/shard_map/ppermute | solution.py:17
  221.0 2.7 copy-start.11
  221.0 2.7 copy-start.16
  284.9 1.3 copy-start.14
  284.9 1.3 copy-start.18
  (4 other events, 3.9 us)

commit v3 on v2

--- a/solution.py
+++ b/solution.py
@@ -75,6 +75,28 @@
     return jnp.where((rows == row) & (lane < 3), meta, body)
 
 
+def prefix_from_all(packed, head_dim):
+    seq_count = lax.axis_size("seq")
+    column_count = packed.shape[1]
+    row = meta_row(head_dim, column_count)
+    gathered = lax.all_gather(packed.astype(jnp.bfloat16), "seq")
+    meta = lax.all_gather(packed[row, :8], "seq")
+    decay, first, last = meta[:, 0], meta[:, 1], meta[:, 2]
+    me = lax.axis_index("seq")
+    order = jnp.arange(seq_count)
+    previous_last = jnp.concatenate([jnp.zeros((1,), jnp.float32), last[:-1]])
+    carry = decay * (previous_last == first).astype(jnp.float32)
+    carry = jnp.where(order < me, carry, 1.0)
+    after = jnp.cumprod(carry[::-1])[::-1]
+    weight = jnp.concatenate([after[1:], jnp.ones((1,), jnp.float32)])
+    weight = jnp.where(order < me, weight, 0.0)
+    total = jnp.einsum("s,src->rc", weight, gathered.astype(jnp.float32))
+    in_last = jnp.where(me > 0, last[jnp.maximum(me - 1, 0)], 0.0)
+    lane = jnp.arange(column_count)[None, :]
+    rows = jnp.arange(packed.shape[0])[:, None]
+    return jnp.where((rows == row) & (lane == 2), in_last, total)
+
+
 def on_device(
     queries, key_rows, values, input_gate, forget_gate, segment_ids, output_gate, norm_gain
 ):
@@ -126,12 +148,7 @@
     packed = pack_summary(
         query_all, key_all, value_all, gate_in, log_forget, segment_ids, key_scale
     )
-    scanned = packed
-    shift = 1
-    while shift < lax.axis_size("seq"):
-        scanned = combine_packed(shifted_narrow(scanned, "seq", shift), scanned, head_dim)
-        shift *= 2
-    incoming = shifted_narrow(scanned, "seq", 1)
+    incoming = prefix_from_all(packed, head_dim)
     in_row = meta_row(head_dim, column_count)
     in_state = incoming[:head_dim]
     in_norm = incoming[head_dim:in_row].reshape(head_dim)

time: 292 us -> 252 us (0.86)
  blocking collectives: 25.2 us -> 111 us
  waiting for transfers between devices: 81.6 us -> 24.7 us
  starting transfers between devices: 26 us -> 3.8 us
  between operations: 45.2 us -> 26 us
  other arithmetic: 50.9 us -> 39.8 us
  local copies, waits for them, and re-layouts: 28.7 us -> 18.2 us
  matrix products: 29.8 us -> 24.2 us
    all_to_all x0 -> x1, blocking collectives: none -> 71.1 us  [on_device(): lax.all_to_all(both_send, 'tensor', split_axis=1, concat_axis=0, tiled=True)]
    all_to_all x1 -> x0, waiting for transfers between devices: 51.5 us -> none  [on_device(): lax.all_to_all(both_send, 'tensor', split_axis=1, concat_axis=0, tiled=True)]
    ppermute x5 -> x0, waiting for transfers between devices: 29.1 us -> none  [shifted(): lax.ppermute(value, axis, [(source, source + steps) for source in range(i...]
    all_gather x0 -> x1, waiting for transfers between devices: none -> 20.8 us  [prefix_from_all(): gathered = lax.all_gather(packed.astype(jnp.bfloat16), 'seq')]
    all_gather x0 -> x1, blocking collectives: none -> 15.3 us  [prefix_from_all(): meta = lax.all_gather(packed[row, :8], 'seq')]
    convert_element_type x5 -> x0, other arithmetic: 10.4 us -> none  [shifted_narrow(): return shifted(value.astype(jnp.bfloat16), axis, steps).astype(jnp.float32)]
    ppermute x5 -> x0, starting transfers between devices: 9.37 us -> none  [shifted(): lax.ppermute(value, axis, [(source, source + steps) for source in range(i...]
    slice x9 -> x5, local copies, waits for them, and re-layouts: 7.57 us -> 0.3 us  [the longest x2 0.22 us: prefix_from_all(): weight = jnp.concatenate([after[1:], jnp.ones((1,), jnp.float32)])]
  transfers between devices with their start and end apart: 8 -> 3, of which waited for: 6 -> 2; matrix products, arithmetic and copies ran while one was open for 18% -> 13% of each run, Pallas kernels for 0% -> 0%
where the time goes in v3:
time: 252 us; the launch traced here: 248 us
  blocking collectives  111 us (44%)
  other arithmetic  39.8 us (16%)
  between operations  26 us (10%)
  waiting for transfers between devices  24.7 us (10%)
  matrix products  24.2 us (10%)
  local copies, waits for them, and re-layouts  18.2 us (7%)
  starting transfers between devices  3.8 us (2%)
    all_to_all x1, blocking collectives, on_device(): lax.all_to_all(both_send, 'tensor', split_axis=1, concat_axis=0, tiled=True)  71.1 us
    all_to_all x1, blocking collectives, on_device(): lax.all_to_all(hidden.reshape(token_count, 1, column_count), 'tensor', sp...  24.9 us
    all_gather x1, waiting for transfers between devices, prefix_from_all(): gathered = lax.all_gather(packed.astype(jnp.bfloat16), 'seq')  20.8 us
    all_gather x1, blocking collectives, prefix_from_all(): meta = lax.all_gather(packed[row, :8], 'seq')  15.3 us
    reduce_sum x2, other arithmetic, on_device(): variance = jnp.mean(centered * centered, axis=2, keepdims=True)  15.2 us
    add x3, other arithmetic, span_step(): jnp.sum(weighted, axis=1)  6.94 us
    dot_general x1, matrix products, prefix_from_all(): total = jnp.einsum('s,src->rc', weight, gathered.astype(jnp.float32))  5.17 us
  transfers between devices with their start and end apart: 3, of which 2 were waited for; matrix products, arithmetic and copies ran while one was open for 13% of the time, Pallas kernels for 0%

profile of v3, /device:TPU:23, one launch (start us, length us, event | category | flops | bytes accessed | tf_op | source)
XLA Modules:
  0.0 247.9 jit_solution(13363437805440863836)
XLA Ops:
  6.5 1.1 copy.63
  7.7 1.4 stack_reshape.7
  11.1 71.1 %all_to_all.33 = bf16[64,16,1280]{2,0,1:T(8,128)(2,1)S(1)} all-to-all(bf16[64,16,1280]{2,0,1:T(8,128)(2,1)S(1)} %pad_maximum_fusion), channel_id=1, replica_groups=mesh['seq'=16,'tensor'=16] {'tensor'}, dimensions={1} | all-to-all | bytes 5242880 | tf_op jit(solution)/shard_map/all_to_all | solution.py:129
  82.2 1.6 slice.290
  84.5 3.8 %all-to-all-start = ((bf16[64,16,2]{0,2,1:T(2,128)(2,1)}), bf16[64,16,2]{0,2,1:T(2,128)(2,1)S(1)}, u32[]{:S(2)}, u32[]{:S(2)}) async-start(bf16[64,16,2]{0,2,1:T(2,128)(2,1)} %bitcast.2), calls=%async_computation | async-start | bytes 16384 | tf_op jit(solution)/shard_map/all_to_all | solution.py:130
  91.4 3.9 %all-to-all-done = bf16[64,16,2]{0,2,1:T(2,128)(2,1)S(1)} async-done(((bf16[64,16,2]{0,2,1:T(2,128)(2,1)}), bf16[64,16,2]{0,2,1:T(2,128)(2,1)S(1)}, u32[]{:S(2)}, u32[]{:S(2)}) %all-to-all-start) | async-done | bytes 4128 | tf_op jit(solution)/shard_map/all_to_all | solution.py:130
  97.3 1.3 select_multiply_fusion
  99.4 3.6 %fusion.9 = bf16[1,1024,256]{2,1,0:T(8,128)(2,1)S(1)} fusion(bf16[1024,1024]{1,0:T(8,128)(2,1)S(1)} %get-tuple-element.28, f32[1024]{0:T(1024)S(1)} %select_multiply_fusion, bf16[1024,1280]{1,0:T(8,128)(2,1)S(1)} %bitcast.144), kind=kOutput, calls=%fused_computation.19 | convolution fusion | flops 3223584768 | bytes 3149824 | tf_op jit(solution)/shard_map/dot_general | solution.py:39
  103.0 2.1 concatenate.43
  110.6 1.3 compare_select_fusion.7
  118.7 15.3 %all-gather = f32[16,1,8]{2,1,0:T(1,128)S(1)} all-gather(f32[1,1,8]{2,1,0:T(1,128)S(1)} %slice_bitcast_fusion.1), channel_id=1, replica_groups=mesh['seq'=16,'tensor'=16] {'seq'}, dimensions={0}, use_global_device_ids=true | all-gather | bytes 544 | tf_op jit(solution)/shard_map/all_gather | solution.py:83
  135.9 2.0 broadcast_select_fusion.1
  138.8 4.4 %multiply_add_fusion.5 = (f32[256]{0:T(256)S(1)}, f32[256]{0:T(256)S(1)}, f32[256]{0:T(256)S(1)}, f32[256]{0:T(256)S(1)}, f32[256]{0:T(256)S(1)}) fusion(f32[256]{0:T(256)S(1)} %get-tuple-element.57, f32[256]{0:T(256)S(1)} %bitcast.183, f32[256]{0:T(256)S(1)} %add_bitcast_fusion.4, s32[]{:T(128)} %bitcast.14, s32[1024]{0:T(1024)S(1)} %copy-done.7, ...), kind=kLoop, calls=%fused_computation.146 | loop fusion | flops 4864 | bytes 16412 | tf_op jit(solution)/shard_map/eval_jaxpr/add | solution.py:179
  145.4 1.9 multiply_add_fusion.4
  152.4 1.1 convolution_add_fusion.1
  157.5 20.8 %all-gather.3.cloned.1.call-done = bf16[16,1032,256]{2,1,0:T(8,128)(2,1)} async-done(((bf16[1,1032,256]{2,1,0:T(8,128)(2,1)}), bf16[16,1032,256]{2,1,0:T(8,128)(2,1)}) %all-gather.3.cloned.1.call-update) | async-done | bytes 8454160 | tf_op jit(solution)/shard_map/all_gather | solution.py:82
  178.2 5.2 %fusion = f32[1,1032,256]{2,0,1:T(1,128)S(1)} fusion(bf16[16,1032,256]{2,1,0:T(8,128)(2,1)} %all-gather.3.cloned.1.call-done, bf16[1]{0:T(256)(128)(2,1)} %constant.190, bf16[15]{0:T(256)(128)(2,1)S(1)} %slice.282, s32[]{:T(128)S(6)} %axis_index.25), kind=kOutput, calls=%fused_computation | convolution fusion | flops 8454240 | bytes 9510948 | tf_op jit(solution)/shard_map/s,src->rc/dot_general | solution.py:93
  185.2 1.7 fusion.101
  186.9 2.7 %fusion.10 = bf16[1024,1,256]{2,0,1:T(8,128)(2,1)} fusion(f32[1024,256]{1,0:T(8,128)S(1)} %bitcast.163, bf16[1024,1024]{1,0:T(8,128)(2,1)S(1)} %copy-done.1, f32[1032,256]{1,0:T(8,128)S(1)} %bitcast_select_fusion, f32[1024]{0:T(1024)S(1)} %abs_maximum_fusion, f32[1024]{0:T(1024)S(1)} %bitcast.176), kind=kOutput, calls=%fused_computation.20 | convolution fusion | flops 3222274048 | bytes 4726784 | tf_op jit(solution)/shard_map/dot_general | solution.py:218
  190.2 2.1 reduce.16
  192.5 24.9 %all_to_all.34 = bf16[16,2,8192]{2,1,0:T(2,128)(2,1)S(1)} all-to-all(bf16[16,2,8192]{2,1,0:T(2,128)(2,1)S(1)} %reshape.465), channel_id=1, replica_groups=mesh['seq'=16,'tensor'=16] {'tensor'}, dimensions={0} | all-to-all | bytes 1048576 | tf_op jit(solution)/shard_map/all_to_all | solution.py:221
  219.0 2.4 fusion.88
  221.5 15.2 %multiply_reduce_fusion = f32[64,16]{0,1:T(8,128)S(1)} fusion(f32[64,16]{0,1:T(8,128)S(1)} %bitcast.165, bf16[16,64,1,256]{3,2,1,0:T(2,128)(2,1)S(1)} %bitcast.154), kind=kLoop, calls=%fused_computation.50 | loop fusion | flops 1047552 | bytes 532480 | tf_op jit(solution)/shard_map/reduce_sum | solution.py:231
  239.9 1.2 fusion.31
  (135 shorter events, 30.0 us)
Async XLA Ops:
  6.5 2.6 %copy-start.5 = (bf16[64,4096]{1,0:T(8,128)(2,1)S(1)}, bf16[64,4096]{1,0:T(8,128)(2,1)}, u32[]{:S(2)}) copy-start(bf16[64,4096]{1,0:T(8,128)(2,1)} %param.8) | copy-start | bytes 1572868
  82.2 1.7 copy-start.9
  82.2 1.7 copy-start.10
  82.2 6.1 %copy-start.7 = (s32[1024]{0:T(1024)S(1)}, s32[1024]{0:T(1024)}, u32[]{:S(2)}) copy-start(s32[1024]{0:T(1024)} %param.13) | copy-start | bytes 12292
  83.9 14.7 %collective-permute-start = (bf16[1024,1024]{1,0:T(8,128)(2,1)}, bf16[1024,1024]{1,0:T(8,128)(2,1)}, u32[]{:S(2)}, u32[]{:S(2)}) collective-permute-start(bf16[1024,1024]{1,0:T(8,128)(2,1)} %slice.290), channel_id=1, source_target_pairs={{0,1},{1,0},{2,3},{3,2},{4,5},{5,4},{6,7},{7,6},{8,9},{9,8},{10,11... | collective-permute-start | bytes 6291464 | tf_op jit(solution)/shard_map/ppermute | solution.py:134
  84.5 10.8 %all-to-all-start = ((bf16[64,16,2]{0,2,1:T(2,128)(2,1)}), bf16[64,16,2]{0,2,1:T(2,128)(2,1)S(1)}, u32[]{:S(2)}, u32[]{:S(2)}) async-start(bf16[64,16,2]{0,2,1:T(2,128)(2,1)} %bitcast.2), calls=%async_computation | async-start | bytes 16384 | tf_op jit(solution)/shard_map/all_to_all | solution.py:130
  88.3 90.0 %all-gather.3.cloned.1.call-start = ((), (), s32[]{:S(2)}) async-start(), calls=%async_computation.3 | async-start | bytes 8982528 | tf_op jit(solution)/shard_map/all_gather | solution.py:82
  99.4 3.6 %copy-start.2 = (bf16[1024,1024]{1,0:T(8,128)(2,1)}, bf16[1024,1024]{1,0:T(8,128)(2,1)S(1)}, u32[]{:S(2)}) copy-start(bf16[1024,1024]{1,0:T(8,128)(2,1)S(1)} %get-tuple-element.28) | copy-start | bytes 6291460
  135.9 2.5 copy-start.3
  137.9 17.8 %copy-start = (bf16[1024,1024]{1,0:T(8,128)(2,1)}, bf16[1024,1024]{1,0:T(8,128)(2,1)S(1)}, u32[]{:S(2)}) copy-start(bf16[1024,1024]{1,0:T(8,128)(2,1)S(1)} %broadcast_select_fusion.1) | copy-start | bytes 6291460
  183.4 1.7 copy-start.1
  185.1 1.8 copy-start.4
  238.9 1.0 copy-start.6
  238.9 1.0 copy-start.8
Sparse Core Ops, SparseCore 0:
  105.2 73.0 all-gather.2

commit v4 on v3

--- a/solution.py
+++ b/solution.py
@@ -43,13 +43,18 @@
     rows = meta_row(head_dim, column_count) + 1
     padded = -(-rows // 8) * 8
     lane = jnp.arange(column_count)
+    decay_high = lax.reduce_precision(decay, exponent_bits=8, mantissa_bits=7)
     meta = jnp.where(
         lane == 0,
-        decay,
+        decay_high,
         jnp.where(
             lane == 1,
             (first_seg + 1).astype(jnp.float32),
-            jnp.where(lane == 2, (last_seg + 1).astype(jnp.float32), 0.0),
+            jnp.where(
+                lane == 2,
+                (last_seg + 1).astype(jnp.float32),
+                jnp.where(lane == 3, decay - decay_high, 0.0),
+            ),
         ),
     )
     filler = jnp.zeros((padded - rows, column_count), jnp.float32)
@@ -80,8 +85,8 @@
     column_count = packed.shape[1]
     row = meta_row(head_dim, column_count)
     gathered = lax.all_gather(packed.astype(jnp.bfloat16), "seq")
-    meta = lax.all_gather(packed[row, :8], "seq")
-    decay, first, last = meta[:, 0], meta[:, 1], meta[:, 2]
+    meta = gathered[:, row, :8].astype(jnp.float32)
+    decay, first, last = meta[:, 0] + meta[:, 3], meta[:, 1], meta[:, 2]
     me = lax.axis_index("seq")
     order = jnp.arange(seq_count)
     previous_last = jnp.concatenate([jnp.zeros((1,), jnp.float32), last[:-1]])

time: 252 us -> 255 us (1.012)
  waiting for transfers between devices: 24.7 us -> 41.9 us
  blocking collectives: 111 us -> 96 us
    all_gather x1, waiting for transfers between devices: 20.8 us -> 38 us  [prefix_from_all(): gathered = lax.all_gather(packed.astype(jnp.bfloat16), 'seq')]
    all_gather x1 -> x0, blocking collectives: 15.3 us -> none  [prefix_from_all(): meta = lax.all_gather(packed[row, :8], 'seq')]
where the time goes in v4:
time: 255 us; the launch traced here: 252 us
  blocking collectives  96 us (38%)
  waiting for transfers between devices  41.9 us (16%)
  other arithmetic  39.1 us (15%)
  between operations  27.1 us (11%)
  matrix products  24.8 us (10%)
  local copies, waits for them, and re-layouts  19.3 us (8%)
  starting transfers between devices  3.8 us (1%)
    all_to_all x1, blocking collectives, on_device(): lax.all_to_all(both_send, 'tensor', split_axis=1, concat_axis=0, tiled=True)  71.1 us
    all_gather x1, waiting for transfers between devices, prefix_from_all(): gathered = lax.all_gather(packed.astype(jnp.bfloat16), 'seq')  38 us
    all_to_all x1, blocking collectives, on_device(): lax.all_to_all(hidden.reshape(token_count, 1, column_count), 'tensor', sp...  24.9 us
    reduce_sum x2, other arithmetic, on_device(): variance = jnp.mean(centered * centered, axis=2, keepdims=True)  15.2 us
    add x3, other arithmetic, span_step(): jnp.sum(weighted, axis=1)  6.94 us
    dot_general x1, matrix products, prefix_from_all(): total = jnp.einsum('s,src->rc', weight, gathered.astype(jnp.float32))  5.4 us
  transfers between devices with their start and end apart: 3, of which 2 were waited for; matrix products, arithmetic and copies ran while one was open for 13% of the time, Pallas kernels for 0%

profile of v4, /device:TPU:23, one launch (start us, length us, event | category | flops | bytes accessed | tf_op | source)
XLA Modules:
  0.0 252.0 jit_solution(15087151382184007879)
XLA Ops:
  6.5 1.1 copy.64
  7.7 1.4 stack_reshape.7
  11.1 71.1 %all_to_all.33 = bf16[64,16,1280]{2,0,1:T(8,128)(2,1)S(1)} all-to-all(bf16[64,16,1280]{2,0,1:T(8,128)(2,1)S(1)} %pad_maximum_fusion), channel_id=1, replica_groups=mesh['seq'=16,'tensor'=16] {'tensor'}, dimensions={1} | all-to-all | bytes 5242880 | tf_op jit(solution)/shard_map/all_to_all | solution.py:134
  82.2 1.6 slice.294
  84.5 3.8 %all-to-all-start = ((bf16[64,16,2]{0,2,1:T(2,128)(2,1)}), bf16[64,16,2]{0,2,1:T(2,128)(2,1)S(1)}, u32[]{:S(2)}, u32[]{:S(2)}) async-start(bf16[64,16,2]{0,2,1:T(2,128)(2,1)} %bitcast.2), calls=%async_computation | async-start | bytes 16384 | tf_op jit(solution)/shard_map/all_to_all | solution.py:135
  91.4 3.9 %all-to-all-done = bf16[64,16,2]{0,2,1:T(2,128)(2,1)S(1)} async-done(((bf16[64,16,2]{0,2,1:T(2,128)(2,1)}), bf16[64,16,2]{0,2,1:T(2,128)(2,1)S(1)}, u32[]{:S(2)}, u32[]{:S(2)}) %all-to-all-start) | async-done | bytes 4128 | tf_op jit(solution)/shard_map/all_to_all | solution.py:135
  98.9 1.3 select_multiply_fusion
  101.0 3.6 %fusion.9 = bf16[1,1024,256]{2,1,0:T(8,128)(2,1)S(1)} fusion(bf16[1024,1024]{1,0:T(8,128)(2,1)S(1)} %get-tuple-element.26, f32[1024]{0:T(1024)S(1)} %select_multiply_fusion, bf16[1024,1280]{1,0:T(8,128)(2,1)S(1)} %bitcast.144), kind=kOutput, calls=%fused_computation.19 | convolution fusion | flops 3223584768 | bytes 3149824 | tf_op jit(solution)/shard_map/dot_general | solution.py:39
  104.6 2.1 concatenate.41
  112.2 1.3 compare_select_fusion.8
  120.4 2.0 broadcast_select_fusion.1
  123.3 4.4 %multiply_add_fusion.5 = (f32[256]{0:T(256)S(1)}, f32[256]{0:T(256)S(1)}, f32[256]{0:T(256)S(1)}, f32[256]{0:T(256)S(1)}, f32[256]{0:T(256)S(1)}) fusion(f32[256]{0:T(256)S(1)} %get-tuple-element.55, f32[256]{0:T(256)S(1)} %bitcast.180, f32[256]{0:T(256)S(1)} %add_bitcast_fusion.4, s32[]{:T(128)} %bitcast.14, s32[1024]{0:T(1024)S(1)} %copy-done.8, ...), kind=kLoop, calls=%fused_computation.150 | loop fusion | flops 4864 | bytes 16412 | tf_op jit(solution)/shard_map/eval_jaxpr/add | solution.py:184
  129.9 1.9 multiply_add_fusion.4
  134.7 1.1 convolution_add_fusion.2
  136.9 1.1 convolution_add_fusion.1
  139.1 1.1 convolution_add_fusion
  141.9 38.0 %all-gather.2.cloned.1.call-done = bf16[16,1032,256]{2,1,0:T(8,128)(2,1)} async-done(((bf16[1,1032,256]{2,1,0:T(8,128)(2,1)}), bf16[16,1032,256]{2,1,0:T(8,128)(2,1)}) %all-gather.2.cloned.1.call-update) | async-done | bytes 8454160 | tf_op jit(solution)/shard_map/all_gather | solution.py:87
  182.6 5.4 %fusion = f32[1,1032,256]{2,0,1:T(1,128)S(1)} fusion(bf16[16,1032,256]{2,1,0:T(8,128)(2,1)} %all-gather.2.cloned.1.call-done, bf16[1]{0:T(256)(128)(2,1)} %constant.195, bf16[15]{0:T(256)(128)(2,1)S(1)} %slice.288, s32[]{:T(128)S(6)} %axis_index.25), kind=kOutput, calls=%fused_computation | convolution fusion | flops 8454240 | bytes 9510948 | tf_op jit(solution)/shard_map/s,src->rc/dot_general | solution.py:98
  190.0 1.7 fusion.103
  191.7 3.1 %fusion.10 = bf16[1024,1,256]{2,0,1:T(8,128)(2,1)S(1)} fusion(f32[1024,256]{1,0:T(8,128)} %bitcast.163, bf16[1024,1024]{1,0:T(8,128)(2,1)S(1)} %copy-done.1, f32[1032,256]{1,0:T(8,128)S(1)} %copy-done.5, f32[1024]{0:T(1024)S(1)} %abs_maximum_fusion, f32[1024]{0:T(1024)S(1)} %bitcast.176), kind=kOutput, calls=%fused_computation.20 | convolution fusion | flops 3222274048 | bytes 4726784 | tf_op jit(solution)/shard_map/dot_general | solution.py:223
  196.5 24.9 %all_to_all.34 = bf16[16,2,8192]{2,1,0:T(2,128)(2,1)S(1)} all-to-all(bf16[16,2,8192]{2,1,0:T(2,128)(2,1)S(1)} %reshape.476), channel_id=1, replica_groups=mesh['seq'=16,'tensor'=16] {'tensor'}, dimensions={0} | all-to-all | bytes 1048576 | tf_op jit(solution)/shard_map/all_to_all | solution.py:226
  223.0 2.4 fusion.90
  225.5 15.2 %multiply_reduce_fusion = f32[64,16]{0,1:T(8,128)S(1)} fusion(f32[64,16]{0,1:T(8,128)S(1)} %bitcast.165, bf16[16,64,1,256]{3,2,1,0:T(2,128)(2,1)S(1)} %bitcast.154), kind=kLoop, calls=%fused_computation.50 | loop fusion | flops 1047552 | bytes 532480 | tf_op jit(solution)/shard_map/reduce_sum | solution.py:236
  243.9 1.2 fusion.31
  (137 shorter events, 30.3 us)
Async XLA Ops:
  6.5 2.6 %copy-start.6 = (bf16[64,4096]{1,0:T(8,128)(2,1)S(1)}, bf16[64,4096]{1,0:T(8,128)(2,1)}, u32[]{:S(2)}) copy-start(bf16[64,4096]{1,0:T(8,128)(2,1)} %param.8) | copy-start | bytes 1572868
  82.2 1.7 copy-start.10
  82.2 1.7 copy-start.11
  82.2 6.1 %copy-start.8 = (s32[1024]{0:T(1024)S(1)}, s32[1024]{0:T(1024)}, u32[]{:S(2)}) copy-start(s32[1024]{0:T(1024)} %param.13) | copy-start | bytes 12292
  83.8 16.3 %collective-permute-start = (bf16[1024,1024]{1,0:T(8,128)(2,1)}, bf16[1024,1024]{1,0:T(8,128)(2,1)}, u32[]{:S(2)}, u32[]{:S(2)}) collective-permute-start(bf16[1024,1024]{1,0:T(8,128)(2,1)} %slice.294), channel_id=1, source_target_pairs={{0,1},{1,0},{2,3},{3,2},{4,5},{5,4},{6,7},{7,6},{8,9},{9,8},{10,11... | collective-permute-start | bytes 6291464 | tf_op jit(solution)/shard_map/ppermute | solution.py:139
  84.5 10.8 %all-to-all-start = ((bf16[64,16,2]{0,2,1:T(2,128)(2,1)}), bf16[64,16,2]{0,2,1:T(2,128)(2,1)S(1)}, u32[]{:S(2)}, u32[]{:S(2)}) async-start(bf16[64,16,2]{0,2,1:T(2,128)(2,1)} %bitcast.2), calls=%async_computation | async-start | bytes 16384 | tf_op jit(solution)/shard_map/all_to_all | solution.py:135
  88.2 91.7 %all-gather.2.cloned.1.call-start = ((), (), s32[]{:S(2)}) async-start(), calls=%async_computation.3 | async-start | bytes 8982528 | tf_op jit(solution)/shard_map/all_gather | solution.py:87
  101.0 3.6 %copy-start.2 = (bf16[1024,1024]{1,0:T(8,128)(2,1)}, bf16[1024,1024]{1,0:T(8,128)(2,1)S(1)}, u32[]{:S(2)}) copy-start(bf16[1024,1024]{1,0:T(8,128)(2,1)S(1)} %get-tuple-element.26) | copy-start | bytes 6291460
  120.4 2.5 copy-start.3
  122.4 17.8 %copy-start = (bf16[1024,1024]{1,0:T(8,128)(2,1)}, bf16[1024,1024]{1,0:T(8,128)(2,1)S(1)}, u32[]{:S(2)}) copy-start(bf16[1024,1024]{1,0:T(8,128)(2,1)S(1)} %broadcast_select_fusion.1) | copy-start | bytes 6291460
  188.0 2.0 copy-start.1
  188.2 1.0 copy-start.4
  189.9 1.8 copy-start.5
  242.9 1.0 copy-start.7
  242.9 1.0 copy-start.9
Sparse Core Ops, SparseCore 0:
  106.8 73.1 all-gather.1

commit v5 on v4

--- a/solution.py
+++ b/solution.py
@@ -130,9 +130,10 @@
     ).reshape(row_count, tensor_size, head_dim)
     value_send = values.reshape(row_count, tensor_size, column_count)
     both_send = jnp.concatenate([pair_send, value_send], axis=2)
-    gate_send = spread_heads(jnp.stack([input_gate, forget_gate], axis=2), 2)
     both_all = lax.all_to_all(both_send, "tensor", split_axis=1, concat_axis=0, tiled=True)
-    gate_all = lax.all_to_all(gate_send, "tensor", split_axis=1, concat_axis=0, tiled=True)
+    gate_every = lax.all_gather(jnp.stack([input_gate, forget_gate], axis=0), "tensor", axis=1, tiled=True)
+    my_head = lax.axis_index("tensor") // group_size
+    gate_all = lax.dynamic_index_in_dim(gate_every, my_head, axis=2, keepdims=False)
     both_all = both_all.reshape(-1, head_dim + column_count)
     own_part = both_all[:, :head_dim]
     value_all = both_all[:, head_dim:]
@@ -143,9 +144,9 @@
     query_all = jnp.where(is_even, own_part, other_part)
     key_all = jnp.where(is_even, other_part, own_part)
     token_count = query_all.shape[0]
-    gate_f = gate_all.reshape(token_count, 2).astype(jnp.float32)
-    gate_in = gate_f[:, 0]
-    log_forget = jax.nn.log_sigmoid(gate_f[:, 1])
+    gate_f = gate_all.astype(jnp.float32)
+    gate_in = gate_f[0]
+    log_forget = jax.nn.log_sigmoid(gate_f[1])
     block_count = token_count // BLOCK
     key_scale = 1.0 / math.sqrt(head_dim)
     first_seg = segment_ids[0]
@@ -212,7 +213,7 @@
         log_forget.reshape(block_count, BLOCK),
         segment_ids.reshape(block_count, BLOCK),
     )
-    unused, outputs = lax.scan(span_step, initial, blocks_in, unroll=True)
+    unused, outputs = lax.scan(span_step, initial, blocks_in)
     numerator = outputs[0].reshape(token_count, column_count)
     q_norm = outputs[1].reshape(token_count)
     entry_factor = outputs[2].reshape(token_count)
@@ -224,13 +225,15 @@
     q_norm = q_norm + scale_rows * jnp.dot(query_full, in_norm, precision=precise)
     hidden = (numerator / jnp.maximum(jnp.abs(q_norm), 1.0)[:, None]).astype(jnp.bfloat16)
     returned = lax.all_to_all(
-        hidden.reshape(token_count, 1, column_count),
+        hidden.reshape(tensor_size, row_count, column_count),
         "tensor",
         split_axis=0,
-        concat_axis=1,
+        concat_axis=0,
         tiled=True,
     )
-    hidden_f = returned.astype(jnp.float32).reshape(row_count, head_count, head_dim)
+    hidden_f = (
+        jnp.transpose(returned, (1, 0, 2)).astype(jnp.float32).reshape(row_count, head_count, head_dim)
+    )
     mean_val = jnp.mean(hidden_f, axis=2, keepdims=True)
     centered = hidden_f - mean_val
     variance = jnp.mean(centered * centered, axis=2, keepdims=True)

time: 255 us -> 249 us (0.976)
  waiting for transfers between devices: 41.9 us -> 10.4 us
  matrix products: 24.8 us -> 41 us
  blocking collectives: 96 us -> 112 us
  other arithmetic: 39.1 us -> 28.3 us
  loops' own time: 0 us -> 10.6 us
  between operations: 27.1 us -> 20.2 us
  starting transfers between devices: 3.8 us -> 0.01 us
    all_gather x1, waiting for transfers between devices: 38 us -> 10.4 us  [prefix_from_all(): gathered = lax.all_gather(packed.astype(jnp.bfloat16), 'seq')]
    all_gather x0 -> x1, blocking collectives: none -> 16.3 us  [on_device(): lax.all_gather(jnp.stack([input_gate, forget_gate], axis=0), 'tensor', ax...]
    reduce_sum x2, other arithmetic: 15.2 us -> 0.42 us  [on_device(): variance = jnp.mean(centered * centered, axis=2, keepdims=True)]
    another operation x0 -> x1, loops' own time: none -> 10.6 us  [on_device(): unused, outputs = lax.scan(span_step, initial, blocks_in)]
    add x3 -> x4, other arithmetic: 6.94 us -> 0.04 us  [span_step(): jnp.sum(weighted, axis=1)]
    dot_general x3 -> x4, matrix products: 3.25 us -> 9.86 us  [span_step(): jnp.dot(scaled_keys.T, value_f, precision=precise)]
    mul x0 -> x4, other arithmetic: none -> 5.02 us  [span_step(): scaled_keys = key_f * tail_weight[:, None]]
    slice x0 -> x1, other arithmetic: none -> 4.69 us  [on_device(): gate_in = gate_f[0]]
  transfers between devices with their start and end apart: 3 -> 2, of which waited for: 2 -> 1; matrix products, arithmetic and copies ran while one was open for 13% -> 26% of each run, Pallas kernels for 0% -> 0%
where the time goes in v5:
time: 249 us; the launch traced here: 244 us
  blocking collectives  112 us (45%)
  matrix products  41 us (16%)
  other arithmetic  28.3 us (11%)
  local copies, waits for them, and re-layouts  21.8 us (9%)
  between operations  20.2 us (8%)
  loops' own time  10.6 us (4%)
  waiting for transfers between devices  10.4 us (4%)
    all_to_all x1, blocking collectives, on_device(): lax.all_to_all(both_send, 'tensor', split_axis=1, concat_axis=0, tiled=True)  71.1 us
    all_to_all x1, blocking collectives, on_device(): lax.all_to_all(hidden.reshape(tensor_size, row_count, column_count), 'ten...  24.9 us
    all_gather x1, blocking collectives, on_device(): lax.all_gather(jnp.stack([input_gate, forget_gate], axis=0), 'tensor', ax...  16.3 us
    another operation x1, loops' own time, on_device(): unused, outputs = lax.scan(span_step, initial, blocks_in)  10.6 us
    all_gather x1, waiting for transfers between devices, prefix_from_all(): gathered = lax.all_gather(packed.astype(jnp.bfloat16), 'seq')  10.4 us
    dot_general x4, matrix products, span_step(): jnp.dot(scaled_keys.T, value_f, precision=precise)  9.86 us
    dot_general x4, matrix products, span_step(): jnp.einsum('id,jd->ij', query_b, key_b, preferred_element_type=jnp.float32)  5.75 us
    dot_general x4, matrix products, span_step(): jnp.dot(query_float, cell_state, precision=precise)  5.75 us
  transfers between devices with their start and end apart: 2, of which 1 were waited for; matrix products, arithmetic and copies ran while one was open for 26% of the time, Pallas kernels for 0%

profile of v5, /device:TPU:23, one launch (start us, length us, event | category | flops | bytes accessed | tf_op | source)
XLA Modules:
  0.0 244.5 jit_solution(8922701927694546952)
XLA Ops:
  8.0 1.4 stack_reshape.7
  11.1 71.1 %all_to_all.20 = bf16[64,16,1280]{2,0,1:T(8,128)(2,1)S(1)} all-to-all(bf16[64,16,1280]{2,0,1:T(8,128)(2,1)S(1)} %pad_maximum_fusion), channel_id=1, replica_groups=mesh['seq'=16,'tensor'=16] {'tensor'}, dimensions={1} | all-to-all | bytes 5242880 | tf_op jit(solution)/shard_map/all_to_all | solution.py:133
  82.2 1.8 slice.114
  87.3 16.3 %all_gather.7 = bf16[2,1024,4]{2,0,1:T(2,128)(2,1)S(1)} all-gather(bf16[2,64,4]{2,0,1:T(2,128)(2,1)S(1)} %copy.30), channel_id=1, replica_groups=mesh['seq'=16,'tensor'=16] {'tensor'}, dimensions={1}, use_global_device_ids=true | all-gather | bytes 17408 | tf_op jit(solution)/shard_map/all_gather | solution.py:134
  104.2 4.7 %slice_reduce_fusion.1 = (f32[1024]{0:T(1024)S(1)}, f32[1024]{0:T(1024)S(1)}) fusion(f32[2,1024,1]{2,0,1:T(2,128)S(1)} %dynamic-slice_convert_fusion), kind=kLoop, calls=%fused_computation.84 | loop fusion | flops 1024 | bytes 16384 | tf_op jit(solution)/shard_map/slice | solution.py:148
  114.8 3.6 %fusion.47 = bf16[1,1024,256]{2,1,0:T(8,128)(2,1)S(1)} fusion(bf16[1024,1024]{1,0:T(8,128)(2,1)S(1)} %get-tuple-element.181, f32[1024]{0:T(1024)S(1)} %select_multiply_fusion, bf16[1024,1280]{1,0:T(8,128)(2,1)S(1)} %bitcast.201), kind=kOutput, calls=%fused_computation.72 | convolution fusion | flops 3223584768 | bytes 3149824 | tf_op jit(solution)/shard_map/dot_general | solution.py:39
  118.4 2.3 concatenate.30
  121.5 1.9 slice.116
  123.4 2.4 broadcast_select_fusion.1
  125.8 59.5 %while.24 = (s32[]{:T(128)}, f32[1024,256]{1,0:T(8,128)S(1)}, f32[1024]{0:T(1024)S(1)}, s32[]{:T(128)}, f32[]{:T(128)}, /*index=5*/f32[4,256,256]{2,1,0:T(8,128)...) while((s32[]{:T(128)}, f32[1024,256]{1,0:T(8,128)S(1)}, ...), condition=%wide.region_5.6_spmd.clone.clone, body=%wide.region_0.5_spmd.clone.sunk.clone | while | flops 1952486144 | bytes 7931753 | solution.py:216
  133.4 1.5 fusion.118
  136.3 1.4 fusion.121
  137.7 2.5 %convolution_add_fusion.3 = f32[1024,256]{1,0:T(8,128)S(1)} fusion(f32[1024,256]{1,0:T(8,128)S(1)} %get-tuple-element.364, f32[256]{0:T(256)S(1)} %fusion.117, f32[]{:T(128)S(6)} %mul.315, pred[]{:T(512)S(6)} %compare.7, bf16[4,256,1024]{2,1,0:T(8,128)(2,1)} %get-tuple-element.388, s32[]{:T(128)S(6)} %copy.64, ...), kind=kOutput, calls=%fused_computation.1.clone.1.clone | convolution fusion | flops 806617088 | bytes 2755584 | tf_op jit(solution)/shard_map/while/body/eval_jaxpr/dot_general | solution.py:195
  151.1 1.4 fusion.121
  152.5 2.4 %convolution_add_fusion.3 = f32[1024,256]{1,0:T(8,128)S(1)} fusion(f32[1024,256]{1,0:T(8,128)S(1)} %get-tuple-element.364, f32[256]{0:T(256)S(1)} %fusion.117, f32[]{:T(128)S(6)} %mul.315, pred[]{:T(512)S(6)} %compare.7, bf16[4,256,1024]{2,1,0:T(8,128)(2,1)} %get-tuple-element.388, s32[]{:T(128)S(6)} %copy.64, ...), kind=kOutput, calls=%fused_computation.1.clone.1.clone | convolution fusion | flops 806617088 | bytes 2755584 | tf_op jit(solution)/shard_map/while/body/eval_jaxpr/dot_general | solution.py:195
  165.9 1.4 fusion.121
  167.4 2.5 %convolution_add_fusion.3 = f32[1024,256]{1,0:T(8,128)S(1)} fusion(f32[1024,256]{1,0:T(8,128)S(1)} %get-tuple-element.364, f32[256]{0:T(256)S(1)} %fusion.117, f32[]{:T(128)S(6)} %mul.315, pred[]{:T(512)S(6)} %compare.7, bf16[4,256,1024]{2,1,0:T(8,128)(2,1)} %get-tuple-element.388, s32[]{:T(128)S(6)} %copy.64, ...), kind=kOutput, calls=%fused_computation.1.clone.1.clone | convolution fusion | flops 806617088 | bytes 2755584 | tf_op jit(solution)/shard_map/while/body/eval_jaxpr/dot_general | solution.py:195
  180.8 1.4 fusion.121
  182.2 2.5 %convolution_add_fusion.3 = f32[1024,256]{1,0:T(8,128)S(1)} fusion(f32[1024,256]{1,0:T(8,128)S(1)} %get-tuple-element.364, f32[256]{0:T(256)S(1)} %fusion.117, f32[]{:T(128)S(6)} %mul.315, pred[]{:T(512)S(6)} %compare.7, bf16[4,256,1024]{2,1,0:T(8,128)(2,1)} %get-tuple-element.388, s32[]{:T(128)S(6)} %copy.64, ...), kind=kOutput, calls=%fused_computation.1.clone.1.clone | convolution fusion | flops 806617088 | bytes 2755584 | tf_op jit(solution)/shard_map/while/body/eval_jaxpr/dot_general | solution.py:195
  185.3 10.4 %all-gather.2.cloned.1.call-done = bf16[16,1032,256]{2,1,0:T(8,128)(2,1)} async-done(((bf16[1,1032,256]{2,1,0:T(8,128)(2,1)}), bf16[16,1032,256]{2,1,0:T(8,128)(2,1)}) %all-gather.2.cloned.1.call-update) | async-done | bytes 8454160 | tf_op jit(solution)/shard_map/all_gather | solution.py:87
  198.3 5.2 %fusion.36 = f32[1,1032,256]{2,0,1:T(1,128)S(1)} fusion(bf16[16,1032,256]{2,1,0:T(8,128)(2,1)} %all-gather.2.cloned.1.call-done, bf16[1]{0:T(256)(128)(2,1)} %constant.220, bf16[15]{0:T(256)(128)(2,1)S(1)} %slice.105, s32[]{:T(128)S(6)} %axis_index.29), kind=kOutput, calls=%fused_computation.52 | convolution fusion | flops 8454240 | bytes 9510948 | tf_op jit(solution)/shard_map/s,src->rc/dot_general | solution.py:98
  205.0 1.7 fusion.77
  206.8 1.9 fusion.45
  208.7 24.9 %all_to_all.21 = bf16[16,64,256]{2,1,0:T(8,128)(2,1)S(1)} all-to-all(bf16[16,64,256]{2,1,0:T(8,128)(2,1)S(1)} %bitcast.214), channel_id=1, replica_groups=mesh['seq'=16,'tensor'=16] {'tensor'}, dimensions={0} | all-to-all | bytes 1048576 | tf_op jit(solution)/shard_map/all_to_all | solution.py:227
  (162 shorter events, 47.1 us)
Async XLA Ops:
  6.5 189.2 %all-gather.2.cloned.1.call-start = ((), (), s32[]{:S(2)}) async-start(), calls=%async_computation.2 | async-start | bytes 8982528 | tf_op jit(solution)/shard_map/all_gather | solution.py:87
  9.4 1.1 copy-start.2
  82.2 32.6 %copy-start = (bf16[64,16,1280]{2,0,1:T(8,128)(2,1)}, bf16[64,16,1280]{2,0,1:T(8,128)(2,1)S(1)}, u32[]{:S(2)}) copy-start(bf16[64,16,1280]{2,0,1:T(8,128)(2,1)S(1)} %all_to_all.20) | copy-start | bytes 7864324
  82.2 1.9 copy-start.4
  82.2 5.0 %copy-start.6 = (bf16[64,4]{0,1:T(4,128)(2,1)S(1)}, bf16[64,4]{0,1:T(4,128)(2,1)}, u32[]{:S(2)}) copy-start(bf16[64,4]{0,1:T(4,128)(2,1)} %param.14) | copy-start | bytes 1540
  82.2 5.0 %copy-start.7 = (bf16[64,4]{0,1:T(4,128)(2,1)S(1)}, bf16[64,4]{0,1:T(4,128)(2,1)}, u32[]{:S(2)}) copy-start(bf16[64,4]{0,1:T(4,128)(2,1)} %param.13) | copy-start | bytes 1540
  84.0 30.0 %collective-permute-start = (bf16[1024,1024]{1,0:T(8,128)(2,1)}, bf16[1024,1024]{1,0:T(8,128)(2,1)}, u32[]{:S(2)}, u32[]{:S(2)}) collective-permute-start(bf16[1024,1024]{1,0:T(8,128)(2,1)} %slice.114), channel_id=1, source_target_pairs={{0,1},{1,0},{2,3},{3,2},{4,5},{5,4},{6,7},{7,6},{8,9},{9,8},{10,11... | collective-permute-start | bytes 6291464 | tf_op jit(solution)/shard_map/ppermute | solution.py:140
  114.8 3.6 %copy-start.1 = (bf16[1024,1024]{1,0:T(8,128)(2,1)}, bf16[1024,1024]{1,0:T(8,128)(2,1)S(1)}, u32[]{:S(2)}) copy-start(bf16[1024,1024]{1,0:T(8,128)(2,1)S(1)} %get-tuple-element.181) | copy-start | bytes 6291460
  205.0 1.8 copy-start.8
  235.4 1.0 copy-start.3
  235.4 1.0 copy-start.5
Sparse Core Ops, SparseCore 0:
  120.9 74.7 all-gather.1

commit v6 on v5

--- a/solution.py
+++ b/solution.py
@@ -9,6 +9,28 @@
 
 
 precise = lax.Precision.HIGHEST
+
+
+def split_dot(wide, narrow, dims):
+    high = lax.reduce_precision(wide, exponent_bits=8, mantissa_bits=7)
+    low = wide - high
+    def one(part):
+        return lax.dot_general(
+            part.astype(jnp.bfloat16), narrow.astype(jnp.bfloat16), dims,
+            preferred_element_type=jnp.float32,
+        )
+    return one(high) + one(low)
+
+
+def split_dot_left(narrow, wide, dims):
+    high = lax.reduce_precision(wide, exponent_bits=8, mantissa_bits=7)
+    low = wide - high
+    def one(part):
+        return lax.dot_general(
+            narrow.astype(jnp.bfloat16), part.astype(jnp.bfloat16), dims,
+            preferred_element_type=jnp.float32,
+        )
+    return one(high) + one(low)
 
 
 def shifted(value, axis, steps):
@@ -36,7 +58,7 @@
         jnp.float32
     )
     scaled_keys = key_all.astype(jnp.float32) * (key_scale * tail_weight)[:, None]
-    state = jnp.dot(scaled_keys.T, value_all.astype(jnp.float32), precision=precise)
+    state = split_dot(scaled_keys, value_all, (((0,), (0,)), ((), ())))
     norm = jnp.sum(scaled_keys, axis=0)
     decay = jnp.exp(total_log) * (last_seg == first_seg).astype(jnp.float32)
     norm_rows = head_dim // column_count
@@ -123,18 +145,30 @@
             queries.reshape(row_count, head_count, head_dim),
             key_rows.reshape(row_count, head_count, head_dim),
         ],
-        axis=2,
+        axis=1,
     )
     pair_send = jnp.broadcast_to(
-        pair_q_k[:, :, None], (row_count, head_count, group_size // 2, 2, head_dim)
-    ).reshape(row_count, tensor_size, head_dim)
-    value_send = values.reshape(row_count, tensor_size, column_count)
-    both_send = jnp.concatenate([pair_send, value_send], axis=2)
-    both_all = lax.all_to_all(both_send, "tensor", split_axis=1, concat_axis=0, tiled=True)
-    gate_every = lax.all_gather(jnp.stack([input_gate, forget_gate], axis=0), "tensor", axis=1, tiled=True)
-    my_head = lax.axis_index("tensor") // group_size
-    gate_all = lax.dynamic_index_in_dim(gate_every, my_head, axis=2, keepdims=False)
-    both_all = both_all.reshape(-1, head_dim + column_count)
+        jnp.transpose(pair_q_k, (2, 1, 0, 3))[:, None],
+        (head_count, group_size // 2, 2, row_count, head_dim),
+    ).reshape(tensor_size, row_count, head_dim)
+    value_send = jnp.transpose(values.reshape(row_count, tensor_size, column_count), (1, 0, 2))
+    body_width = row_count * (head_dim + column_count)
+    gate_pair = jnp.stack([input_gate, forget_gate], axis=0)
+    gate_send = jnp.broadcast_to(
+        jnp.transpose(gate_pair, (2, 0, 1))[:, None], (head_count, group_size, 2, row_count)
+    ).reshape(tensor_size, 2 * row_count)
+    both_send = jnp.concatenate(
+        [
+            jnp.concatenate([pair_send, value_send], axis=2).reshape(tensor_size, body_width),
+            gate_send,
+        ],
+        axis=1,
+    )
+    both_all = lax.all_to_all(both_send, "tensor", split_axis=0, concat_axis=0, tiled=True)
+    gate_all = jnp.transpose(
+        both_all[:, body_width:].reshape(tensor_size, 2, row_count), (1, 0, 2)
+    ).reshape(2, tensor_size * row_count)
+    both_all = both_all[:, :body_width].reshape(tensor_size * row_count, head_dim + column_count)
     own_part = both_all[:, :head_dim]
     value_all = both_all[:, head_dim:]
     other_part = lax.ppermute(
@@ -177,14 +211,14 @@
         query_float = query_b.astype(jnp.float32)
         key_f = key_b.astype(jnp.float32) * key_scale
         value_f = value_b.astype(jnp.float32)
-        numerator = jnp.dot(weighted, value_f, precision=precise)
+        numerator = split_dot(weighted, value_b, (((1,), (0,)), ((), ())))
         carried = jnp.exp(cumulative) * (seg_b == prev_seg).astype(jnp.float32)
-        numerator = numerator + carried[:, None] * jnp.dot(
-            query_float, cell_state, precision=precise
-        )
-        q_norm = jnp.sum(weighted, axis=1) + carried * jnp.dot(
-            query_float, norm_vec, precision=precise
-        )
+        numerator = numerator + carried[:, None] * split_dot_left(
+            query_b, cell_state, (((1,), (0,)), ((), ()))
+        )
+        q_norm = jnp.sum(weighted, axis=1) + carried * split_dot_left(
+            query_b, norm_vec[:, None], (((1,), (0,)), ((), ()))
+        )[:, 0]
         entry_factor = jnp.exp(total_log + cumulative) * (seg_b == first_seg).astype(jnp.float32)
         last_seg = seg_b[BLOCK - 1]
         tail_weight = jnp.exp(cumulative[BLOCK - 1] - cumulative + gate_b) * (
@@ -192,7 +226,9 @@
         ).astype(jnp.float32)
         keep_factor = jnp.exp(cumulative[BLOCK - 1]) * (last_seg == prev_seg).astype(jnp.float32)
         scaled_keys = key_f * tail_weight[:, None]
-        cell_state = keep_factor * cell_state + jnp.dot(scaled_keys.T, value_f, precision=precise)
+        cell_state = keep_factor * cell_state + split_dot(
+            scaled_keys, value_b, (((0,), (0,)), ((), ()))
+        )
         norm_vec = keep_factor * norm_vec + jnp.sum(scaled_keys, axis=0)
         return (
             (cell_state, norm_vec, last_seg, total_log + cumulative[BLOCK - 1]),
@@ -220,9 +256,12 @@
 
     linked = (in_last == (first_seg + 1).astype(jnp.float32)).astype(jnp.float32)
     scale_rows = entry_factor * linked
-    query_full = query_all.astype(jnp.float32)
-    numerator = numerator + scale_rows[:, None] * jnp.dot(query_full, in_state, precision=precise)
-    q_norm = q_norm + scale_rows * jnp.dot(query_full, in_norm, precision=precise)
+    numerator = numerator + scale_rows[:, None] * split_dot_left(
+        query_all, in_state, (((1,), (0,)), ((), ()))
+    )
+    q_norm = q_norm + scale_rows * split_dot_left(
+        query_all, in_norm[:, None], (((1,), (0,)), ((), ()))
+    )[:, 0]
     hidden = (numerator / jnp.maximum(jnp.abs(q_norm), 1.0)[:, None]).astype(jnp.bfloat16)
     returned = lax.all_to_all(
         hidden.reshape(tensor_size, row_count, column_count),

time: 249 us -> 266 us (1.068)
  local copies, waits for them, and re-layouts: 21.8 us -> 53.5 us
  blocking collectives: 112 us -> 96.7 us
  matrix products: 41 us -> 37.5 us
    unnamed x25 -> x33, local copies, waits for them, and re-layouts: 1.56 us -> 25.1 us
    all_gather x1 -> x0, blocking collectives: 16.3 us -> none  [on_device(): lax.all_gather(jnp.stack([input_gate, forget_gate], axis=0), 'tensor', ax...]
    slice x1, other arithmetic: 4.69 us -> 0.05 us  [on_device(): gate_in = gate_f[0]]
    dot_general x19 -> x38, matrix products: 30.1 us -> 26.6 us  [the longest x18 18.1 us: one(): lax.dot_general(part.astype(jnp.bfloat16), narrow.astype(jnp.bfloat16), d...]
    all_to_all x0 -> x2, other arithmetic: none -> 3.49 us  [on_device(): lax.all_to_all(both_send, 'tensor', split_axis=0, concat_axis=0, tiled=True)]
  transfers between devices with their start and end apart: 2 -> 2, of which waited for: 1 -> 1; matrix products, arithmetic and copies ran while one was open for 26% -> 20% of each run, Pallas kernels for 0% -> 0%
where the time goes in v6:
time: 266 us; the launch traced here: 261 us
  blocking collectives  96.7 us (36%)
  local copies, waits for them, and re-layouts  53.5 us (20%)
  matrix products  37.5 us (14%)
  other arithmetic  29.9 us (11%)
  between operations  20.2 us (8%)
  waiting for transfers between devices  12.3 us (5%)
  loops' own time  10.8 us (4%)
    all_to_all x1, blocking collectives, on_device(): lax.all_to_all(both_send, 'tensor', split_axis=0, concat_axis=0, tiled=True)  71.8 us
    unnamed x33, local copies, waits for them, and re-layouts  25.1 us
    all_to_all x1, blocking collectives, on_device(): lax.all_to_all(hidden.reshape(tensor_size, row_count, column_count), 'ten...  24.9 us
    dot_general x18, matrix products, one(): lax.dot_general(part.astype(jnp.bfloat16), narrow.astype(jnp.bfloat16), d...  18.1 us
    all_gather x1, waiting for transfers between devices, prefix_from_all(): gathered = lax.all_gather(packed.astype(jnp.bfloat16), 'seq')  12.3 us
    another operation x1, loops' own time, on_device(): unused, outputs = lax.scan(span_step, initial, blocks_in)  10.8 us
    dot_general x20, matrix products, one(): lax.dot_general(narrow.astype(jnp.bfloat16), part.astype(jnp.bfloat16), d...  8.46 us
    dot_general x4, matrix products, span_step(): jnp.einsum('id,jd->ij', query_b, key_b, preferred_element_type=jnp.float32)  5.81 us
  transfers between devices with their start and end apart: 2, of which 1 were waited for; matrix products, arithmetic and copies ran while one was open for 20% of the time, Pallas kernels for 0%

profile of v6, /device:TPU:23, one launch (start us, length us, event | category | flops | bytes accessed | tf_op | source)
XLA Modules:
  0.0 261.4 jit_solution(13585204268864116252)
XLA Ops:
  8.8 1.4 stack_reshape.7
  11.9 1.4 copy.46
  14.0 3.3 %reduce.22 = bf16[16,82048]{1,0:T(8,128)(2,1)} reduce(bf16[16,1,82048]{2,0,1:T(8,128)(2,1)S(1)} %maximum_bitcast_fusion, bf16[]{:T(256)} %broadcast.322), dimensions={1}, to_apply=%copy.34.reduce_sub_computation | reduce | bytes 5251074 | tf_op jit(solution)/shard_map/all_to_all | solution.py:167
  17.4 3.0 %reshape.428 = bf16[16,2,41024]{2,1,0:T(2,128)(2,1)S(1)} reshape(bf16[16,82048]{1,0:T(8,128)(2,1)} %reduce.22) | data formatting | bytes 5251072
  20.4 71.8 %all_to_all.17 = bf16[16,2,41024]{2,1,0:T(2,128)(2,1)} all-to-all(bf16[16,2,41024]{2,1,0:T(2,128)(2,1)S(1)} %reshape.428), channel_id=1, replica_groups=mesh['seq'=16,'tensor'=16] {'tensor'}, dimensions={0} | all-to-all | bytes 5251072 | tf_op jit(solution)/shard_map/all_to_all | solution.py:167
  92.2 14.0 %reshape.429 = bf16[16,1,82048]{2,1,0:T(2,128)(2,1)} reshape(bf16[16,2,41024]{2,1,0:T(2,128)(2,1)} %all_to_all.17) | data formatting | bytes 5251072
  106.2 2.8 %copy.57 = bf16[16,1,82048]{2,0,1:T(8,128)(2,1)S(1)} copy(bf16[16,1,82048]{2,1,0:T(2,128)(2,1)} %reshape.429) | data formatting | bytes 5251072
  109.0 1.5 copy-done.4
  110.5 1.7 slice.123
  112.2 2.5 reshape.383
  114.7 1.8 slice.124
  121.1 1.9 slice.126
  129.3 2.4 fusion.69
  131.7 2.4 fusion.70
  134.1 2.8 %fusion.83 = bf16[1,1024,256]{2,1,0:T(8,128)(2,1)} fusion(f32[1024,256]{1,0:T(8,128)S(1)} %fusion.70, bf16[1024,1024]{1,0:T(8,128)(2,1)S(1)} %get-tuple-element.179, f32[1024]{0:T(1024)S(1)} %select_multiply_fusion, bf16[1024,1280]{1,0:T(8,128)(2,1)} %copy-done.2), kind=kOutput, calls=%fused_computation.119 | convolution fusion | flops 541589504 | bytes 4198400 | tf_op jit(solution)/shard_map/dot_general | solution.py:18
  137.0 3.8 %concatenate.34 = bf16[1,1032,256]{2,1,0:T(8,128)(2,1)} concatenate(bf16[1,1024,256]{2,1,0:T(8,128)(2,1)} %fusion.83, bf16[1,4,256]{2,1,0:T(4,128)(2,1)S(1)} %concatenate.32, bf16[1,1,256]{2,1,0:T(2,128)(2,1)S(1)} %fusion.98, bf16[1,3,256]{2,1,0:T(4,128)(2,1)S(1)} %broadcast_in_dim.95), dimensions={1} | concatenate | bytes 1056768 | tf_op jit(solution)/shard_map/concatenate | solution.py:83
  140.8 2.4 broadcast_select_fusion
  143.2 56.2 %while.24 = (s32[]{:T(128)}, f32[1024,256]{1,0:T(8,128)S(1)}, f32[1024]{0:T(1024)S(1)}, s32[]{:T(128)}, f32[]{:T(128)}, /*index=5*/f32[4,256,256]{2,1,0:T(8,128)...) while((s32[]{:T(128)}, f32[1024,256]{1,0:T(8,128)S(1)}, ...), condition=%wide.region_5.6_spmd.clone.clone, body=%wide.region_0.5_spmd.clone.sunk.clone | while | flops 746563328 | bytes 24730040 | solution.py:252
  150.9 1.5 fusion.195
  193.0 1.4 fusion.195
  199.4 12.3 %all-gather.2.cloned.1.call-done = bf16[16,1032,256]{2,1,0:T(8,128)(2,1)} async-done(((bf16[1,1032,256]{2,1,0:T(8,128)(2,1)}), bf16[16,1032,256]{2,1,0:T(8,128)(2,1)}) %all-gather.2.cloned.1.call-update) | async-done | bytes 8454160 | tf_op jit(solution)/shard_map/all_gather | solution.py:109
  214.3 5.2 %fusion.66 = f32[1,1032,256]{2,0,1:T(1,128)S(1)} fusion(bf16[16,1032,256]{2,1,0:T(8,128)(2,1)} %all-gather.2.cloned.1.call-done, bf16[1]{0:T(256)(128)(2,1)} %constant.236, bf16[15]{0:T(256)(128)(2,1)S(1)} %slice.113, s32[]{:T(128)S(6)} %axis_index.25), kind=kOutput, calls=%fused_computation.88 | convolution fusion | flops 8454240 | bytes 9510948 | tf_op jit(solution)/shard_map/s,src->rc/dot_general | solution.py:120
  220.4 1.8 fusion.92
  225.5 24.9 %all_to_all.18 = bf16[16,64,256]{2,1,0:T(8,128)(2,1)S(1)} all-to-all(bf16[16,64,256]{2,1,0:T(8,128)(2,1)S(1)} %bitcast.245), channel_id=1, replica_groups=mesh['seq'=16,'tensor'=16] {'tensor'}, dimensions={0} | all-to-all | bytes 1048576 | tf_op jit(solution)/shard_map/all_to_all | solution.py:266
  (233 shorter events, 62.3 us)
Async XLA Ops:
  6.5 205.2 %all-gather.2.cloned.1.call-start = ((), (), s32[]{:S(2)}) async-start(), calls=%async_computation.2 | async-start | bytes 8982528 | tf_op jit(solution)/shard_map/all_gather | solution.py:109
  10.2 1.1 copy-start.7
  109.0 1.5 copy-start.4
  114.7 2.1 copy-start.2
  114.7 2.6 copy-start.9
  116.8 12.4 %collective-permute-start = (bf16[1024,1024]{1,0:T(8,128)(2,1)}, bf16[1024,1024]{1,0:T(8,128)(2,1)}, u32[]{:S(2)}, u32[]{:S(2)}) collective-permute-start(bf16[1024,1024]{1,0:T(8,128)(2,1)} %slice.124), channel_id=1, source_target_pairs={{0,1},{1,0},{2,3},{3,2},{4,5},{5,4},{6,7},{7,6},{8,9},{9,8},{10,11... | collective-permute-start | bytes 6291464 | tf_op jit(solution)/shard_map/ppermute | solution.py:174
  131.6 2.5 copy-start
  153.6 1.1 copy-start.3
  154.0 1.7 copy-start.1
  167.6 1.0 copy-start.3
  168.0 1.6 copy-start.1
  181.6 1.1 copy-start.3
  182.0 1.7 copy-start.1
  195.7 1.1 copy-start.3
  196.0 1.7 copy-start.1
  219.7 2.4 copy-start.5
  222.9 1.4 copy-start.6
  222.9 1.5 copy-start.11
  222.9 1.8 copy-start.12
  252.3 1.0 copy-start.8
  252.3 1.0 copy-start.10
Sparse Core Ops, SparseCore 0:
  140.9 70.7 all-gather.1

commit v7 on v2

v7 whole, which is shorter than its diff:
```python
import math

import jax
import jax.numpy as jnp
import numpy as np
from jax import lax
from jax.sharding import Mesh
from jax.sharding import PartitionSpec as P


def split_dot(wide, narrow, dims):
    high = lax.reduce_precision(wide, exponent_bits=8, mantissa_bits=7)
    low = wide - high

    def one(part):
        return lax.dot_general(
            part.astype(jnp.bfloat16),
            narrow.astype(jnp.bfloat16),
            dims,
            preferred_element_type=jnp.float32,
        )

    return one(high) + one(low)


def split_dot_left(narrow, wide, dims):
    high = lax.reduce_precision(wide, exponent_bits=8, mantissa_bits=7)
    low = wide - high

    def one(part):
        return lax.dot_general(
            narrow.astype(jnp.bfloat16),
            part.astype(jnp.bfloat16),
            dims,
            preferred_element_type=jnp.float32,
        )

    return one(high) + one(low)


def meta_row(head_dim, column_count):
    return head_dim + head_dim // column_count


def with_meta(body, row, decay, first, last, low=None):
    lane = jnp.arange(body.shape[1])[None, :]
    rows = jnp.arange(body.shape[0])[:, None]
    values = jnp.where(lane == 0, decay, jnp.where(lane == 1, first, last))
    if low is not None:
        values = jnp.where(lane == 3, low, values)
    return jnp.where((rows == row) & (lane < (3 if low is None else 4)), values, body)


def pack_summary(key_all, value_all, gate_in, cumulative, segment_ids, key_scale):
    head_dim = key_all.shape[1]
    column_count = value_all.shape[1]
    total_log = cumulative[-1]
    first_seg = segment_ids[0]
    last_seg = segment_ids[-1]
    tail_weight = jnp.exp(total_log - cumulative + gate_in) * (segment_ids == last_seg).astype(
        jnp.float32
    )
    scaled_keys = key_all.astype(jnp.float32) * (key_scale * tail_weight)[:, None]
    state = split_dot(scaled_keys, value_all, (((0,), (0,)), ((), ())))
    norm = jnp.sum(scaled_keys, axis=0)
    decay = jnp.exp(total_log) * (last_seg == first_seg).astype(jnp.float32)
    norm_rows = head_dim // column_count
    rows = meta_row(head_dim, column_count) + 1
    padded = -(-rows // 8) * 8
    filler = jnp.zeros((padded - rows + 1, column_count), jnp.float32)
    body = jnp.concatenate([state, norm.reshape(norm_rows, column_count), filler], axis=0)
    decay_high = lax.reduce_precision(decay, exponent_bits=8, mantissa_bits=7)
    return with_meta(
        body,
        meta_row(head_dim, column_count),
        decay_high,
        (first_seg + 1).astype(jnp.float32),
        (last_seg + 1).astype(jnp.float32),
        decay - decay_high,
    )


def prefix_weights(decay, first, last, mine):
    count = decay.shape[0]
    order = jnp.arange(count)
    previous_last = jnp.concatenate([jnp.zeros((1,), jnp.float32), last[:-1]])
    carry = decay * (previous_last == first).astype(jnp.float32)
    carry = jnp.where((order < mine) & (order >= 1), carry, 1.0)
    after = jnp.cumprod(carry[::-1])[::-1]
    weight = jnp.concatenate([after[1:], jnp.ones((1,), jnp.float32)])
    weight = jnp.where(order < mine, weight, 0.0)
    combined_decay = decay[0] * after[1] if count > 1 else decay[0]
    combined_last = jnp.where(mine > 0, last[jnp.maximum(mine - 1, 0)], 0.0)
    combined_first = jnp.where(mine > 0, first[0], 0.0)
    return weight, combined_decay, combined_first, combined_last


def prefix_2d(packed, head_dim, row_axis, col_axis):
    column_count = packed.shape[1]
    row = meta_row(head_dim, column_count)
    row_size = lax.axis_size(row_axis)
    me_y = lax.axis_index(row_axis)
    me_x = lax.axis_index(col_axis)

    along_row = lax.all_gather(packed.astype(jnp.bfloat16), row_axis).astype(jnp.float32)
    meta = along_row[:, row, :4]
    decay, first, last = meta[:, 0] + meta[:, 3], meta[:, 1], meta[:, 2]
    w_row, decay_r, first_r, last_r = prefix_weights(decay, first, last, me_y)
    w_all, decay_t, first_t, last_t = prefix_weights(decay, first, last, row_size)
    row_part = jnp.einsum("s,src->rc", w_row, along_row)
    row_total = with_meta(
        jnp.einsum("s,src->rc", w_all, along_row), row, decay_t, first_t, last_t
    )

    along_col = lax.all_gather(row_total, col_axis)
    meta_c = along_col[:, row, :3]
    w_col, unused_decay, unused_first, last_p = prefix_weights(
        meta_c[:, 0], meta_c[:, 1], meta_c[:, 2], me_x
    )
    col_part = jnp.einsum("s,src->rc", w_col, along_col)

    has_row = me_y > 0
    factor = jnp.where(has_row, decay_r * (last_p == first_r).astype(jnp.float32), 1.0)
    state = factor * col_part + row_part
    in_last = jnp.where(has_row, last_r, last_p)
    return state, in_last


def on_device(
    queries, key_rows, values, input_gate, forget_gate, segment_ids, output_gate, norm_gain
):
    tensor_size = lax.axis_size("tensor")
    row_count, inner = queries.shape
    head_count = input_gate.shape[1]
    head_dim = inner // head_count
    group_size = tensor_size // head_count
    column_count = head_dim // group_size

    def spread_heads(array, width):
        shaped = array.reshape(row_count, head_count, 1, width)
        return jnp.broadcast_to(shaped, (row_count, head_count, group_size, width)).reshape(
            row_count, tensor_size, width
        )

    pair_q_k = jnp.stack(
        [
            queries.reshape(row_count, head_count, head_dim),
            key_rows.reshape(row_count, head_count, head_dim),
        ],
        axis=2,
    )
    pair_send = jnp.broadcast_to(
        pair_q_k[:, :, None], (row_count, head_count, group_size // 2, 2, head_dim)
    ).reshape(row_count, tensor_size, head_dim)
    value_send = values.reshape(row_count, tensor_size, column_count)
    both_send = jnp.concatenate([pair_send, value_send], axis=2)
    gate_send = spread_heads(jnp.stack([input_gate, forget_gate], axis=2), 2)
    both_all = lax.all_to_all(both_send, "tensor", split_axis=1, concat_axis=0, tiled=True)
    gate_all = lax.all_to_all(gate_send, "tensor", split_axis=1, concat_axis=0, tiled=True)
    both_all = both_all.reshape(-1, head_dim + column_count)
    own_part = both_all[:, :head_dim]
    value_all = both_all[:, head_dim:]
    other_part = lax.ppermute(
        own_part, "tensor", [(index, index ^ 1) for index in range(tensor_size)]
    )
    is_even = lax.axis_index("tensor") % 2 == 0
    query_all = jnp.where(is_even, own_part, other_part)
    key_all = jnp.where(is_even, other_part, own_part)
    token_count = query_all.shape[0]
    gate_f = gate_all.reshape(token_count, 2).astype(jnp.float32)
    gate_in = gate_f[:, 0]
    log_forget = jax.nn.log_sigmoid(gate_f[:, 1])
    key_scale = 1.0 / math.sqrt(head_dim)
    first_seg = segment_ids[0]
    cumulative = jnp.cumsum(log_forget)

    packed = pack_summary(key_all, value_all, gate_in, cumulative, segment_ids, key_scale)
    in_packed, in_last = prefix_2d(packed, head_dim, "sy", "sx")
    in_row = meta_row(head_dim, column_count)
    in_state = in_packed[:head_dim]
    in_norm = in_packed[head_dim:in_row].reshape(head_dim)

    token_ids = jnp.arange(token_count, dtype=jnp.int32)
    allowed = (token_ids[:, None] >= token_ids[None, :]) & (
        segment_ids[:, None] == segment_ids[None, :]
    )
    exponent = cumulative[:, None] - cumulative[None, :] + gate_in[None, :]
    weights = jnp.where(allowed, jnp.exp(jnp.where(allowed, exponent, 0.0)), 0.0)
    scores = (
        lax.dot_general(
            query_all, key_all, (((1,), (1,)), ((), ())), preferred_element_type=jnp.float32
        )
        * key_scale
    )
    weighted = weights * scores
    numerator = split_dot(weighted, value_all, (((1,), (0,)), ((), ())))
    q_norm = jnp.sum(weighted, axis=1)
    entry_factor = jnp.exp(cumulative) * (segment_ids == first_seg).astype(jnp.float32)

    linked = (in_last == (first_seg + 1).astype(jnp.float32)).astype(jnp.float32)
    scale_rows = entry_factor * linked
    numerator = numerator + scale_rows[:, None] * split_dot_left(
        query_all, in_state, (((1,), (0,)), ((), ()))
    )
    q_norm = q_norm + scale_rows * split_dot_left(
        query_all, in_norm[:, None], (((1,), (0,)), ((), ()))
    )[:, 0]
    hidden = (numerator / jnp.maximum(jnp.abs(q_norm), 1.0)[:, None]).astype(jnp.bfloat16)
    returned = lax.all_to_all(
        hidden.reshape(tensor_size, row_count, column_count),
        "tensor",
        split_axis=0,
        concat_axis=0,
        tiled=True,
    )
    hidden_f = (
        jnp.transpose(returned, (1, 0, 2)).astype(jnp.float32).reshape(row_count, head_count, head_dim)
    )
    mean_val = jnp.mean(hidden_f, axis=2, keepdims=True)
    centered = hidden_f - mean_val
    variance = jnp.mean(centered * centered, axis=2, keepdims=True)
    normed = (centered * lax.rsqrt(variance + 1e-05)).reshape(row_count, inner)
    return (normed * norm_gain * jax.nn.silu(output_gate.astype(jnp.float32))).astype(jnp.bfloat16)


def split_seq_mesh(mesh):
    devices = np.asarray(mesh.devices)
    seq_size, tensor_size = devices.shape
    row_size = len({int(d.coords[1]) for d in devices[:, 0]})
    return Mesh(
        devices.reshape(seq_size // row_size, row_size, tensor_size), ("sx", "sy", "tensor")
    )


def solution(mesh):
    split = split_seq_mesh(mesh)
    tokens = P(("sx", "sy", "tensor"), None)
    in_specs = (tokens, tokens, tokens, tokens, tokens, P(("sx", "sy")), tokens, P())
    return jax.shard_map(
        on_device, mesh=split, in_specs=in_specs, out_specs=tokens, check_vma=False
    )
```

time: 292 us -> 254 us (0.87)
  blocking collectives: 25.2 us -> 95.9 us
  other arithmetic: 50.9 us -> 15.1 us
  between operations: 45.2 us -> 22.6 us
  starting transfers between devices: 26 us -> 4.02 us
  waiting for transfers between devices: 81.6 us -> 69.6 us
  local copies, waits for them, and re-layouts: 28.7 us -> 17.6 us
  matrix products: 29.8 us -> 25.3 us
    all_to_all x1 -> x2, blocking collectives: 25.2 us -> 95.9 us  [the longest x1 71.1 us: on_device(): lax.all_to_all(both_send, 'tensor', split_axis=1, concat_axis=0, tiled=True)]
    all_gather x0 -> x2, waiting for transfers between devices: none -> 65.7 us  [the longest x1 35.1 us: prefix_2d(): along_col = lax.all_gather(row_total, col_axis)]
    all_to_all x1 -> x0, waiting for transfers between devices: 51.5 us -> none  [on_device(): lax.all_to_all(both_send, 'tensor', split_axis=1, concat_axis=0, tiled=True)]
    ppermute x5 -> x0, waiting for transfers between devices: 29.1 us -> none  [shifted(): lax.ppermute(value, axis, [(source, source + steps) for source in range(i...]
    reduce_sum x2, other arithmetic: 15.2 us -> 0.42 us  [on_device(): variance = jnp.mean(centered * centered, axis=2, keepdims=True)]
    convert_element_type x6 -> x2, other arithmetic: 11.5 us -> 1.04 us  [the longest x1 1.04 us: prefix_2d(): packed.astype(jnp.bfloat16)]
    ppermute x5 -> x0, starting transfers between devices: 9.37 us -> none  [shifted(): lax.ppermute(value, axis, [(source, source + steps) for source in range(i...]
    all_to_all x1 -> x0, starting transfers between devices: 6.41 us -> none  [on_device(): lax.all_to_all(both_send, 'tensor', split_axis=1, concat_axis=0, tiled=True)]
  transfers between devices with their start and end apart: 8 -> 4, of which waited for: 6 -> 3; matrix products, arithmetic and copies ran while one was open for 18% -> 7% of each run, Pallas kernels for 0% -> 0%
where the time goes in v7:
time: 254 us; the launch traced here: 250 us
  blocking collectives  95.9 us (38%)
  waiting for transfers between devices  69.6 us (27%)
  matrix products  25.3 us (10%)
  between operations  22.6 us (9%)
  local copies, waits for them, and re-layouts  17.6 us (7%)
  other arithmetic  15.1 us (6%)
  starting transfers between devices  4.02 us (2%)
    all_to_all x1, blocking collectives, on_device(): lax.all_to_all(both_send, 'tensor', split_axis=1, concat_axis=0, tiled=True)  71.1 us
    all_gather x1, waiting for transfers between devices, prefix_2d(): along_col = lax.all_gather(row_total, col_axis)  35.1 us
    all_gather x1, waiting for transfers between devices, prefix_2d(): lax.all_gather(packed.astype(jnp.bfloat16), row_axis).astype(jnp.float32)  30.6 us
    all_to_all x1, blocking collectives, on_device(): lax.all_to_all(hidden.reshape(tensor_size, row_count, column_count), 'ten...  24.9 us
    dot_general x4, matrix products, one(): lax.dot_general(part.astype(jnp.bfloat16), narrow.astype(jnp.bfloat16), d...  5.31 us
    dot_general x4, matrix products, one(): lax.dot_general(narrow.astype(jnp.bfloat16), part.astype(jnp.bfloat16), d...  5.27 us
  transfers between devices with their start and end apart: 4, of which 3 were waited for; matrix products, arithmetic and copies ran while one was open for 7% of the time, Pallas kernels for 0%

profile of v7, /device:TPU:23, one launch (start us, length us, event | category | flops | bytes accessed | tf_op | source)
XLA Modules:
  0.0 250.1 jit_solution(3867928449295998567)
XLA Ops:
  6.5 1.1 copy.67
  7.7 1.4 stack_reshape.7
  11.1 71.1 %all_to_all.29 = bf16[64,16,1280]{2,0,1:T(8,128)(2,1)S(1)} all-to-all(bf16[64,16,1280]{2,0,1:T(8,128)(2,1)S(1)} %pad_maximum_fusion), channel_id=1, replica_groups=mesh['sx'=4,'sy'=4,'tensor'=16] {'tensor'}, dimensions={1} | all-to-all | bytes 5242880 | tf_op jit(solution)/shard_map/all_to_all | solution.py:158
  82.2 1.6 slice.168
  84.5 3.8 %all-to-all-start = ((bf16[64,16,2]{0,2,1:T(2,128)(2,1)}), bf16[64,16,2]{0,2,1:T(2,128)(2,1)S(1)}, u32[]{:S(2)}, u32[]{:S(2)}) async-start(bf16[64,16,2]{0,2,1:T(2,128)(2,1)} %bitcast.2), calls=%async_computation | async-start | bytes 16384 | tf_op jit(solution)/shard_map/all_to_all | solution.py:159
  91.4 3.8 %all-to-all-done = bf16[64,16,2]{0,2,1:T(2,128)(2,1)S(1)} async-done(((bf16[64,16,2]{0,2,1:T(2,128)(2,1)}), bf16[64,16,2]{0,2,1:T(2,128)(2,1)S(1)}, u32[]{:S(2)}, u32[]{:S(2)}) %all-to-all-start) | async-done | bytes 4128 | tf_op jit(solution)/shard_map/all_to_all | solution.py:159
  98.9 1.3 select_multiply_fusion
  102.3 1.8 fusion.20
  104.1 1.9 concatenate.36
  107.4 30.6 %all-gather.4.cloned.1.call-done = bf16[4,1032,256]{2,1,0:T(8,128)(2,1)} async-done(((bf16[1,1032,256]{2,1,0:T(8,128)(2,1)}), bf16[4,1032,256]{2,1,0:T(8,128)(2,1)}) %all-gather.4.cloned.1.call-update) | async-done | bytes 2113552 | tf_op jit(solution)/shard_map/all_gather | solution.py:105
  142.5 1.3 select_select_fusion
  143.8 2.9 %fusion.16 = f32[1,1032,256]{2,0,1:T(1,128)S(1)} fusion(bf16[4,1032,256]{2,1,0:T(8,128)(2,1)} %all-gather.4.cloned.1.call-done, bf16[1]{0:T(256)(128)(2,1)} %constant.195, bf16[3]{0:T(256)(128)(2,1)S(1)} %slice.149), kind=kOutput, calls=%fused_computation.24 | convolution fusion | flops 2113560 | bytes 3170312 | tf_op jit(solution)/shard_map/s,src->rc/dot_general | solution.py:112
  146.7 1.2 bitcast_select_fusion
  148.0 2.0 broadcast_select_fusion.1
  150.2 2.9 %fusion.69 = (f32[1024]{0:T(1024)S(1)}, f32[1024,1024]{0,1:T(8,128)S(1)}) fusion(bf16[1024,1024]{1,0:T(8,128)(2,1)S(1)} %broadcast_select_fusion.1, bf16[1024,1024]{1,0:T(8,128)(2,1)S(1)} %copy-done.3, f32[1024]{0:T(1024)S(1)} %bitcast.123, f32[1024]{0:T(1024)S(1)} %add_bitcast_fusion, s32[1024]{0:T(1024)S(1)} %copy-done.6), kind=kOutput, calls=%fused_computation.133 | convolution fusion | flops 2157968384 | bytes 8404992 | tf_op jit(solution)/shard_map/dot_general | solution.py:190
  153.9 1.8 fusion.18
  159.7 4.0 %fusion.14 = f32[1,1032,256]{2,0,1:T(1,128)} fusion(bf16[4,1032,256]{2,1,0:T(8,128)(2,1)} %all-gather.4.cloned.1.call-done, bf16[1]{0:T(256)(128)(2,1)} %constant.195, bf16[3]{0:T(256)(128)(2,1)S(1)} %slice.162, s32[]{:T(128)S(6)} %axis_index.35), kind=kOutput, calls=%fused_computation.22 | convolution fusion | flops 2113560 | bytes 3170316 | tf_op jit(solution)/shard_map/s,src->rc/dot_general | solution.py:110
  163.7 35.1 %all-gather.6.cloned.1.call-done = f32[4128,256]{1,0:T(8,128)} async-done(((f32[1032,256]{1,0:T(8,128)}), f32[4128,256]{1,0:T(8,128)}) %all-gather.6.cloned.1.call-update) | async-done | bytes 4227088 | tf_op jit(solution)/shard_map/all_gather | solution.py:115
  200.4 5.0 %fusion = f32[1,1032,256]{2,0,1:T(1,128)} fusion(f32[4,1032,256]{2,1,0:T(8,128)} %bitcast.131, bf16[1]{0:T(256)(128)(2,1)} %constant.195, bf16[3]{0:T(256)(128)(2,1)S(1)} %slice.159, s32[]{:T(128)S(6)} %axis_index.38), kind=kOutput, calls=%fused_computation.4 | convolution fusion | flops 2113560 | bytes 5283852 | tf_op jit(solution)/shard_map/s,src->rc/dot_general | solution.py:120
  206.6 1.7 bitcast_add_fusion
  208.3 1.7 fusion.35
  212.0 2.3 fusion.26
  214.3 24.9 %all_to_all.30 = bf16[16,64,256]{2,1,0:T(8,128)(2,1)S(1)} all-to-all(bf16[16,64,256]{2,1,0:T(8,128)(2,1)S(1)} %bitcast.111), channel_id=1, replica_groups=mesh['sx'=4,'sy'=4,'tensor'=16] {'tensor'}, dimensions={0} | all-to-all | bytes 1048576 | tf_op jit(solution)/shard_map/all_to_all | solution.py:209
  242.1 1.2 fusion.34
  (108 shorter events, 21.3 us)
Async XLA Ops:
  6.5 2.6 %copy-start.4 = (bf16[64,4096]{1,0:T(8,128)(2,1)S(1)}, bf16[64,4096]{1,0:T(8,128)(2,1)}, u32[]{:S(2)}) copy-start(bf16[64,4096]{1,0:T(8,128)(2,1)} %param.8) | copy-start | bytes 1572868
  82.2 1.7 copy-start.8
  82.2 1.7 copy-start.9
  82.2 6.1 %copy-start.6 = (s32[1024]{0:T(1024)S(1)}, s32[1024]{0:T(1024)}, u32[]{:S(2)}) copy-start(s32[1024]{0:T(1024)} %param.13) | copy-start | bytes 12292
  83.9 16.3 %collective-permute-start = (bf16[1024,1024]{1,0:T(8,128)(2,1)}, bf16[1024,1024]{1,0:T(8,128)(2,1)}, u32[]{:S(2)}, u32[]{:S(2)}) collective-permute-start(bf16[1024,1024]{1,0:T(8,128)(2,1)} %slice.168), channel_id=1, source_target_pairs={{0,1},{1,0},{2,3},{3,2},{4,5},{5,4},{6,7},{7,6},{8,9},{9,8},{10,11... | collective-permute-start | bytes 6291464 | tf_op jit(solution)/shard_map/ppermute | solution.py:163
  84.5 10.8 %all-to-all-start = ((bf16[64,16,2]{0,2,1:T(2,128)(2,1)}), bf16[64,16,2]{0,2,1:T(2,128)(2,1)S(1)}, u32[]{:S(2)}, u32[]{:S(2)}) async-start(bf16[64,16,2]{0,2,1:T(2,128)(2,1)} %bitcast.2), calls=%async_computation | async-start | bytes 16384 | tf_op jit(solution)/shard_map/all_to_all | solution.py:159
  88.3 49.7 %all-gather.4.cloned.1.call-start = ((), (), s32[]{:S(2)}) async-start(), calls=%async_computation.3 | async-start | bytes 2641920 | tf_op jit(solution)/shard_map/all_gather | solution.py:105
  100.9 1.4 copy-start.2
  107.1 91.7 %all-gather.6.cloned.1.call-start = ((), (), s32[]{:S(2)}) async-start(), calls=%async_computation.4 | async-start | bytes 5283840 | tf_op jit(solution)/shard_map/all_gather | solution.py:115
  147.9 2.2 copy-start.3
  150.2 2.9 %copy-start = (bf16[1024,1024]{1,0:T(8,128)(2,1)}, bf16[1024,1024]{1,0:T(8,128)(2,1)S(1)}, u32[]{:S(2)}) copy-start(bf16[1024,1024]{1,0:T(8,128)(2,1)S(1)} %broadcast_select_fusion.1) | copy-start | bytes 6291460
  205.3 3.0 %copy-start.1 = (bf16[1024,1024]{1,0:T(8,128)(2,1)S(1)}, bf16[1024,1024]{1,0:T(8,128)(2,1)}, u32[]{:S(2)}) copy-start(bf16[1024,1024]{1,0:T(8,128)(2,1)} %copy-done) | copy-start | bytes 6291460
  241.1 1.0 copy-start.5
  241.1 1.0 copy-start.7
Sparse Core Ops, SparseCore 0:
  107.2 30.6 all-gather.3
  148.0 50.7 all-gather.5

commit v8 on v7

--- a/solution.py
+++ b/solution.py
@@ -126,6 +126,19 @@
     return state, in_last
 
 
+def prefix_from_all(packed, head_dim, row_axis, col_axis):
+    column_count = packed.shape[1]
+    row = meta_row(head_dim, column_count)
+    axes = (col_axis, row_axis)
+    gathered = lax.all_gather(packed.astype(jnp.bfloat16), axes)
+    meta = gathered[:, row, :4].astype(jnp.float32)
+    decay, first, last = meta[:, 0] + meta[:, 3], meta[:, 1], meta[:, 2]
+    me = lax.axis_index(col_axis) * lax.axis_size(row_axis) + lax.axis_index(row_axis)
+    weight, unused_decay, unused_first, in_last = prefix_weights(decay, first, last, me)
+    state = jnp.einsum("s,src->rc", weight, gathered.astype(jnp.float32))
+    return state, in_last
+
+
 def on_device(
     queries, key_rows, values, input_gate, forget_gate, segment_ids, output_gate, norm_gain
 ):
@@ -175,7 +188,7 @@
     cumulative = jnp.cumsum(log_forget)
 
     packed = pack_summary(key_all, value_all, gate_in, cumulative, segment_ids, key_scale)
-    in_packed, in_last = prefix_2d(packed, head_dim, "sy", "sx")
+    in_packed, in_last = prefix_from_all(packed, head_dim, "sy", "sx")
     in_row = meta_row(head_dim, column_count)
     in_state = in_packed[:head_dim]
     in_norm = in_packed[head_dim:in_row].reshape(head_dim)

time: 254 us -> 235 us (0.925)
  matrix products: 25.3 us -> 19.2 us
  other arithmetic: 15.1 us -> 9.75 us
  between operations: 22.6 us -> 18.7 us
  local copies, waits for them, and re-layouts: 17.6 us -> 14.8 us
    dot_general x3 -> x1, matrix products: 11.9 us -> 5.33 us  [prefix_from_all(): state = jnp.einsum('s,src->rc', weight, gathered.astype(jnp.float32))]
    all_gather x2 -> x1, waiting for transfers between devices: 65.7 us -> 65.8 us  [prefix_from_all(): gathered = lax.all_gather(packed.astype(jnp.bfloat16), axes)]
  transfers between devices with their start and end apart: 4 -> 3, of which waited for: 3 -> 2; matrix products, arithmetic and copies ran while one was open for 7% -> 5% of each run, Pallas kernels for 0% -> 0%
where the time goes in v8:
time: 235 us; the launch traced here: 232 us
  blocking collectives  96.2 us (41%)
  waiting for transfers between devices  69.4 us (30%)
  matrix products  19.2 us (8%)
  between operations  18.7 us (8%)
  local copies, waits for them, and re-layouts  14.8 us (6%)
  other arithmetic  9.75 us (4%)
  starting transfers between devices  3.98 us (2%)
    all_to_all x1, blocking collectives, on_device(): lax.all_to_all(both_send, 'tensor', split_axis=1, concat_axis=0, tiled=True)  71.1 us
    all_gather x1, waiting for transfers between devices, prefix_from_all(): gathered = lax.all_gather(packed.astype(jnp.bfloat16), axes)  65.8 us
    all_to_all x1, blocking collectives, on_device(): lax.all_to_all(hidden.reshape(tensor_size, row_count, column_count), 'ten...  25.1 us
    dot_general x4, matrix products, one(): lax.dot_general(narrow.astype(jnp.bfloat16), part.astype(jnp.bfloat16), d...  5.63 us
    dot_general x1, matrix products, prefix_from_all(): state = jnp.einsum('s,src->rc', weight, gathered.astype(jnp.float32))  5.33 us
    dot_general x4, matrix products, one(): lax.dot_general(part.astype(jnp.bfloat16), narrow.astype(jnp.bfloat16), d...  5.31 us
  transfers between devices with their start and end apart: 3, of which 2 were waited for; matrix products, arithmetic and copies ran while one was open for 5% of the time, Pallas kernels for 0%

profile of v8, /device:TPU:23, one launch (start us, length us, event | category | flops | bytes accessed | tf_op | source)
XLA Modules:
  0.0 231.9 jit_solution(16700881353495895327)
XLA Ops:
  6.5 1.1 copy.69
  7.6 1.4 stack_reshape.7
  9.1 1.4 stack_reshape.6
  12.1 71.1 %all_to_all.29 = bf16[64,16,1280]{2,0,1:T(8,128)(2,1)S(1)} all-to-all(bf16[64,16,1280]{2,0,1:T(8,128)(2,1)S(1)} %pad_maximum_fusion), channel_id=1, replica_groups=mesh['sx'=4,'sy'=4,'tensor'=16] {'tensor'}, dimensions={1} | all-to-all | bytes 5242880 | tf_op jit(solution)/shard_map/all_to_all | solution.py:171
  83.2 1.6 slice.90
  85.5 3.8 %all-to-all-start = ((bf16[64,16,2]{0,2,1:T(2,128)(2,1)}), bf16[64,16,2]{0,2,1:T(2,128)(2,1)S(1)}, u32[]{:S(2)}, u32[]{:S(2)}) async-start(bf16[64,16,2]{0,2,1:T(2,128)(2,1)} %bitcast.2), calls=%async_computation | async-start | bytes 16384 | tf_op jit(solution)/shard_map/all_to_all | solution.py:172
  92.6 3.6 %all-to-all-done = bf16[64,16,2]{0,2,1:T(2,128)(2,1)S(1)} async-done(((bf16[64,16,2]{0,2,1:T(2,128)(2,1)}), bf16[64,16,2]{0,2,1:T(2,128)(2,1)S(1)}, u32[]{:S(2)}, u32[]{:S(2)}) %all-to-all-start) | async-done | bytes 4128 | tf_op jit(solution)/shard_map/all_to_all | solution.py:172
  99.9 1.3 select_multiply_fusion
  101.2 0.8 fusion.4
  102.0 1.0 fusion.6
  103.3 1.8 fusion.16
  105.1 1.9 concatenate.26
  107.0 1.1 select_convert_fusion
  108.1 2.0 broadcast_select_fusion.1
  110.4 2.9 %fusion.49 = (f32[1024]{0:T(1024)S(1)}, f32[1024,1024]{0,1:T(8,128)S(1)}) fusion(bf16[1024,1024]{1,0:T(8,128)(2,1)S(1)} %broadcast_select_fusion.1, bf16[1024,1024]{1,0:T(8,128)(2,1)S(1)} %copy-done.3, f32[1024]{0:T(1024)S(1)} %bitcast.107, f32[1024]{0:T(1024)S(1)} %add_bitcast_fusion, s32[1024]{0:T(1024)S(1)} %copy-done.6), kind=kOutput, calls=%fused_computation.92 | convolution fusion | flops 2157968384 | bytes 8404992 | tf_op jit(solution)/shard_map/dot_general | solution.py:203
  113.3 0.8 fusion.8
  114.0 1.8 fusion.14
  115.8 65.8 %all-gather.2.cloned.1.call-done = bf16[16,1032,256]{2,1,0:T(8,128)(2,1)} async-done(((bf16[1,1032,256]{2,1,0:T(8,128)(2,1)}), bf16[16,1032,256]{2,1,0:T(8,128)(2,1)}) %all-gather.2.cloned.1.call-update) | async-done | bytes 8454160 | tf_op jit(solution)/shard_map/all_gather | solution.py:133
  181.5 0.8 slice.92
  182.9 5.3 %fusion = f32[1,1032,256]{2,0,1:T(1,128)S(1)} fusion(bf16[16,1032,256]{2,1,0:T(8,128)(2,1)} %all-gather.2.cloned.1.call-done, bf16[1]{0:T(256)(128)(2,1)} %constant.140, bf16[15]{0:T(256)(128)(2,1)S(1)} %slice.84, s32[]{:T(128)S(6)} %add.81), kind=kOutput, calls=%fused_computation | convolution fusion | flops 8454240 | bytes 9510948 | tf_op jit(solution)/shard_map/s,src->rc/dot_general | solution.py:138
  188.4 1.8 fusion.31
  193.4 2.6 %fusion.22 = bf16[1024,256]{1,0:T(8,128)(2,1)S(1)} fusion(f32[1024,256]{1,0:T(8,128)} %fusion.14, f32[1024,256]{1,0:T(8,128)} %fusion.31, bf16[1024,1024]{1,0:T(8,128)(2,1)S(1)} %copy-done.1, f32[1032,256]{1,0:T(8,128)} %bitcast.98, f32[1024]{0:T(1024)S(1)} %get-tuple-element.5, f32[1024]{0:T(1024)S(1)} %get-tuple-element.6), kind=kOutput, calls=%fused_computation.37 | convolution fusion | flops 538705920 | bytes 5775360 | tf_op jit(solution)/shard_map/dot_general | solution.py:31
  196.0 25.1 %all_to_all.30 = bf16[16,64,256]{2,1,0:T(8,128)(2,1)S(1)} all-to-all(bf16[16,64,256]{2,1,0:T(8,128)(2,1)S(1)} %bitcast.100), channel_id=1, replica_groups=mesh['sx'=4,'sy'=4,'tensor'=16] {'tensor'}, dimensions={0} | all-to-all | bytes 1048576 | tf_op jit(solution)/shard_map/all_to_all | solution.py:222
  223.9 1.2 fusion.30
  (83 shorter events, 11.5 us)
Async XLA Ops:
  83.2 1.7 copy-start.8
  83.2 1.7 copy-start.9
  83.2 6.3 %copy-start.6 = (s32[1024]{0:T(1024)S(1)}, s32[1024]{0:T(1024)}, u32[]{:S(2)}) copy-start(s32[1024]{0:T(1024)} %param.13) | copy-start | bytes 12292
  84.8 16.3 %collective-permute-start = (bf16[1024,1024]{1,0:T(8,128)(2,1)}, bf16[1024,1024]{1,0:T(8,128)(2,1)}, u32[]{:S(2)}, u32[]{:S(2)}) collective-permute-start(bf16[1024,1024]{1,0:T(8,128)(2,1)} %slice.90), channel_id=1, source_target_pairs={{0,1},{1,0},{2,3},{3,2},{4,5},{5,4},{6,7},{7,6},{8,9},{9,8},{10,11... | collective-permute-start | bytes 6291464 | tf_op jit(solution)/shard_map/ppermute | solution.py:176
  85.5 10.8 %all-to-all-start = ((bf16[64,16,2]{0,2,1:T(2,128)(2,1)}), bf16[64,16,2]{0,2,1:T(2,128)(2,1)S(1)}, u32[]{:S(2)}, u32[]{:S(2)}) async-start(bf16[64,16,2]{0,2,1:T(2,128)(2,1)} %bitcast.2), calls=%async_computation | async-start | bytes 16384 | tf_op jit(solution)/shard_map/all_to_all | solution.py:172
  89.2 92.3 %all-gather.2.cloned.1.call-start = ((), (), s32[]{:S(2)}) async-start(), calls=%async_computation.3 | async-start | bytes 8982528 | tf_op jit(solution)/shard_map/all_gather | solution.py:133
  102.0 1.3 copy-start.2
  108.1 2.2 copy-start.3
  110.3 2.9 %copy-start = (bf16[1024,1024]{1,0:T(8,128)(2,1)}, bf16[1024,1024]{1,0:T(8,128)(2,1)S(1)}, u32[]{:S(2)}) copy-start(bf16[1024,1024]{1,0:T(8,128)(2,1)S(1)} %broadcast_select_fusion.1) | copy-start | bytes 6291460
  182.9 5.4 %copy-start.1 = (bf16[1024,1024]{1,0:T(8,128)(2,1)S(1)}, bf16[1024,1024]{1,0:T(8,128)(2,1)}, u32[]{:S(2)}) copy-start(bf16[1024,1024]{1,0:T(8,128)(2,1)} %copy-done) | copy-start | bytes 6291460
  188.4 1.8 copy-start.4
  222.9 1.0 copy-start.5
  222.9 1.0 copy-start.7
Sparse Core Ops, SparseCore 0:
  108.2 73.2 all-gather.1

commit v9 on v8

--- a/solution.py
+++ b/solution.py
@@ -155,30 +155,35 @@
             row_count, tensor_size, width
         )
 
-    pair_q_k = jnp.stack(
-        [
-            queries.reshape(row_count, head_count, head_dim),
-            key_rows.reshape(row_count, head_count, head_dim),
-        ],
-        axis=2,
-    )
-    pair_send = jnp.broadcast_to(
-        pair_q_k[:, :, None], (row_count, head_count, group_size // 2, 2, head_dim)
-    ).reshape(row_count, tensor_size, head_dim)
+    half = head_dim // 2
+
+    def halves_send(array):
+        shaped = array.reshape(row_count, head_count, 1, 2, half)
+        return jnp.broadcast_to(
+            shaped, (row_count, head_count, group_size // 2, 2, half)
+        ).reshape(row_count, tensor_size, half)
+
+    is_even = lax.axis_index("tensor") % 2 == 0
+    pairs = [(index, index ^ 1) for index in range(tensor_size)]
+
+    def joined(own):
+        other = lax.ppermute(own, "tensor", pairs)
+        return jnp.where(
+            is_even, jnp.concatenate([own, other], axis=1), jnp.concatenate([other, own], axis=1)
+        )
+
     value_send = values.reshape(row_count, tensor_size, column_count)
-    both_send = jnp.concatenate([pair_send, value_send], axis=2)
+    first_send = jnp.concatenate([halves_send(key_rows), value_send], axis=2)
+    first_all = lax.all_to_all(first_send, "tensor", split_axis=1, concat_axis=0, tiled=True)
+    first_all = first_all.reshape(-1, half + column_count)
+    value_all = first_all[:, half:]
+    key_all = joined(first_all[:, :half])
     gate_send = spread_heads(jnp.stack([input_gate, forget_gate], axis=2), 2)
-    both_all = lax.all_to_all(both_send, "tensor", split_axis=1, concat_axis=0, tiled=True)
     gate_all = lax.all_to_all(gate_send, "tensor", split_axis=1, concat_axis=0, tiled=True)
-    both_all = both_all.reshape(-1, head_dim + column_count)
-    own_part = both_all[:, :head_dim]
-    value_all = both_all[:, head_dim:]
-    other_part = lax.ppermute(
-        own_part, "tensor", [(index, index ^ 1) for index in range(tensor_size)]
-    )
-    is_even = lax.axis_index("tensor") % 2 == 0
-    query_all = jnp.where(is_even, own_part, other_part)
-    key_all = jnp.where(is_even, other_part, own_part)
+    query_half = lax.all_to_all(
+        halves_send(queries), "tensor", split_axis=1, concat_axis=0, tiled=True
+    ).reshape(-1, half)
+    query_all = joined(query_half)
     token_count = query_all.shape[0]
     gate_f = gate_all.reshape(token_count, 2).astype(jnp.float32)
     gate_in = gate_f[:, 0]

time: 235 us -> 207 us (0.88)
  blocking collectives: 96.2 us -> 57.3 us
  starting transfers between devices: 3.98 us -> 13.8 us
  local copies, waits for them, and re-layouts: 14.8 us -> 9.83 us
  matrix products: 19.2 us -> 23.9 us
  other arithmetic: 9.75 us -> 13.1 us
  waiting for transfers between devices: 69.4 us -> 67 us
    all_gather x1, waiting for transfers between devices: 65.8 us -> 26 us  [prefix_from_all(): gathered = lax.all_gather(packed.astype(jnp.bfloat16), axes)]
    all_to_all x1, blocking collectives: 71.1 us -> 32.5 us  [on_device(): lax.all_to_all(halves_send(queries), 'tensor', split_axis=1, concat_axis=...]
    all_to_all x0 -> x1, waiting for transfers between devices: none -> 35.3 us  [on_device(): lax.all_to_all(first_send, 'tensor', split_axis=1, concat_axis=0, tiled=T...]
    all_to_all x1, starting transfers between devices: 3.76 us -> 9.15 us  [on_device(): lax.all_to_all(gate_send, 'tensor', split_axis=1, concat_axis=0, tiled=True)]
    all_to_all x0 -> x1, starting transfers between devices: none -> 4.47 us  [on_device(): lax.all_to_all(first_send, 'tensor', split_axis=1, concat_axis=0, tiled=T...]
    another operation x5 -> x2, local copies, waits for them, and re-layouts: 3.38 us -> 0.2 us  [the longest x3 3.18 us: on_device(): jnp.stack([queries.reshape(row_count, head_count, head_dim), key_rows.res...]
    ppermute x1 -> x2, waiting for transfers between devices: 0.01 us -> 2.79 us  [joined(): other = lax.ppermute(own, 'tensor', pairs)]
    dot_general x4, matrix products: 5.31 us -> 8 us  [one(): lax.dot_general(part.astype(jnp.bfloat16), narrow.astype(jnp.bfloat16), d...]
  transfers between devices with their start and end apart: 3 -> 5, of which waited for: 2 -> 4; matrix products, arithmetic and copies ran while one was open for 5% -> 9% of each run, Pallas kernels for 0% -> 0%
where the time goes in v9:
time: 207 us; the launch traced here: 204 us
  waiting for transfers between devices  67 us (32%)
  blocking collectives  57.3 us (28%)
  matrix products  23.9 us (12%)
  between operations  18.8 us (9%)
  starting transfers between devices  13.8 us (7%)
  other arithmetic  13.1 us (6%)
  local copies, waits for them, and re-layouts  9.83 us (5%)
    all_to_all x1, waiting for transfers between devices, on_device(): lax.all_to_all(first_send, 'tensor', split_axis=1, concat_axis=0, tiled=T...  35.3 us
    all_to_all x1, blocking collectives, on_device(): lax.all_to_all(halves_send(queries), 'tensor', split_axis=1, concat_axis=...  32.5 us
    all_gather x1, waiting for transfers between devices, prefix_from_all(): gathered = lax.all_gather(packed.astype(jnp.bfloat16), axes)  26 us
    all_to_all x1, blocking collectives, on_device(): lax.all_to_all(hidden.reshape(tensor_size, row_count, column_count), 'ten...  24.9 us
    all_to_all x1, starting transfers between devices, on_device(): lax.all_to_all(gate_send, 'tensor', split_axis=1, concat_axis=0, tiled=True)  9.15 us
    dot_general x4, matrix products, one(): lax.dot_general(part.astype(jnp.bfloat16), narrow.astype(jnp.bfloat16), d...  8 us
    dot_general x1, matrix products, on_device(): lax.dot_general(query_all, key_all, (((1,), (1,)), ((), ())), preferred_e...  5.46 us
    dot_general x4, matrix products, one(): lax.dot_general(narrow.astype(jnp.bfloat16), part.astype(jnp.bfloat16), d...  5.27 us
  transfers between devices with their start and end apart: 5, of which 4 were waited for; matrix products, arithmetic and copies ran while one was open for 9% of the time, Pallas kernels for 0%

profile of v9, /device:TPU:23, one launch (start us, length us, event | category | flops | bytes accessed | tf_op | source)
XLA Modules:
  0.0 203.7 jit_solution(12626471096548999098)
XLA Ops:
  7.9 9.2 %all-to-all-start = ((bf16[64,16,2]{0,2,1:T(2,128)(2,1)}), bf16[64,16,2]{0,2,1:T(2,128)(2,1)S(1)}, u32[]{:S(2)}, u32[]{:S(2)}) async-start(bf16[64,16,2]{0,2,1:T(2,128)(2,1)} %bitcast.2), calls=%async_computation | async-start | bytes 16384 | tf_op jit(solution)/shard_map/all_to_all | solution.py:182
  17.0 1.1 copy.75
  18.1 1.4 broadcast_in_dim.73
  19.8 1.3 pad_maximum_fusion
  21.1 2.9 %all-to-all-done = bf16[64,16,2]{0,2,1:T(2,128)(2,1)S(1)} async-done(((bf16[64,16,2]{0,2,1:T(2,128)(2,1)}), bf16[64,16,2]{0,2,1:T(2,128)(2,1)S(1)}, u32[]{:S(2)}, u32[]{:S(2)}) %all-to-all-start) | async-done | bytes 4128 | tf_op jit(solution)/shard_map/all_to_all | solution.py:182
  24.0 4.5 %all-to-all-start.2 = ((bf16[64,16,768]{2,0,1:T(8,128)(2,1)}), bf16[64,16,768]{2,0,1:T(8,128)(2,1)S(1)}, u32[]{:S(2)}, u32[]{:S(2)}) async-start(bf16[64,16,768]{2,0,1:T(8,128)(2,1)} %pad_maximum_fusion), calls=%async_computation.2 | async-start | bytes 3145728 | tf_op jit(solution)/shard_map/all_to_all | solution.py:177
  31.7 35.3 %all-to-all-done.2 = bf16[64,16,768]{2,0,1:T(8,128)(2,1)S(1)} async-done(((bf16[64,16,768]{2,0,1:T(8,128)(2,1)}), bf16[64,16,768]{2,0,1:T(8,128)(2,1)S(1)}, u32[]{:S(2)}, u32[]{:S(2)}) %all-to-all-start.2) | async-done | bytes 1572896 | tf_op jit(solution)/shard_map/all_to_all | solution.py:177
  70.9 1.2 select_multiply_fusion
  72.1 2.6 %fusion.4 = bf16[1024]{0:T(1024)(128)(2,1)S(1)} fusion(f32[1024]{0:T(1024)S(1)} %select_multiply_fusion, bf16[1024,512]{1,0:T(8,128)(2,1)S(1)} %slice.90, bf16[1024,512]{1,0:T(8,128)(2,1)} %collective-permute-done.1, pred[]{:T(512)S(6)} %eq.86), kind=kLoop, calls=%fused_computation.9 | loop fusion | flops 12581888 | bytes 2103297 | tf_op jit(solution)/shard_map/reduce_sum | solution.py:65
  74.7 2.7 %fusion.6 = f32[1024,256]{1,0:T(8,128)S(1)} fusion(f32[1024]{0:T(1024)S(1)} %select_multiply_fusion, bf16[1024,768]{1,0:T(8,128)(2,1)S(1)} %bitcast.88, bf16[1024,512]{1,0:T(8,128)(2,1)} %collective-permute-done.1, bf16[1024,512]{1,0:T(8,128)(2,1)S(1)} %slice.90, pred[]{:T(512)S(6)} %eq.86), kind=kOutput, calls=%fused_computation.13 | convolution fusion | flops 551550976 | bytes 3674113 | tf_op jit(solution)/shard_map/dot_general | solution.py:16
  77.5 2.7 %fusion.16 = bf16[1,1024,256]{2,1,0:T(8,128)(2,1)S(1)} fusion(f32[1024,256]{1,0:T(8,128)S(1)} %fusion.6, f32[1024]{0:T(1024)S(1)} %select_multiply_fusion, bf16[1024,768]{1,0:T(8,128)(2,1)S(1)} %bitcast.89, bf16[1024,512]{1,0:T(8,128)(2,1)} %collective-permute-done.1, bf16[1024,512]{1,0:T(8,128)(2,1)S(1)} %slice.90, pred[]{:T(512)S(6)} %eq.86), kind=kOutput, calls=%fused_computation.26 | convolution fusion | flops 551026688 | bytes 4198401 | tf_op jit(solution)/shard_map/dot_general | solution.py:16
  80.4 1.1 select_convert_fusion
  82.2 32.5 %all_to_all.44 = bf16[64,16,512]{2,0,1:T(8,128)(2,1)S(1)} all-to-all(bf16[64,16,512]{2,0,1:T(8,128)(2,1)S(1)} %bitcast.95), channel_id=1, replica_groups=mesh['sx'=4,'sy'=4,'tensor'=16] {'tensor'}, dimensions={1} | all-to-all | bytes 2097152 | tf_op jit(solution)/shard_map/all_to_all | solution.py:183
  114.7 2.8 %collective-permute-done = bf16[1024,512]{1,0:T(8,128)(2,1)} collective-permute-done((bf16[1024,512]{1,0:T(8,128)(2,1)S(1)}, bf16[1024,512]{1,0:T(8,128)(2,1)}, u32[]{:S(2)}, u32[]{:S(2)}) %collective-permute-start) | collective-permute-done | bytes 1048608 | tf_op jit(solution)/shard_map/ppermute | solution.py:170
  117.4 2.5 %maximum_select_fusion = bf16[1024,1024]{1,0:T(8,128)(2,1)S(1)} fusion(bf16[1024,512]{1,0:T(8,128)(2,1)} %collective-permute-done, bf16[1024,512]{1,0:T(8,128)(2,1)S(1)} %bitcast.93, pred[]{:T(512)S(6)} %eq.86), kind=kLoop, calls=%fused_computation.17 | loop fusion | flops 9437184 | bytes 4194305 | tf_op jit(solution)/shard_map/jit(_where)/select_n | solution.py:171
  119.9 5.5 %fusion.49 = (f32[1024]{0:T(1024)S(1)}, f32[1024,1024]{0,1:T(8,128)S(1)}) fusion(bf16[1024,1024]{1,0:T(8,128)(2,1)S(1)} %maximum_select_fusion, bf16[1024,512]{1,0:T(8,128)(2,1)} %collective-permute-done.1, bf16[1024,512]{1,0:T(8,128)(2,1)S(1)} %copy-done.3, pred[]{:T(512)S(6)} %eq.86, f32[1024]{0:T(1024)S(1)} %bitcast.113, f32[1024]{0:T(1024)S(1)} %add_bitcast_fusion, ...), kind=kOutput, calls=%fused_computation.91 | convolution fusion | flops 2167405568 | bytes 8404993 | tf_op jit(solution)/shard_map/dot_general | solution.py:208
  126.2 1.8 fusion.14
  128.0 26.0 %all-gather.2.cloned.1.call-done = bf16[16,1032,256]{2,1,0:T(8,128)(2,1)} async-done(((bf16[1,1032,256]{2,1,0:T(8,128)(2,1)}), bf16[16,1032,256]{2,1,0:T(8,128)(2,1)}) %all-gather.2.cloned.1.call-update) | async-done | bytes 8454160 | tf_op jit(solution)/shard_map/all_gather | solution.py:133
  154.0 0.8 slice.92
  155.4 5.2 %fusion = f32[1,1032,256]{2,0,1:T(1,128)S(1)} fusion(bf16[16,1032,256]{2,1,0:T(8,128)(2,1)} %all-gather.2.cloned.1.call-done, bf16[1]{0:T(256)(128)(2,1)} %constant.156, bf16[15]{0:T(256)(128)(2,1)S(1)} %slice.84, s32[]{:T(128)S(6)} %add.81), kind=kOutput, calls=%fused_computation | convolution fusion | flops 8454240 | bytes 9510948 | tf_op jit(solution)/shard_map/s,src->rc/dot_general | solution.py:138
  160.6 1.7 fusion.31
  165.6 2.3 %fusion.22 = bf16[1024,256]{1,0:T(8,128)(2,1)S(1)} fusion(f32[1024,256]{1,0:T(8,128)} %fusion.14, f32[1024,256]{1,0:T(8,128)} %fusion.31, bf16[1024,1024]{1,0:T(8,128)(2,1)S(1)} %maximum_select_fusion, f32[1032,256]{1,0:T(8,128)S(1)} %bitcast.104, f32[1024]{0:T(1024)S(1)} %get-tuple-element.5, f32[1024]{0:T(1024)S(1)} %get-tuple-element.6), kind=kOutput, calls=%fused_computation.37 | convolution fusion | flops 538705920 | bytes 5775360 | tf_op jit(solution)/shard_map/dot_general | solution.py:31
  167.9 24.9 %all_to_all.45 = bf16[16,64,256]{2,1,0:T(8,128)(2,1)S(1)} all-to-all(bf16[16,64,256]{2,1,0:T(8,128)(2,1)S(1)} %bitcast.106), channel_id=1, replica_groups=mesh['sx'=4,'sy'=4,'tensor'=16] {'tensor'}, dimensions={0} | all-to-all | bytes 1048576 | tf_op jit(solution)/shard_map/all_to_all | solution.py:227
  195.7 1.2 fusion.30
  (84 shorter events, 12.1 us)
Async XLA Ops:
  7.9 16.1 %all-to-all-start = ((bf16[64,16,2]{0,2,1:T(2,128)(2,1)}), bf16[64,16,2]{0,2,1:T(2,128)(2,1)S(1)}, u32[]{:S(2)}, u32[]{:S(2)}) async-start(bf16[64,16,2]{0,2,1:T(2,128)(2,1)} %bitcast.2), calls=%async_computation | async-start | bytes 16384 | tf_op jit(solution)/shard_map/all_to_all | solution.py:182
  21.1 7.4 %copy-start.6 = (s32[1024]{0:T(1024)S(1)}, s32[1024]{0:T(1024)}, u32[]{:S(2)}) copy-start(s32[1024]{0:T(1024)} %param.13) | copy-start | bytes 12292
  24.0 43.0 %all-to-all-start.2 = ((bf16[64,16,768]{2,0,1:T(8,128)(2,1)}), bf16[64,16,768]{2,0,1:T(8,128)(2,1)S(1)}, u32[]{:S(2)}, u32[]{:S(2)}) async-start(bf16[64,16,768]{2,0,1:T(8,128)(2,1)} %pad_maximum_fusion), calls=%async_computation.2 | async-start | bytes 3145728 | tf_op jit(solution)/shard_map/all_to_all | solution.py:177
  28.4 125.5 %all-gather.2.cloned.1.call-start = ((), (), s32[]{:S(2)}) async-start(), calls=%async_computation.4 | async-start | bytes 8982528 | tf_op jit(solution)/shard_map/all_gather | solution.py:133
  67.0 10.5 %copy-start = (bf16[64,16,768]{2,0,1:T(8,128)(2,1)}, bf16[64,16,768]{2,0,1:T(8,128)(2,1)S(1)}, u32[]{:S(2)}) copy-start(bf16[64,16,768]{2,0,1:T(8,128)(2,1)S(1)} %all-to-all-done.2) | copy-start | bytes 4718596
  67.1 10.4 %copy-start.2 = (bf16[1024,512]{1,0:T(8,128)(2,1)}, bf16[1024,512]{1,0:T(8,128)(2,1)S(1)}, u32[]{:S(2)}) copy-start(bf16[1024,512]{1,0:T(8,128)(2,1)S(1)} %slice.90) | copy-start | bytes 3145732
  67.1 5.0 %collective-permute-start.1 = (bf16[1024,512]{1,0:T(8,128)(2,1)S(1)}, bf16[1024,512]{1,0:T(8,128)(2,1)}, u32[]{:S(2)}, u32[]{:S(2)}) collective-permute-start(bf16[1024,512]{1,0:T(8,128)(2,1)S(1)} %slice.90), channel_id=1, source_target_pairs={{0,1},{1,0},{2,3},{3,2},{4,5},{5,4},{6,7},{7,6},{8,9},{9,8},{10,11... | collective-permute-start | bytes 3145736 | tf_op jit(solution)/shard_map/ppermute | solution.py:170
  80.2 1.3 copy-start.4
  114.7 2.8 %collective-permute-start = (bf16[1024,512]{1,0:T(8,128)(2,1)S(1)}, bf16[1024,512]{1,0:T(8,128)(2,1)}, u32[]{:S(2)}, u32[]{:S(2)}) collective-permute-start(bf16[1024,512]{1,0:T(8,128)(2,1)S(1)} %bitcast.92), channel_id=1, source_target_pairs={{0,1},{1,0},{2,3},{3,2},{4,5},{5,4},{6,7},{7,6},{8,9},{9,8},{10,11... | collective-permute-start | bytes 3145736 | tf_op jit(solution)/shard_map/ppermute | solution.py:170
  114.7 5.3 %copy-start.3 = (bf16[1024,512]{1,0:T(8,128)(2,1)S(1)}, bf16[1024,512]{1,0:T(8,128)(2,1)}, u32[]{:S(2)}) copy-start(bf16[1024,512]{1,0:T(8,128)(2,1)} %copy-done.2) | copy-start | bytes 3145732
  119.9 5.5 %copy-start.1 = (bf16[64,16,768]{2,0,1:T(8,128)(2,1)S(1)}, bf16[64,16,768]{2,0,1:T(8,128)(2,1)}, u32[]{:S(2)}) copy-start(bf16[64,16,768]{2,0,1:T(8,128)(2,1)} %copy-done) | copy-start | bytes 4718596
  194.7 1.0 copy-start.5
  194.7 1.0 copy-start.7
Sparse Core Ops, SparseCore 0:
  81.7 72.2 all-gather.1

commit v10 on v9

--- a/solution.py
+++ b/solution.py
@@ -60,9 +60,10 @@
     tail_weight = jnp.exp(total_log - cumulative + gate_in) * (segment_ids == last_seg).astype(
         jnp.float32
     )
-    scaled_keys = key_all.astype(jnp.float32) * (key_scale * tail_weight)[:, None]
-    state = split_dot(scaled_keys, value_all, (((0,), (0,)), ((), ())))
-    norm = jnp.sum(scaled_keys, axis=0)
+    token_weight = key_scale * tail_weight
+    weighted_values = value_all.astype(jnp.float32) * token_weight[:, None]
+    state = split_dot_left(key_all, weighted_values, (((0,), (0,)), ((), ())))
+    norm = split_dot_left(key_all, token_weight[:, None], (((0,), (0,)), ((), ())))[:, 0]
     decay = jnp.exp(total_log) * (last_seg == first_seg).astype(jnp.float32)
     norm_rows = head_dim // column_count
     rows = meta_row(head_dim, column_count) + 1
@@ -173,13 +174,17 @@
         )
 
     value_send = values.reshape(row_count, tensor_size, column_count)
-    first_send = jnp.concatenate([halves_send(key_rows), value_send], axis=2)
+    gate_lanes = 128
+    gate_send = jnp.pad(
+        spread_heads(jnp.stack([input_gate, forget_gate], axis=2), 2),
+        ((0, 0), (0, 0), (0, gate_lanes - 2)),
+    )
+    first_send = jnp.concatenate([halves_send(key_rows), value_send, gate_send], axis=2)
     first_all = lax.all_to_all(first_send, "tensor", split_axis=1, concat_axis=0, tiled=True)
-    first_all = first_all.reshape(-1, half + column_count)
-    value_all = first_all[:, half:]
+    first_all = first_all.reshape(-1, half + column_count + gate_lanes)
+    value_all = first_all[:, half : half + column_count]
+    gate_all = first_all[:, half + column_count : half + column_count + 2]
     key_all = joined(first_all[:, :half])
-    gate_send = spread_heads(jnp.stack([input_gate, forget_gate], axis=2), 2)
-    gate_all = lax.all_to_all(gate_send, "tensor", split_axis=1, concat_axis=0, tiled=True)
     query_half = lax.all_to_all(
         halves_send(queries), "tensor", split_axis=1, concat_axis=0, tiled=True
     ).reshape(-1, half)

time: 207 us -> 203 us (0.981)
  matrix products: 23.9 us -> 18.7 us
  waiting for transfers between devices: 67 us -> 71.8 us
  starting transfers between devices: 13.8 us -> 9.42 us
    all_to_all x1 -> x0, starting transfers between devices: 9.15 us -> none  [on_device(): lax.all_to_all(gate_send, 'tensor', split_axis=1, concat_axis=0, tiled=True)]
    dot_general x4 -> x2, matrix products: 8 us -> 2.54 us  [one(): lax.dot_general(part.astype(jnp.bfloat16), narrow.astype(jnp.bfloat16), d...]
    all_to_all x1, waiting for transfers between devices: 35.3 us -> 40.5 us  [on_device(): lax.all_to_all(first_send, 'tensor', split_axis=1, concat_axis=0, tiled=T...]
    all_to_all x1, starting transfers between devices: 4.47 us -> 9.28 us  [on_device(): lax.all_to_all(first_send, 'tensor', split_axis=1, concat_axis=0, tiled=T...]
    all_to_all x1 -> x0, waiting for transfers between devices: 2.89 us -> none  [on_device(): lax.all_to_all(gate_send, 'tensor', split_axis=1, concat_axis=0, tiled=True)]
    dot_general x4 -> x8, matrix products: 5.27 us -> 8.05 us  [one(): lax.dot_general(narrow.astype(jnp.bfloat16), part.astype(jnp.bfloat16), d...]
    reduce_sum x1 -> x0, other arithmetic: 2.6 us -> none  [pack_summary(): norm = jnp.sum(scaled_keys, axis=0)]
    dot_general x1, matrix products: 5.46 us -> 2.95 us  [on_device(): lax.dot_general(query_all, key_all, (((1,), (1,)), ((), ())), preferred_e...]
  transfers between devices with their start and end apart: 5 -> 4, of which waited for: 4 -> 3; matrix products, arithmetic and copies ran while one was open for 9% -> 6% of each run, Pallas kernels for 0% -> 0%
where the time goes in v10:
time: 203 us; the launch traced here: 199 us
  waiting for transfers between devices  71.8 us (35%)
  blocking collectives  57.7 us (28%)
  between operations  18.8 us (9%)
  matrix products  18.7 us (9%)
  other arithmetic  13.6 us (7%)
  starting transfers between devices  9.42 us (5%)
  local copies, waits for them, and re-layouts  9.39 us (5%)
    all_to_all x1, waiting for transfers between devices, on_device(): lax.all_to_all(first_send, 'tensor', split_axis=1, concat_axis=0, tiled=T...  40.5 us
    all_to_all x1, blocking collectives, on_device(): lax.all_to_all(halves_send(queries), 'tensor', split_axis=1, concat_axis=...  32.8 us
    all_gather x1, waiting for transfers between devices, prefix_from_all(): gathered = lax.all_gather(packed.astype(jnp.bfloat16), axes)  28.4 us
    all_to_all x1, blocking collectives, on_device(): lax.all_to_all(hidden.reshape(tensor_size, row_count, column_count), 'ten...  24.9 us
    all_to_all x1, starting transfers between devices, on_device(): lax.all_to_all(first_send, 'tensor', split_axis=1, concat_axis=0, tiled=T...  9.28 us
    dot_general x8, matrix products, one(): lax.dot_general(narrow.astype(jnp.bfloat16), part.astype(jnp.bfloat16), d...  8.05 us
    dot_general x1, matrix products, prefix_from_all(): state = jnp.einsum('s,src->rc', weight, gathered.astype(jnp.float32))  5.18 us
    select_n x2, other arithmetic, joined(): jnp.where(is_even, jnp.concatenate([own, other], axis=1), jnp.concatenate...  4.78 us
  transfers between devices with their start and end apart: 4, of which 3 were waited for; matrix products, arithmetic and copies ran while one was open for 6% of the time, Pallas kernels for 0%

profile of v10, /device:TPU:23, one launch (start us, length us, event | category | flops | bytes accessed | tf_op | source)
XLA Modules:
  0.0 199.4 jit_solution(2589575085323115205)
XLA Ops:
  6.5 0.7 pad_maximum_fusion
  7.4 1.1 copy.62
  8.5 1.4 broadcast_in_dim.70
  10.2 1.5 fusion.8
  11.7 9.3 %all-to-all-start = ((bf16[64,16,896]{2,0,1:T(8,128)(2,1)}), bf16[64,16,896]{2,0,1:T(8,128)(2,1)S(1)}, u32[]{:S(2)}, u32[]{:S(2)}) async-start(bf16[64,16,896]{2,0,1:T(8,128)(2,1)} %fusion.8), calls=%async_computation | async-start | bytes 3670016 | tf_op jit(solution)/shard_map/all_to_all | solution.py:183
  24.3 40.5 %all-to-all-done = bf16[64,16,896]{2,0,1:T(8,128)(2,1)S(1)} async-done(((bf16[64,16,896]{2,0,1:T(8,128)(2,1)}), bf16[64,16,896]{2,0,1:T(8,128)(2,1)S(1)}, u32[]{:S(2)}, u32[]{:S(2)}) %all-to-all-start) | async-done | bytes 1835040 | tf_op jit(solution)/shard_map/all_to_all | solution.py:183
  67.4 1.3 fusion.37
  70.6 2.3 %maximum_select_fusion.1 = bf16[1024,1024]{1,0:T(8,128)(2,1)S(1)} fusion(bf16[1024,512]{1,0:T(8,128)(2,1)} %collective-permute-done.1, bf16[1024,512]{1,0:T(8,128)(2,1)S(1)} %slice.95, pred[]{:T(512)S(6)} %eq.86), kind=kLoop, calls=%fused_computation.13 | loop fusion | flops 9437184 | bytes 4194305 | tf_op jit(solution)/shard_map/jit(_where)/select_n | solution.py:172
  72.8 1.0 fusion.28
  73.8 1.0 fusion.12
  75.8 1.1 select_convert_fusion
  77.5 32.8 %all_to_all.35 = bf16[64,16,512]{2,0,1:T(8,128)(2,1)S(1)} all-to-all(bf16[64,16,512]{2,0,1:T(8,128)(2,1)S(1)} %bitcast.110), channel_id=1, replica_groups=mesh['sx'=4,'sy'=4,'tensor'=16] {'tensor'}, dimensions={1} | all-to-all | bytes 2097152 | tf_op jit(solution)/shard_map/all_to_all | solution.py:188
  110.4 2.8 %collective-permute-done = bf16[1024,512]{1,0:T(8,128)(2,1)} collective-permute-done((bf16[1024,512]{1,0:T(8,128)(2,1)S(1)}, bf16[1024,512]{1,0:T(8,128)(2,1)}, u32[]{:S(2)}, u32[]{:S(2)}) %collective-permute-start) | collective-permute-done | bytes 1048608 | tf_op jit(solution)/shard_map/ppermute | solution.py:171
  113.1 2.5 %maximum_select_fusion = bf16[1024,1024]{1,0:T(8,128)(2,1)S(1)} fusion(bf16[1024,512]{1,0:T(8,128)(2,1)} %collective-permute-done, bf16[1024,512]{1,0:T(8,128)(2,1)S(1)} %bitcast.108, pred[]{:T(512)S(6)} %eq.86), kind=kLoop, calls=%fused_computation.12 | loop fusion | flops 9437184 | bytes 4194305 | tf_op jit(solution)/shard_map/jit(_where)/select_n | solution.py:172
  115.7 2.9 %fusion.54 = (f32[1024]{0:T(1024)S(1)}, f32[1024,1024]{0,1:T(8,128)S(1)}) fusion(bf16[1024,1024]{1,0:T(8,128)(2,1)S(1)} %maximum_select_fusion, bf16[1024,1024]{1,0:T(8,128)(2,1)S(1)} %copy-done.1, f32[1024]{0:T(1024)S(1)} %get-tuple-element.6, f32[1024]{0:T(1024)S(1)} %add_bitcast_fusion, s32[1024]{0:T(1024)S(1)} %copy-done.6), kind=kOutput, calls=%fused_computation.102 | convolution fusion | flops 2157968384 | bytes 8404992 | tf_op jit(solution)/shard_map/dot_general | solution.py:213
  118.7 0.7 fusion.5
  119.4 1.8 fusion.9
  121.2 28.4 %all-gather.2.cloned.1.call-done = bf16[16,1032,256]{2,1,0:T(8,128)(2,1)} async-done(((bf16[1,1032,256]{2,1,0:T(8,128)(2,1)}), bf16[16,1032,256]{2,1,0:T(8,128)(2,1)}) %all-gather.2.cloned.1.call-update) | async-done | bytes 8454160 | tf_op jit(solution)/shard_map/all_gather | solution.py:134
  149.6 0.8 slice.97
  151.0 5.2 %fusion = f32[1,1032,256]{2,0,1:T(1,128)S(1)} fusion(bf16[16,1032,256]{2,1,0:T(8,128)(2,1)} %all-gather.2.cloned.1.call-done, bf16[1]{0:T(256)(128)(2,1)} %constant.164, bf16[15]{0:T(256)(128)(2,1)S(1)} %slice.88, s32[]{:T(128)S(6)} %add.87), kind=kOutput, calls=%fused_computation | convolution fusion | flops 8454240 | bytes 9510948 | tf_op jit(solution)/shard_map/s,src->rc/dot_general | solution.py:139
  156.3 1.7 fusion.26
  161.2 2.3 %fusion.16 = bf16[1024,256]{1,0:T(8,128)(2,1)S(1)} fusion(f32[1024,256]{1,0:T(8,128)} %fusion.9, f32[1024,256]{1,0:T(8,128)} %fusion.26, bf16[1024,1024]{1,0:T(8,128)(2,1)S(1)} %maximum_select_fusion, f32[1032,256]{1,0:T(8,128)S(1)} %bitcast.119, f32[1024]{0:T(1024)S(1)} %get-tuple-element.7, f32[1024]{0:T(1024)S(1)} %get-tuple-element.8), kind=kOutput, calls=%fused_computation.32 | convolution fusion | flops 538705920 | bytes 5775360 | tf_op jit(solution)/shard_map/dot_general | solution.py:31
  163.5 24.9 %all_to_all.36 = bf16[16,64,256]{2,1,0:T(8,128)(2,1)S(1)} all-to-all(bf16[16,64,256]{2,1,0:T(8,128)(2,1)S(1)} %bitcast.122), channel_id=1, replica_groups=mesh['sx'=4,'sy'=4,'tensor'=16] {'tensor'}, dimensions={0} | all-to-all | bytes 1048576 | tf_op jit(solution)/shard_map/all_to_all | solution.py:232
  191.4 1.2 fusion.25
  (86 shorter events, 11.5 us)
Async XLA Ops:
  11.7 9.3 %copy-start.6 = (s32[1024]{0:T(1024)S(1)}, s32[1024]{0:T(1024)}, u32[]{:S(2)}) copy-start(s32[1024]{0:T(1024)} %param.13) | copy-start | bytes 12292
  11.7 53.1 %all-to-all-start = ((bf16[64,16,896]{2,0,1:T(8,128)(2,1)}), bf16[64,16,896]{2,0,1:T(8,128)(2,1)S(1)}, u32[]{:S(2)}, u32[]{:S(2)}) async-start(bf16[64,16,896]{2,0,1:T(8,128)(2,1)} %fusion.8), calls=%async_computation | async-start | bytes 3670016 | tf_op jit(solution)/shard_map/all_to_all | solution.py:183
  21.0 128.6 %all-gather.2.cloned.1.call-start = ((), (), s32[]{:S(2)}) async-start(), calls=%async_computation.3 | async-start | bytes 8982528 | tf_op jit(solution)/shard_map/all_gather | solution.py:134
  64.8 9.0 %copy-start.2 = (bf16[64,16,896]{2,0,1:T(8,128)(2,1)}, bf16[64,16,896]{2,0,1:T(8,128)(2,1)S(1)}, u32[]{:S(2)}) copy-start(bf16[64,16,896]{2,0,1:T(8,128)(2,1)S(1)} %all-to-all-done) | copy-start | bytes 5505028
  64.9 5.6 %collective-permute-start.1 = (bf16[1024,512]{1,0:T(8,128)(2,1)S(1)}, bf16[1024,512]{1,0:T(8,128)(2,1)}, u32[]{:S(2)}, u32[]{:S(2)}) collective-permute-start(bf16[1024,512]{1,0:T(8,128)(2,1)S(1)} %slice.95), channel_id=1, source_target_pairs={{0,1},{1,0},{2,3},{3,2},{4,5},{5,4},{6,7},{7,6},{8,9},{9,8},{10,11... | collective-permute-start | bytes 3145736 | tf_op jit(solution)/shard_map/ppermute | solution.py:171
  72.8 2.4 %copy-start = (bf16[1024,1024]{1,0:T(8,128)(2,1)}, bf16[1024,1024]{1,0:T(8,128)(2,1)S(1)}, u32[]{:S(2)}) copy-start(bf16[1024,1024]{1,0:T(8,128)(2,1)S(1)} %maximum_select_fusion.1) | copy-start | bytes 6291460
  75.2 1.7 copy-start.4
  110.3 2.8 %collective-permute-start = (bf16[1024,512]{1,0:T(8,128)(2,1)S(1)}, bf16[1024,512]{1,0:T(8,128)(2,1)}, u32[]{:S(2)}, u32[]{:S(2)}) collective-permute-start(bf16[1024,512]{1,0:T(8,128)(2,1)S(1)} %bitcast.107), channel_id=1, source_target_pairs={{0,1},{1,0},{2,3},{3,2},{4,5},{5,4},{6,7},{7,6},{8,9},{9,8},{10,11... | collective-permute-start | bytes 3145736 | tf_op jit(solution)/shard_map/ppermute | solution.py:171
  110.4 5.3 %copy-start.1 = (bf16[1024,1024]{1,0:T(8,128)(2,1)S(1)}, bf16[1024,1024]{1,0:T(8,128)(2,1)}, u32[]{:S(2)}) copy-start(bf16[1024,1024]{1,0:T(8,128)(2,1)} %copy-done) | copy-start | bytes 6291460
  115.7 3.0 %copy-start.3 = (bf16[64,16,896]{2,0,1:T(8,128)(2,1)S(1)}, bf16[64,16,896]{2,0,1:T(8,128)(2,1)}, u32[]{:S(2)}) copy-start(bf16[64,16,896]{2,0,1:T(8,128)(2,1)} %copy-done.2) | copy-start | bytes 5505028
  190.3 1.0 copy-start.5
  190.3 1.0 copy-start.7
Sparse Core Ops, SparseCore 0:
  77.0 72.5 all-gather.1

commit v11 on v10

--- a/solution.py
+++ b/solution.py
@@ -136,7 +136,7 @@
     decay, first, last = meta[:, 0] + meta[:, 3], meta[:, 1], meta[:, 2]
     me = lax.axis_index(col_axis) * lax.axis_size(row_axis) + lax.axis_index(row_axis)
     weight, unused_decay, unused_first, in_last = prefix_weights(decay, first, last, me)
-    state = jnp.einsum("s,src->rc", weight, gathered.astype(jnp.float32))
+    state = jnp.sum(gathered.astype(jnp.float32) * weight[:, None, None], axis=0)
     return state, in_last
 
 

time: 203 us -> 203 us (level)
  other arithmetic: 13.6 us -> 18.9 us
  matrix products: 18.7 us -> 13.5 us
    reduce_sum x0 -> x1, other arithmetic: none -> 5.23 us  [prefix_from_all(): jnp.sum(gathered.astype(jnp.float32) * weight[:, None, None], axis=0)]
    dot_general x1 -> x0, matrix products: 5.18 us -> none  [prefix_from_all(): state = jnp.einsum('s,src->rc', weight, gathered.astype(jnp.float32))]
where the time goes in v11:
time: 203 us; the launch traced here: 199 us
  waiting for transfers between devices  71.8 us (35%)
  blocking collectives  57.7 us (28%)
  other arithmetic  18.9 us (9%)
  between operations  18.8 us (9%)
  matrix products  13.5 us (7%)
  starting transfers between devices  9.42 us (5%)
  local copies, waits for them, and re-layouts  9.32 us (5%)
    all_to_all x1, waiting for transfers between devices, on_device(): lax.all_to_all(first_send, 'tensor', split_axis=1, concat_axis=0, tiled=T...  40.5 us
    all_to_all x1, blocking collectives, on_device(): lax.all_to_all(halves_send(queries), 'tensor', split_axis=1, concat_axis=...  32.8 us
    all_gather x1, waiting for transfers between devices, prefix_from_all(): gathered = lax.all_gather(packed.astype(jnp.bfloat16), axes)  28.4 us
    all_to_all x1, blocking collectives, on_device(): lax.all_to_all(hidden.reshape(tensor_size, row_count, column_count), 'ten...  24.9 us
    all_to_all x1, starting transfers between devices, on_device(): lax.all_to_all(first_send, 'tensor', split_axis=1, concat_axis=0, tiled=T...  9.28 us
    dot_general x8, matrix products, one(): lax.dot_general(narrow.astype(jnp.bfloat16), part.astype(jnp.bfloat16), d...  8.05 us
    reduce_sum x1, other arithmetic, prefix_from_all(): jnp.sum(gathered.astype(jnp.float32) * weight[:, None, None], axis=0)  5.23 us
    select_n x2, other arithmetic, joined(): jnp.where(is_even, jnp.concatenate([own, other], axis=1), jnp.concatenate...  4.78 us
  transfers between devices with their start and end apart: 4, of which 3 were waited for; matrix products, arithmetic and copies ran while one was open for 6% of the time, Pallas kernels for 0%

profile of v11, /device:TPU:23, one launch (start us, length us, event | category | flops | bytes accessed | tf_op | source)
XLA Modules:
  0.0 199.4 jit_solution(18172257512671947018)
XLA Ops:
  6.5 0.7 pad_maximum_fusion
  7.4 1.1 copy.56
  8.5 1.4 broadcast_in_dim.71
  10.2 1.5 fusion.6
  11.7 9.3 %all-to-all-start = ((bf16[64,16,896]{2,0,1:T(8,128)(2,1)}), bf16[64,16,896]{2,0,1:T(8,128)(2,1)S(1)}, u32[]{:S(2)}, u32[]{:S(2)}) async-start(bf16[64,16,896]{2,0,1:T(8,128)(2,1)} %fusion.6), calls=%async_computation | async-start | bytes 3670016 | tf_op jit(solution)/shard_map/all_to_all | solution.py:183
  24.3 40.5 %all-to-all-done = bf16[64,16,896]{2,0,1:T(8,128)(2,1)S(1)} async-done(((bf16[64,16,896]{2,0,1:T(8,128)(2,1)}), bf16[64,16,896]{2,0,1:T(8,128)(2,1)S(1)}, u32[]{:S(2)}, u32[]{:S(2)}) %all-to-all-start) | async-done | bytes 1835040 | tf_op jit(solution)/shard_map/all_to_all | solution.py:183
  67.4 1.3 fusion.35
  70.6 2.3 %maximum_select_fusion.1 = bf16[1024,1024]{1,0:T(8,128)(2,1)S(1)} fusion(bf16[1024,512]{1,0:T(8,128)(2,1)} %collective-permute-done.1, bf16[1024,512]{1,0:T(8,128)(2,1)S(1)} %slice.95, pred[]{:T(512)S(6)} %eq.86), kind=kLoop, calls=%fused_computation.12 | loop fusion | flops 9437184 | bytes 4194305 | tf_op jit(solution)/shard_map/jit(_where)/select_n | solution.py:172
  72.8 1.0 fusion.26
  73.8 1.0 fusion.10
  75.8 1.1 select_convert_fusion
  77.5 32.8 %all_to_all.35 = bf16[64,16,512]{2,0,1:T(8,128)(2,1)S(1)} all-to-all(bf16[64,16,512]{2,0,1:T(8,128)(2,1)S(1)} %bitcast.104), channel_id=1, replica_groups=mesh['sx'=4,'sy'=4,'tensor'=16] {'tensor'}, dimensions={1} | all-to-all | bytes 2097152 | tf_op jit(solution)/shard_map/all_to_all | solution.py:188
  110.4 2.8 %collective-permute-done = bf16[1024,512]{1,0:T(8,128)(2,1)} collective-permute-done((bf16[1024,512]{1,0:T(8,128)(2,1)S(1)}, bf16[1024,512]{1,0:T(8,128)(2,1)}, u32[]{:S(2)}, u32[]{:S(2)}) %collective-permute-start) | collective-permute-done | bytes 1048608 | tf_op jit(solution)/shard_map/ppermute | solution.py:171
  113.1 2.5 %maximum_select_fusion = bf16[1024,1024]{1,0:T(8,128)(2,1)S(1)} fusion(bf16[1024,512]{1,0:T(8,128)(2,1)} %collective-permute-done, bf16[1024,512]{1,0:T(8,128)(2,1)S(1)} %bitcast.102, pred[]{:T(512)S(6)} %eq.86), kind=kLoop, calls=%fused_computation.11 | loop fusion | flops 9437184 | bytes 4194305 | tf_op jit(solution)/shard_map/jit(_where)/select_n | solution.py:172
  115.7 2.9 %fusion.43 = (f32[1024]{0:T(1024)S(1)}, f32[1024,1024]{0,1:T(8,128)S(1)}) fusion(bf16[1024,1024]{1,0:T(8,128)(2,1)S(1)} %maximum_select_fusion, bf16[1024,1024]{1,0:T(8,128)(2,1)S(1)} %copy-done.1, f32[1024]{0:T(1024)S(1)} %get-tuple-element.6, f32[1024]{0:T(1024)S(1)} %add_bitcast_fusion, s32[1024]{0:T(1024)S(1)} %copy-done.6), kind=kOutput, calls=%fused_computation.92 | convolution fusion | flops 2157968384 | bytes 8404992 | tf_op jit(solution)/shard_map/dot_general | solution.py:213
  118.7 0.7 fusion.3
  119.4 1.8 fusion.7
  121.2 28.4 %all-gather.2.cloned.1.call-done = bf16[16,1032,256]{2,1,0:T(8,128)(2,1)} async-done(((bf16[1,1032,256]{2,1,0:T(8,128)(2,1)}), bf16[16,1032,256]{2,1,0:T(8,128)(2,1)}) %all-gather.2.cloned.1.call-update) | async-done | bytes 8454160 | tf_op jit(solution)/shard_map/all_gather | solution.py:134
  149.6 0.8 slice.97
  151.1 5.2 %multiply_reduce_fusion = f32[1032,256]{1,0:T(8,128)S(1)} fusion(bf16[16,1032,256]{2,1,0:T(8,128)(2,1)} %all-gather.2.cloned.1.call-done, f32[16]{0:T(128)S(1)} %compare_select_fusion.5), kind=kLoop, calls=%fused_computation | loop fusion | flops 12417024 | bytes 9510976 | tf_op jit(solution)/shard_map/reduce_sum | solution.py:139
  156.3 1.7 fusion.24
  161.3 2.3 %fusion.14 = bf16[1024,256]{1,0:T(8,128)(2,1)S(1)} fusion(f32[1024,256]{1,0:T(8,128)} %fusion.7, f32[1024,256]{1,0:T(8,128)} %fusion.24, bf16[1024,1024]{1,0:T(8,128)(2,1)S(1)} %maximum_select_fusion, f32[1032,256]{1,0:T(8,128)S(1)} %multiply_reduce_fusion, f32[1024]{0:T(1024)S(1)} %get-tuple-element.7, f32[1024]{0:T(1024)S(1)} %get-tuple-element.8), kind=kOutput, calls=%fused_computation.31 | convolution fusion | flops 538705920 | bytes 5775360 | tf_op jit(solution)/shard_map/dot_general | solution.py:31
  163.6 24.9 %all_to_all.36 = bf16[16,64,256]{2,1,0:T(8,128)(2,1)S(1)} all-to-all(bf16[16,64,256]{2,1,0:T(8,128)(2,1)S(1)} %bitcast.113), channel_id=1, replica_groups=mesh['sx'=4,'sy'=4,'tensor'=16] {'tensor'}, dimensions={0} | all-to-all | bytes 1048576 | tf_op jit(solution)/shard_map/all_to_all | solution.py:232
  191.4 1.2 fusion.23
  (86 shorter events, 11.5 us)
Async XLA Ops:
  11.7 9.3 %copy-start.6 = (s32[1024]{0:T(1024)S(1)}, s32[1024]{0:T(1024)}, u32[]{:S(2)}) copy-start(s32[1024]{0:T(1024)} %param.13) | copy-start | bytes 12292
  11.7 53.1 %all-to-all-start = ((bf16[64,16,896]{2,0,1:T(8,128)(2,1)}), bf16[64,16,896]{2,0,1:T(8,128)(2,1)S(1)}, u32[]{:S(2)}, u32[]{:S(2)}) async-start(bf16[64,16,896]{2,0,1:T(8,128)(2,1)} %fusion.6), calls=%async_computation | async-start | bytes 3670016 | tf_op jit(solution)/shard_map/all_to_all | solution.py:183
  21.0 128.6 %all-gather.2.cloned.1.call-start = ((), (), s32[]{:S(2)}) async-start(), calls=%async_computation.3 | async-start | bytes 8982528 | tf_op jit(solution)/shard_map/all_gather | solution.py:134
  64.8 9.0 %copy-start.2 = (bf16[64,16,896]{2,0,1:T(8,128)(2,1)}, bf16[64,16,896]{2,0,1:T(8,128)(2,1)S(1)}, u32[]{:S(2)}) copy-start(bf16[64,16,896]{2,0,1:T(8,128)(2,1)S(1)} %all-to-all-done) | copy-start | bytes 5505028
  64.9 5.6 %collective-permute-start.1 = (bf16[1024,512]{1,0:T(8,128)(2,1)S(1)}, bf16[1024,512]{1,0:T(8,128)(2,1)}, u32[]{:S(2)}, u32[]{:S(2)}) collective-permute-start(bf16[1024,512]{1,0:T(8,128)(2,1)S(1)} %slice.95), channel_id=1, source_target_pairs={{0,1},{1,0},{2,3},{3,2},{4,5},{5,4},{6,7},{7,6},{8,9},{9,8},{10,11... | collective-permute-start | bytes 3145736 | tf_op jit(solution)/shard_map/ppermute | solution.py:171
  72.8 2.4 %copy-start = (bf16[1024,1024]{1,0:T(8,128)(2,1)}, bf16[1024,1024]{1,0:T(8,128)(2,1)S(1)}, u32[]{:S(2)}) copy-start(bf16[1024,1024]{1,0:T(8,128)(2,1)S(1)} %maximum_select_fusion.1) | copy-start | bytes 6291460
  75.2 1.7 copy-start.4
  110.3 2.8 %collective-permute-start = (bf16[1024,512]{1,0:T(8,128)(2,1)S(1)}, bf16[1024,512]{1,0:T(8,128)(2,1)}, u32[]{:S(2)}, u32[]{:S(2)}) collective-permute-start(bf16[1024,512]{1,0:T(8,128)(2,1)S(1)} %bitcast.101), channel_id=1, source_target_pairs={{0,1},{1,0},{2,3},{3,2},{4,5},{5,4},{6,7},{7,6},{8,9},{9,8},{10,11... | collective-permute-start | bytes 3145736 | tf_op jit(solution)/shard_map/ppermute | solution.py:171
  110.4 5.3 %copy-start.1 = (bf16[1024,1024]{1,0:T(8,128)(2,1)S(1)}, bf16[1024,1024]{1,0:T(8,128)(2,1)}, u32[]{:S(2)}) copy-start(bf16[1024,1024]{1,0:T(8,128)(2,1)} %copy-done) | copy-start | bytes 6291460
  115.7 3.0 %copy-start.3 = (bf16[64,16,896]{2,0,1:T(8,128)(2,1)S(1)}, bf16[64,16,896]{2,0,1:T(8,128)(2,1)}, u32[]{:S(2)}) copy-start(bf16[64,16,896]{2,0,1:T(8,128)(2,1)} %copy-done.2) | copy-start | bytes 5505028
  190.4 1.0 copy-start.5
  190.4 1.0 copy-start.7
Sparse Core Ops, SparseCore 0:
  77.0 72.5 all-gather.1

commit v12 on v11

--- a/solution.py
+++ b/solution.py
@@ -140,6 +140,36 @@
     return state, in_last
 
 
+def prefix_radix(packed, head_dim, row_axis, col_axis):
+    column_count = packed.shape[1]
+    row = meta_row(head_dim, column_count)
+    axes = (col_axis, row_axis)
+    count = lax.axis_size(col_axis) * lax.axis_size(row_axis)
+
+    def moved(value, steps):
+        pairs = [(source, source + steps) for source in range(count - steps)]
+        return lax.ppermute(value, axes, pairs)
+
+    def merged(parts):
+        stack = jnp.stack(parts, axis=0)
+        meta = stack[:, row, :4]
+        decay, first, last = meta[:, 0] + meta[:, 3], meta[:, 1], meta[:, 2]
+        weight, decay_c, unused_first, last_c = prefix_weights(decay, first, last, len(parts))
+        real = first > 0.0
+        first_real = jnp.max(jnp.where(real, first, 0.0) * (jnp.cumsum(real) == 1))
+        body = jnp.sum(stack * weight[:, None, None], axis=0)
+        return body, decay_c, first_real, last_c
+
+    body, decay_1, first_1, last_1 = merged(
+        [moved(packed, 3), moved(packed, 2), moved(packed, 1), packed]
+    )
+    span = with_meta(body, row, decay_1, first_1, last_1, jnp.zeros((), jnp.float32))
+    state, unused_decay, unused_first, in_last = merged(
+        [moved(span, 13), moved(span, 9), moved(span, 5), moved(span, 1)]
+    )
+    return state, in_last
+
+
 def on_device(
     queries, key_rows, values, input_gate, forget_gate, segment_ids, output_gate, norm_gain
 ):
@@ -198,7 +228,7 @@
     cumulative = jnp.cumsum(log_forget)
 
     packed = pack_summary(key_all, value_all, gate_in, cumulative, segment_ids, key_scale)
-    in_packed, in_last = prefix_from_all(packed, head_dim, "sy", "sx")
+    in_packed, in_last = prefix_radix(packed, head_dim, "sy", "sx")
     in_row = meta_row(head_dim, column_count)
     in_state = in_packed[:head_dim]
     in_norm = in_packed[head_dim:in_row].reshape(head_dim)

time: 203 us -> 365 us (1.80)
  waiting for transfers between devices: 71.8 us -> 244 us
  blocking collectives: 57.7 us -> 25.4 us
  starting transfers between devices: 9.42 us -> 24.5 us
  between operations: 18.8 us -> 6.92 us
  local copies, waits for them, and re-layouts: 9.32 us -> 19 us
  other arithmetic: 18.9 us -> 25.7 us
  matrix products: 13.5 us -> 18.1 us
    ppermute x0 -> x7, waiting for transfers between devices: none -> 178 us  [moved(): return lax.ppermute(value, axes, pairs)]
    all_to_all x1 -> x0, blocking collectives: 32.8 us -> none  [on_device(): lax.all_to_all(halves_send(queries), 'tensor', split_axis=1, concat_axis=...]
    all_gather x1 -> x0, waiting for transfers between devices: 28.4 us -> none  [prefix_from_all(): gathered = lax.all_gather(packed.astype(jnp.bfloat16), axes)]
    all_to_all x0 -> x1, waiting for transfers between devices: none -> 25.6 us  [on_device(): lax.all_to_all(halves_send(queries), 'tensor', split_axis=1, concat_axis=...]
    ppermute x0 -> x7, starting transfers between devices: none -> 11.6 us  [moved(): return lax.ppermute(value, axes, pairs)]
    all_to_all x0 -> x1, starting transfers between devices: none -> 9.15 us  [on_device(): lax.all_to_all(halves_send(queries), 'tensor', split_axis=1, concat_axis=...]
    concatenate x2 -> x3, local copies, waits for them, and re-layouts: 0.19 us -> 6.11 us  [pack_summary(): jnp.concatenate([state, norm.reshape(norm_rows, column_count), filler], a...]
    all_to_all x1, starting transfers between devices: 9.28 us -> 3.61 us  [on_device(): lax.all_to_all(first_send, 'tensor', split_axis=1, concat_axis=0, tiled=T...]
  transfers between devices with their start and end apart: 4 -> 11, of which waited for: 3 -> 6; matrix products, arithmetic and copies ran while one was open for 6% -> 10% of each run, Pallas kernels for 0% -> 0%
where the time goes in v12:
time: 365 us; the launch traced here: 364 us
  waiting for transfers between devices  244 us (67%)
  other arithmetic  25.7 us (7%)
  blocking collectives  25.4 us (7%)
  starting transfers between devices  24.5 us (7%)
  local copies, waits for them, and re-layouts  19 us (5%)
  matrix products  18.1 us (5%)
  between operations  6.92 us (2%)
    ppermute x7, waiting for transfers between devices, moved(): return lax.ppermute(value, axes, pairs)  178 us
    all_to_all x1, waiting for transfers between devices, on_device(): lax.all_to_all(first_send, 'tensor', split_axis=1, concat_axis=0, tiled=T...  40.5 us
    all_to_all x1, waiting for transfers between devices, on_device(): lax.all_to_all(halves_send(queries), 'tensor', split_axis=1, concat_axis=...  25.6 us
    all_to_all x1, blocking collectives, on_device(): lax.all_to_all(hidden.reshape(tensor_size, row_count, column_count), 'ten...  25.4 us
    dot_general x8, matrix products, one(): lax.dot_general(narrow.astype(jnp.bfloat16), part.astype(jnp.bfloat16), d...  12.8 us
    ppermute x7, starting transfers between devices, moved(): return lax.ppermute(value, axes, pairs)  11.6 us
    all_to_all x1, starting transfers between devices, on_device(): lax.all_to_all(halves_send(queries), 'tensor', split_axis=1, concat_axis=...  9.15 us
  transfers between devices with their start and end apart: 11, of which 6 were waited for; matrix products, arithmetic and copies ran while one was open for 10% of the time, Pallas kernels for 0%

profile of v12, /device:TPU:23, one launch (start us, length us, event | category | flops | bytes accessed | tf_op | source)
XLA Modules:
  0.0 364.0 jit_solution(15038375599849122016)
XLA Ops:
  2.7 9.2 %all-to-all-start.1 = ((bf16[64,16,512]{2,0,1:T(8,128)(2,1)}), bf16[64,16,512]{2,0,1:T(8,128)(2,1)S(1)}, u32[]{:S(2)}, u32[]{:S(2)}) async-start(bf16[64,16,512]{2,0,1:T(8,128)(2,1)} %bitcast.8), calls=%async_computation.1 | async-start | bytes 2097152 | tf_op jit(solution)/shard_map/all_to_all | solution.py:218
  12.8 1.5 fusion.6
  14.3 25.6 %all-to-all-done.1 = bf16[64,16,512]{2,0,1:T(8,128)(2,1)S(1)} async-done(((bf16[64,16,512]{2,0,1:T(8,128)(2,1)}), bf16[64,16,512]{2,0,1:T(8,128)(2,1)S(1)}, u32[]{:S(2)}, u32[]{:S(2)}) %all-to-all-start.1) | async-done | bytes 1048608 | tf_op jit(solution)/shard_map/all_to_all | solution.py:218
  39.9 3.6 all-to-all-start
  46.6 40.5 %all-to-all-done = bf16[64,16,896]{2,0,1:T(8,128)(2,1)S(1)} async-done(((bf16[64,16,896]{2,0,1:T(8,128)(2,1)}), bf16[64,16,896]{2,0,1:T(8,128)(2,1)S(1)}, u32[]{:S(2)}, u32[]{:S(2)}) %all-to-all-start) | async-done | bytes 1835040 | tf_op jit(solution)/shard_map/all_to_all | solution.py:213
  93.9 3.1 maximum_select_fusion.1
  97.0 3.3 fusion.25
  101.1 3.3 convolution_add_fusion.1
  104.4 2.1 concatenate.56
  107.7 2.9 collective-permute-start.4
  113.2 2.4 maximum_select_fusion
  115.7 4.0 %concatenate.59 = f32[1,1032,256]{2,1,0:T(8,128)} concatenate(f32[1,1024,256]{2,1,0:T(8,128)} %bitcast.116, f32[1,4,256]{2,1,0:T(4,128)S(1)} %concatenate.58, f32[1,4,256]{2,1,0:T(4,128)S(1)} %broadcast_in_dim.112), dimensions={1} | concatenate | bytes 2113536 | tf_op jit(solution)/shard_map/concatenate | solution.py:72
  121.1 34.6 %collective-permute-done.4 = f32[1032,256]{1,0:T(8,128)} collective-permute-done((f32[1032,256]{1,0:T(8,128)}, f32[1032,256]{1,0:T(8,128)}, u32[]{:S(2)}, u32[]{:S(2)}) %collective-permute-start.4) | collective-permute-done | bytes 1056800 | tf_op jit(solution)/shard_map/ppermute | solution.py:151
  156.9 60.7 %collective-permute-done.2 = f32[1032,256]{1,0:T(8,128)} collective-permute-done((f32[1032,256]{1,0:T(8,128)}, f32[1032,256]{1,0:T(8,128)}, u32[]{:S(2)}, u32[]{:S(2)}) %collective-permute-start.2) | collective-permute-done | bytes 1056800 | tf_op jit(solution)/shard_map/ppermute | solution.py:151
  217.6 2.2 pad_maximum_fusion
  222.9 2.4 multiply_reduce_fusion.1
  228.8 2.1 collective-permute-start.8
  235.0 2.9 fusion.49
  238.6 1.7 fusion.7
  240.4 81.9 %collective-permute-done.8 = f32[1032,256]{1,0:T(8,128)S(1)} collective-permute-done((f32[1032,256]{1,0:T(8,128)S(1)}, f32[1032,256]{1,0:T(8,128)S(1)}, u32[]{:S(2)}, u32[]{:S(2)}) %collective-permute-start.8) | collective-permute-done | bytes 1056800 | tf_op jit(solution)/shard_map/ppermute | solution.py:151
  324.9 2.4 multiply_reduce_fusion
  327.3 1.8 fusion.23
  332.3 2.3 fusion.13
  334.6 25.4 %all_to_all.35 = bf16[16,64,256]{2,1,0:T(8,128)(2,1)S(1)} all-to-all(bf16[16,64,256]{2,1,0:T(8,128)(2,1)S(1)} %bitcast.125), channel_id=1, replica_groups=mesh['sx'=4,'sy'=4,'tensor'=16] {'tensor'}, dimensions={0} | all-to-all | bytes 1048576 | tf_op jit(solution)/shard_map/all_to_all | solution.py:262
  (136 shorter events, 35.3 us)
Async XLA Ops:
  1.6 10.3 %copy-start.14 = (bf16[64,4]{0,1:T(4,128)(2,1)S(1)}, bf16[64,4]{0,1:T(4,128)(2,1)}, u32[]{:S(2)}) copy-start(bf16[64,4]{0,1:T(4,128)(2,1)} %param.12) | copy-start | bytes 1540
  1.6 10.3 %copy-start.15 = (bf16[64,4]{0,1:T(4,128)(2,1)S(1)}, bf16[64,4]{0,1:T(4,128)(2,1)}, u32[]{:S(2)}) copy-start(bf16[64,4]{0,1:T(4,128)(2,1)} %param.11) | copy-start | bytes 1540
  1.6 10.4 %copy-start.9 = (bf16[64,4096]{1,0:T(8,128)(2,1)S(1)}, bf16[64,4096]{1,0:T(8,128)(2,1)}, u32[]{:S(2)}) copy-start(bf16[64,4096]{1,0:T(8,128)(2,1)} %param.10) | copy-start | bytes 1572868
  1.6 10.5 %copy-start.10 = (bf16[64,4096]{1,0:T(8,128)(2,1)S(1)}, bf16[64,4096]{1,0:T(8,128)(2,1)}, u32[]{:S(2)}) copy-start(bf16[64,4096]{1,0:T(8,128)(2,1)} %param.9) | copy-start | bytes 1572868
  2.7 37.1 %all-to-all-start.1 = ((bf16[64,16,512]{2,0,1:T(8,128)(2,1)}), bf16[64,16,512]{2,0,1:T(8,128)(2,1)S(1)}, u32[]{:S(2)}, u32[]{:S(2)}) async-start(bf16[64,16,512]{2,0,1:T(8,128)(2,1)} %bitcast.8), calls=%async_computation.1 | async-start | bytes 2097152 | tf_op jit(solution)/shard_map/all_to_all | solution.py:218
  14.3 29.2 %copy-start.12 = (s32[1024]{0:T(1024)S(1)}, s32[1024]{0:T(1024)}, u32[]{:S(2)}) copy-start(s32[1024]{0:T(1024)} %param.13) | copy-start | bytes 12292
  39.9 47.2 %all-to-all-start = ((bf16[64,16,896]{2,0,1:T(8,128)(2,1)}), bf16[64,16,896]{2,0,1:T(8,128)(2,1)S(1)}, u32[]{:S(2)}, u32[]{:S(2)}) async-start(bf16[64,16,896]{2,0,1:T(8,128)(2,1)} %fusion.6), calls=%async_computation | async-start | bytes 3670016 | tf_op jit(solution)/shard_map/all_to_all | solution.py:213
  46.5 66.7 %collective-permute-start = (bf16[1024,512]{1,0:T(8,128)(2,1)S(1)}, bf16[1024,512]{1,0:T(8,128)(2,1)}, u32[]{:S(2)}, u32[]{:S(2)}) collective-permute-start(bf16[1024,512]{1,0:T(8,128)(2,1)S(1)} %bitcast.113), channel_id=1, source_target_pairs={{0,1},{1,0},{2,3},{3,2},{4,5},{5,4},{6,7},{7,6},{8,9},{9,8},{10,11... | collective-permute-start | bytes 3145736 | tf_op jit(solution)/shard_map/ppermute | solution.py:201
  87.1 6.7 %copy-start.2 = (bf16[64,16,896]{2,0,1:T(8,128)(2,1)}, bf16[64,16,896]{2,0,1:T(8,128)(2,1)S(1)}, u32[]{:S(2)}) copy-start(bf16[64,16,896]{2,0,1:T(8,128)(2,1)S(1)} %all-to-all-done) | copy-start | bytes 5505028
  88.3 5.6 %collective-permute-start.1 = (bf16[1024,512]{1,0:T(8,128)(2,1)}, bf16[1024,512]{1,0:T(8,128)(2,1)}, u32[]{:S(2)}, u32[]{:S(2)}) collective-permute-start(bf16[1024,512]{1,0:T(8,128)(2,1)} %slice.145), channel_id=1, source_target_pairs={{0,1},{1,0},{2,3},{3,2},{4,5},{5,4},{6,7},{7,6},{8,9},{9,8},{10,11... | collective-permute-start | bytes 3145736 | tf_op jit(solution)/shard_map/ppermute | solution.py:201
  96.9 4.1 %copy-start = (bf16[1024,1024]{1,0:T(8,128)(2,1)}, bf16[1024,1024]{1,0:T(8,128)(2,1)S(1)}, u32[]{:S(2)}) copy-start(bf16[1024,1024]{1,0:T(8,128)(2,1)S(1)} %maximum_select_fusion.1) | copy-start | bytes 6291460
  107.7 48.0 %collective-permute-start.4 = (f32[1032,256]{1,0:T(8,128)}, f32[1032,256]{1,0:T(8,128)}, u32[]{:S(2)}, u32[]{:S(2)}) collective-permute-start(f32[1032,256]{1,0:T(8,128)} %and_select_fusion.1), channel_id=1, source_target_pairs={{0,16},{16,32},{32,48},{48,64},{64,80},{80,96},{96,112},{112,128},... | collective-permute-start | bytes 3170312 | tf_op jit(solution)/shard_map/ppermute | solution.py:151
  110.6 46.3 %collective-permute-start.3 = (f32[1032,256]{1,0:T(8,128)}, f32[1032,256]{1,0:T(8,128)}, u32[]{:S(2)}, u32[]{:S(2)}) collective-permute-start(f32[1032,256]{1,0:T(8,128)} %and_select_fusion.1), channel_id=1, source_target_pairs={{0,32},{16,48},{32,64},{48,80},{64,96},{80,112},{96,128},{112,144}... | collective-permute-start | bytes 3170312 | tf_op jit(solution)/shard_map/ppermute | solution.py:151
  111.9 105.7 %collective-permute-start.2 = (f32[1032,256]{1,0:T(8,128)}, f32[1032,256]{1,0:T(8,128)}, u32[]{:S(2)}, u32[]{:S(2)}) collective-permute-start(f32[1032,256]{1,0:T(8,128)} %and_select_fusion.1), channel_id=1, source_target_pairs={{0,48},{16,64},{32,80},{48,96},{64,112},{80,128},{96,144},{112,160... | collective-permute-start | bytes 3170312 | tf_op jit(solution)/shard_map/ppermute | solution.py:151
  225.2 9.7 %copy-start.1 = (bf16[1024,1024]{1,0:T(8,128)(2,1)S(1)}, bf16[1024,1024]{1,0:T(8,128)(2,1)}, u32[]{:S(2)}) copy-start(bf16[1024,1024]{1,0:T(8,128)(2,1)} %copy-done) | copy-start | bytes 6291460
  228.8 9.1 %copy-start.3 = (bf16[64,16,896]{2,0,1:T(8,128)(2,1)S(1)}, bf16[64,16,896]{2,0,1:T(8,128)(2,1)}, u32[]{:S(2)}) copy-start(bf16[64,16,896]{2,0,1:T(8,128)(2,1)} %copy-done.2) | copy-start | bytes 5505028
  228.8 93.4 %collective-permute-start.8 = (f32[1032,256]{1,0:T(8,128)S(1)}, f32[1032,256]{1,0:T(8,128)S(1)}, u32[]{:S(2)}, u32[]{:S(2)}) collective-permute-start(f32[1032,256]{1,0:T(8,128)S(1)} %and_select_fusion), channel_id=1, source_target_pairs={{0,16},{16,32},{32,48},{48,64},{64,80},{80,96},{96,112},{112,128},... | collective-permute-start | bytes 3170312 | tf_op jit(solution)/shard_map/ppermute | solution.py:151
  230.9 91.4 %collective-permute-start.7 = (f32[1032,256]{1,0:T(8,128)S(1)}, f32[1032,256]{1,0:T(8,128)S(1)}, u32[]{:S(2)}, u32[]{:S(2)}) collective-permute-start(f32[1032,256]{1,0:T(8,128)S(1)} %and_select_fusion), channel_id=1, source_target_pairs={{0,80},{16,96},{32,112},{48,128},{64,144},{80,160},{96,176},{112,1... | collective-permute-start | bytes 3170312 | tf_op jit(solution)/shard_map/ppermute | solution.py:151
  232.2 90.1 %collective-permute-start.6 = (f32[1032,256]{1,0:T(8,128)S(1)}, f32[1032,256]{1,0:T(8,128)S(1)}, u32[]{:S(2)}, u32[]{:S(2)}) collective-permute-start(f32[1032,256]{1,0:T(8,128)S(1)} %and_select_fusion), channel_id=1, source_target_pairs={{0,144},{16,160},{32,176},{48,192},{64,208},{80,224},{96,240},{1,1... | collective-permute-start | bytes 3170312 | tf_op jit(solution)/shard_map/ppermute | solution.py:151
  233.5 88.8 %collective-permute-start.5 = (f32[1032,256]{1,0:T(8,128)S(1)}, f32[1032,256]{1,0:T(8,128)S(1)}, u32[]{:S(2)}, u32[]{:S(2)}) collective-permute-start(f32[1032,256]{1,0:T(8,128)S(1)} %and_select_fusion), channel_id=1, source_target_pairs={{0,208},{16,224},{32,240},{1,209},{17,225},{33,241},{2,210},{18,22... | collective-permute-start | bytes 3170312 | tf_op jit(solution)/shard_map/ppermute | solution.py:151
  322.3 1.3 copy-start.5
  322.3 1.6 copy-start.6
  327.3 1.8 copy-start.7
  329.7 2.6 copy-start.8
  (3 other events, 3.2 us)

commit v13 on v10

--- a/solution.py
+++ b/solution.py
@@ -51,8 +51,8 @@
     return jnp.where((rows == row) & (lane < (3 if low is None else 4)), values, body)
 
 
-def pack_summary(key_all, value_all, gate_in, cumulative, segment_ids, key_scale):
-    head_dim = key_all.shape[1]
+def pack_summary(key_own, key_other, is_even, value_all, gate_in, cumulative, segment_ids, key_scale):
+    head_dim = key_own.shape[1] * 2
     column_count = value_all.shape[1]
     total_log = cumulative[-1]
     first_seg = segment_ids[0]
@@ -62,8 +62,16 @@
     )
     token_weight = key_scale * tail_weight
     weighted_values = value_all.astype(jnp.float32) * token_weight[:, None]
-    state = split_dot_left(key_all, weighted_values, (((0,), (0,)), ((), ())))
-    norm = split_dot_left(key_all, token_weight[:, None], (((0,), (0,)), ((), ())))[:, 0]
+    both = jnp.concatenate([weighted_values, token_weight[:, None]], axis=1)
+    own_rows = split_dot_left(key_own, both, (((0,), (0,)), ((), ())))
+    other_rows = split_dot_left(key_other, both, (((0,), (0,)), ((), ())))
+    rows_all = jnp.where(
+        is_even,
+        jnp.concatenate([own_rows, other_rows], axis=0),
+        jnp.concatenate([other_rows, own_rows], axis=0),
+    )
+    state = rows_all[:, :column_count]
+    norm = rows_all[:, column_count]
     decay = jnp.exp(total_log) * (last_seg == first_seg).astype(jnp.float32)
     norm_rows = head_dim // column_count
     rows = meta_row(head_dim, column_count) + 1
@@ -167,8 +175,7 @@
     is_even = lax.axis_index("tensor") % 2 == 0
     pairs = [(index, index ^ 1) for index in range(tensor_size)]
 
-    def joined(own):
-        other = lax.ppermute(own, "tensor", pairs)
+    def joined(own, other):
         return jnp.where(
             is_even, jnp.concatenate([own, other], axis=1), jnp.concatenate([other, own], axis=1)
         )
@@ -184,11 +191,13 @@
     first_all = first_all.reshape(-1, half + column_count + gate_lanes)
     value_all = first_all[:, half : half + column_count]
     gate_all = first_all[:, half + column_count : half + column_count + 2]
-    key_all = joined(first_all[:, :half])
+    key_own = first_all[:, :half]
+    key_other = lax.ppermute(key_own, "tensor", pairs)
+    key_all = joined(key_own, key_other)
     query_half = lax.all_to_all(
         halves_send(queries), "tensor", split_axis=1, concat_axis=0, tiled=True
     ).reshape(-1, half)
-    query_all = joined(query_half)
+    query_all = joined(query_half, lax.ppermute(query_half, "tensor", pairs))
     token_count = query_all.shape[0]
     gate_f = gate_all.reshape(token_count, 2).astype(jnp.float32)
     gate_in = gate_f[:, 0]
@@ -197,7 +206,9 @@
     first_seg = segment_ids[0]
     cumulative = jnp.cumsum(log_forget)
 
-    packed = pack_summary(key_all, value_all, gate_in, cumulative, segment_ids, key_scale)
+    packed = pack_summary(
+        key_own, key_other, is_even, value_all, gate_in, cumulative, segment_ids, key_scale
+    )
     in_packed, in_last = prefix_from_all(packed, head_dim, "sy", "sx")
     in_row = meta_row(head_dim, column_count)
     in_state = in_packed[:head_dim]

time: 203 us -> 204 us (level)
  matrix products: 18.7 us -> 24.1 us
  waiting for transfers between devices: 71.8 us -> 69.4 us
    dot_general x8, matrix products: 8.05 us -> 10.9 us  [one(): lax.dot_general(narrow.astype(jnp.bfloat16), part.astype(jnp.bfloat16), d...]
    dot_general x1, matrix products: 2.95 us -> 5.49 us  [on_device(): lax.dot_general(query_all, key_all, (((1,), (1,)), ((), ())), preferred_e...]
    all_gather x1, waiting for transfers between devices: 28.4 us -> 26 us  [prefix_from_all(): gathered = lax.all_gather(packed.astype(jnp.bfloat16), axes)]
    select_n x2 -> x1, other arithmetic: 4.78 us -> 2.44 us  [joined(): jnp.where(is_even, jnp.concatenate([own, other], axis=1), jnp.concatenate...]
  transfers between devices with their start and end apart: 4 -> 4, of which waited for: 3 -> 3; matrix products, arithmetic and copies ran while one was open for 6% -> 9% of each run, Pallas kernels for 0% -> 0%
where the time goes in v13:
time: 204 us; the launch traced here: 201 us
  waiting for transfers between devices  69.4 us (34%)
  blocking collectives  57.7 us (28%)
  matrix products  24.1 us (12%)
  between operations  18.8 us (9%)
  other arithmetic  11.6 us (6%)
  local copies, waits for them, and re-layouts  9.87 us (5%)
  starting transfers between devices  9.42 us (5%)
    all_to_all x1, waiting for transfers between devices, on_device(): lax.all_to_all(first_send, 'tensor', split_axis=1, concat_axis=0, tiled=T...  40.5 us
    all_to_all x1, blocking collectives, on_device(): lax.all_to_all(halves_send(queries), 'tensor', split_axis=1, concat_axis=...  32.8 us
    all_gather x1, waiting for transfers between devices, prefix_from_all(): gathered = lax.all_gather(packed.astype(jnp.bfloat16), axes)  26 us
    all_to_all x1, blocking collectives, on_device(): lax.all_to_all(hidden.reshape(tensor_size, row_count, column_count), 'ten...  24.9 us
    dot_general x8, matrix products, one(): lax.dot_general(narrow.astype(jnp.bfloat16), part.astype(jnp.bfloat16), d...  10.9 us
    all_to_all x1, starting transfers between devices, on_device(): lax.all_to_all(first_send, 'tensor', split_axis=1, concat_axis=0, tiled=T...  9.28 us
    dot_general x1, matrix products, on_device(): lax.dot_general(query_all, key_all, (((1,), (1,)), ((), ())), preferred_e...  5.49 us
    dot_general x1, matrix products, prefix_from_all(): state = jnp.einsum('s,src->rc', weight, gathered.astype(jnp.float32))  5.18 us
  transfers between devices with their start and end apart: 4, of which 3 were waited for; matrix products, arithmetic and copies ran while one was open for 9% of the time, Pallas kernels for 0%

profile of v13, /device:TPU:23, one launch (start us, length us, event | category | flops | bytes accessed | tf_op | source)
XLA Modules:
  0.0 200.8 jit_solution(18432045226097881558)
XLA Ops:
  7.4 1.1 copy.92
  8.5 1.4 broadcast_in_dim.72
  10.2 1.5 fusion.14
  11.7 9.3 %all-to-all-start = ((bf16[64,16,896]{2,0,1:T(8,128)(2,1)}), bf16[64,16,896]{2,0,1:T(8,128)(2,1)S(1)}, u32[]{:S(2)}, u32[]{:S(2)}) async-start(bf16[64,16,896]{2,0,1:T(8,128)(2,1)} %fusion.14), calls=%async_computation | async-start | bytes 3670016 | tf_op jit(solution)/shard_map/all_to_all | solution.py:190
  24.3 40.5 %all-to-all-done = bf16[64,16,896]{2,0,1:T(8,128)(2,1)S(1)} async-done(((bf16[64,16,896]{2,0,1:T(8,128)(2,1)}), bf16[64,16,896]{2,0,1:T(8,128)(2,1)S(1)}, u32[]{:S(2)}, u32[]{:S(2)}) %all-to-all-start) | async-done | bytes 1835040 | tf_op jit(solution)/shard_map/all_to_all | solution.py:190
  66.7 1.3 select_multiply_fusion
  71.0 0.8 fusion.36
  71.7 0.8 convolution_add_fusion.2
  72.5 2.0 fusion.55
  74.5 2.0 convolution_add_fusion.1
  77.2 1.1 select_convert_fusion
  78.9 32.8 %all_to_all.35 = bf16[64,16,512]{2,0,1:T(8,128)(2,1)S(1)} all-to-all(bf16[64,16,512]{2,0,1:T(8,128)(2,1)S(1)} %bitcast.105), channel_id=1, replica_groups=mesh['sx'=4,'sy'=4,'tensor'=16] {'tensor'}, dimensions={1} | all-to-all | bytes 2097152 | tf_op jit(solution)/shard_map/all_to_all | solution.py:197
  111.7 2.8 %collective-permute-done = bf16[1024,512]{1,0:T(8,128)(2,1)} collective-permute-done((bf16[1024,512]{1,0:T(8,128)(2,1)S(1)}, bf16[1024,512]{1,0:T(8,128)(2,1)}, u32[]{:S(2)}, u32[]{:S(2)}) %collective-permute-start) | collective-permute-done | bytes 1048608 | tf_op jit(solution)/shard_map/ppermute | solution.py:200
  114.5 2.4 %maximum_select_fusion = bf16[1024,1024]{1,0:T(8,128)(2,1)S(1)} fusion(bf16[1024,512]{1,0:T(8,128)(2,1)} %collective-permute-done, bf16[1024,512]{1,0:T(8,128)(2,1)S(1)} %bitcast.103, pred[]{:T(512)S(6)} %eq.86), kind=kLoop, calls=%fused_computation.14 | loop fusion | flops 9437184 | bytes 4194305 | tf_op jit(solution)/shard_map/jit(_where)/select_n | solution.py:179
  117.0 5.5 %fusion.61 = (f32[1024]{0:T(1024)S(1)}, f32[1024,1024]{0,1:T(8,128)S(1)}) fusion(bf16[1024,1024]{1,0:T(8,128)(2,1)S(1)} %maximum_select_fusion, bf16[1024,512]{1,0:T(8,128)(2,1)} %collective-permute-done.1, bf16[1024,512]{1,0:T(8,128)(2,1)S(1)} %copy-done.3, pred[]{:T(512)S(6)} %eq.86, f32[1024]{0:T(1024)S(1)} %get-tuple-element.6, ...), kind=kOutput, calls=%fused_computation.111 | convolution fusion | flops 2167405568 | bytes 8404993 | tf_op jit(solution)/shard_map/dot_general | solution.py:224
  122.5 0.7 fusion.5
  123.2 1.8 fusion.16
  125.0 26.0 %all-gather.2.cloned.1.call-done = bf16[16,1032,256]{2,1,0:T(8,128)(2,1)} async-done(((bf16[1,1032,256]{2,1,0:T(8,128)(2,1)}), bf16[16,1032,256]{2,1,0:T(8,128)(2,1)}) %all-gather.2.cloned.1.call-update) | async-done | bytes 8454160 | tf_op jit(solution)/shard_map/all_gather | solution.py:142
  151.1 0.8 slice.107
  152.5 5.2 %fusion = f32[1,1032,256]{2,0,1:T(1,128)S(1)} fusion(bf16[16,1032,256]{2,1,0:T(8,128)(2,1)} %all-gather.2.cloned.1.call-done, bf16[1]{0:T(256)(128)(2,1)} %constant.187, bf16[15]{0:T(256)(128)(2,1)S(1)} %slice.96, s32[]{:T(128)S(6)} %add.86), kind=kOutput, calls=%fused_computation | convolution fusion | flops 8454240 | bytes 9510948 | tf_op jit(solution)/shard_map/s,src->rc/dot_general | solution.py:147
  157.7 1.7 fusion.31
  162.7 2.3 %fusion.22 = bf16[1024,256]{1,0:T(8,128)(2,1)S(1)} fusion(f32[1024,256]{1,0:T(8,128)} %fusion.16, f32[1024,256]{1,0:T(8,128)} %fusion.31, bf16[1024,1024]{1,0:T(8,128)(2,1)S(1)} %maximum_select_fusion, f32[1032,256]{1,0:T(8,128)S(1)} %bitcast.114, f32[1024]{0:T(1024)S(1)} %get-tuple-element.7, f32[1024]{0:T(1024)S(1)} %get-tuple-element.8), kind=kOutput, calls=%fused_computation.41 | convolution fusion | flops 538705920 | bytes 5775360 | tf_op jit(solution)/shard_map/dot_general | solution.py:31
  165.0 24.9 %all_to_all.36 = bf16[16,64,256]{2,1,0:T(8,128)(2,1)S(1)} all-to-all(bf16[16,64,256]{2,1,0:T(8,128)(2,1)S(1)} %bitcast.117), channel_id=1, replica_groups=mesh['sx'=4,'sy'=4,'tensor'=16] {'tensor'}, dimensions={0} | all-to-all | bytes 1048576 | tf_op jit(solution)/shard_map/all_to_all | solution.py:243
  192.8 1.2 fusion.30
  (86 shorter events, 12.2 us)
Async XLA Ops:
  11.7 9.3 %copy-start.6 = (s32[1024]{0:T(1024)S(1)}, s32[1024]{0:T(1024)}, u32[]{:S(2)}) copy-start(s32[1024]{0:T(1024)} %param.13) | copy-start | bytes 12292
  11.7 53.1 %all-to-all-start = ((bf16[64,16,896]{2,0,1:T(8,128)(2,1)}), bf16[64,16,896]{2,0,1:T(8,128)(2,1)S(1)}, u32[]{:S(2)}, u32[]{:S(2)}) async-start(bf16[64,16,896]{2,0,1:T(8,128)(2,1)} %fusion.14), calls=%async_computation | async-start | bytes 3670016 | tf_op jit(solution)/shard_map/all_to_all | solution.py:190
  21.0 130.1 %all-gather.2.cloned.1.call-start = ((), (), s32[]{:S(2)}) async-start(), calls=%async_computation.3 | async-start | bytes 8982528 | tf_op jit(solution)/shard_map/all_gather | solution.py:142
  64.8 6.9 %copy-start = (bf16[64,16,896]{2,0,1:T(8,128)(2,1)}, bf16[64,16,896]{2,0,1:T(8,128)(2,1)S(1)}, u32[]{:S(2)}) copy-start(bf16[64,16,896]{2,0,1:T(8,128)(2,1)S(1)} %all-to-all-done) | copy-start | bytes 5505028
  64.9 6.9 %copy-start.2 = (bf16[1024,512]{1,0:T(8,128)(2,1)}, bf16[1024,512]{1,0:T(8,128)(2,1)S(1)}, u32[]{:S(2)}) copy-start(bf16[1024,512]{1,0:T(8,128)(2,1)S(1)} %slice.103) | copy-start | bytes 3145732
  64.9 7.6 %collective-permute-start.1 = (bf16[1024,512]{1,0:T(8,128)(2,1)S(1)}, bf16[1024,512]{1,0:T(8,128)(2,1)}, u32[]{:S(2)}, u32[]{:S(2)}) collective-permute-start(bf16[1024,512]{1,0:T(8,128)(2,1)S(1)} %slice.103), channel_id=1, source_target_pairs={{0,1},{1,0},{2,3},{3,2},{4,5},{5,4},{6,7},{7,6},{8,9},{9,8},{10,11... | collective-permute-start | bytes 3145736 | tf_op jit(solution)/shard_map/ppermute | solution.py:195
  76.7 1.6 copy-start.4
  111.7 2.8 %collective-permute-start = (bf16[1024,512]{1,0:T(8,128)(2,1)S(1)}, bf16[1024,512]{1,0:T(8,128)(2,1)}, u32[]{:S(2)}, u32[]{:S(2)}) collective-permute-start(bf16[1024,512]{1,0:T(8,128)(2,1)S(1)} %bitcast.102), channel_id=1, source_target_pairs={{0,1},{1,0},{2,3},{3,2},{4,5},{5,4},{6,7},{7,6},{8,9},{9,8},{10,11... | collective-permute-start | bytes 3145736 | tf_op jit(solution)/shard_map/ppermute | solution.py:200
  111.7 5.2 %copy-start.3 = (bf16[1024,512]{1,0:T(8,128)(2,1)S(1)}, bf16[1024,512]{1,0:T(8,128)(2,1)}, u32[]{:S(2)}) copy-start(bf16[1024,512]{1,0:T(8,128)(2,1)} %copy-done.2) | copy-start | bytes 3145732
  117.0 5.5 %copy-start.1 = (bf16[64,16,896]{2,0,1:T(8,128)(2,1)S(1)}, bf16[64,16,896]{2,0,1:T(8,128)(2,1)}, u32[]{:S(2)}) copy-start(bf16[64,16,896]{2,0,1:T(8,128)(2,1)} %copy-done) | copy-start | bytes 5505028
  191.8 1.0 copy-start.5
  191.8 1.0 copy-start.7
Sparse Core Ops, SparseCore 0:
  78.4 72.6 all-gather.1

commit v14 on v10

--- a/solution.py
+++ b/solution.py
@@ -174,16 +174,23 @@
         )
 
     value_send = values.reshape(row_count, tensor_size, column_count)
-    gate_lanes = 128
-    gate_send = jnp.pad(
-        spread_heads(jnp.stack([input_gate, forget_gate], axis=2), 2),
-        ((0, 0), (0, 0), (0, gate_lanes - 2)),
-    )
-    first_send = jnp.concatenate([halves_send(key_rows), value_send, gate_send], axis=2)
+    gate_rows = 8
+    lanes = half + column_count
+    gate_pair = jnp.stack([input_gate, forget_gate], axis=0)
+    gate_block = jnp.broadcast_to(
+        jnp.transpose(gate_pair, (2, 0, 1))[:, None], (head_count, group_size, 2, row_count)
+    ).reshape(1, tensor_size, 2 * row_count)
+    gate_send = jnp.pad(gate_block, ((0, gate_rows - 1), (0, 0), (0, lanes - 2 * row_count)))
+    first_send = jnp.concatenate(
+        [jnp.concatenate([halves_send(key_rows), value_send], axis=2), gate_send], axis=0
+    )
     first_all = lax.all_to_all(first_send, "tensor", split_axis=1, concat_axis=0, tiled=True)
-    first_all = first_all.reshape(-1, half + column_count + gate_lanes)
-    value_all = first_all[:, half : half + column_count]
-    gate_all = first_all[:, half + column_count : half + column_count + 2]
+    first_all = first_all.reshape(tensor_size, row_count + gate_rows, lanes)
+    gate_all = jnp.transpose(
+        first_all[:, row_count, : 2 * row_count].reshape(tensor_size, 2, row_count), (0, 2, 1)
+    ).reshape(tensor_size * row_count, 2)
+    first_all = first_all[:, :row_count].reshape(tensor_size * row_count, lanes)
+    value_all = first_all[:, half:]
     key_all = joined(first_all[:, :half])
     query_half = lax.all_to_all(
         halves_send(queries), "tensor", split_axis=1, concat_axis=0, tiled=True

time: 203 us -> 201 us (level)
  no operation moved by 1% of the time
where the time goes in v14:
time: 201 us; the launch traced here: 198 us
  waiting for transfers between devices  70.7 us (35%)
  blocking collectives  57.6 us (29%)
  between operations  18.8 us (9%)
  matrix products  18.7 us (9%)
  other arithmetic  12.9 us (6%)
  local copies, waits for them, and re-layouts  9.56 us (5%)
  starting transfers between devices  9.42 us (5%)
    all_to_all x1, waiting for transfers between devices, on_device(): lax.all_to_all(first_send, 'tensor', split_axis=1, concat_axis=0, tiled=T...  39.3 us
    all_to_all x1, blocking collectives, on_device(): lax.all_to_all(halves_send(queries), 'tensor', split_axis=1, concat_axis=...  32.7 us
    all_gather x1, waiting for transfers between devices, prefix_from_all(): gathered = lax.all_gather(packed.astype(jnp.bfloat16), axes)  28.5 us
    all_to_all x1, blocking collectives, on_device(): lax.all_to_all(hidden.reshape(tensor_size, row_count, column_count), 'ten...  24.9 us
    all_to_all x1, starting transfers between devices, on_device(): lax.all_to_all(first_send, 'tensor', split_axis=1, concat_axis=0, tiled=T...  9.28 us
    dot_general x8, matrix products, one(): lax.dot_general(narrow.astype(jnp.bfloat16), part.astype(jnp.bfloat16), d...  8.06 us
    dot_general x1, matrix products, prefix_from_all(): state = jnp.einsum('s,src->rc', weight, gathered.astype(jnp.float32))  5.18 us
    select_n x2, other arithmetic, joined(): jnp.where(is_even, jnp.concatenate([own, other], axis=1), jnp.concatenate...  4.7 us
  transfers between devices with their start and end apart: 4, of which 3 were waited for; matrix products, arithmetic and copies ran while one was open for 6% of the time, Pallas kernels for 0%

profile of v14, /device:TPU:23, one launch (start us, length us, event | category | flops | bytes accessed | tf_op | source)
XLA Modules:
  0.0 197.7 jit_solution(10309274792187816579)
XLA Ops:
  6.5 0.7 maximum_bitcast_fusion
  7.3 1.1 copy.68
  8.4 1.4 broadcast_in_dim.71
  10.1 1.4 fusion.8
  11.5 9.3 %all-to-all-start = ((bf16[72,16,768]{2,0,1:T(8,128)(2,1)}), bf16[72,16,768]{2,0,1:T(8,128)(2,1)S(1)}, u32[]{:S(2)}, u32[]{:S(2)}) async-start(bf16[72,16,768]{2,0,1:T(8,128)(2,1)} %fusion.8), calls=%async_computation | async-start | bytes 3538944 | tf_op jit(solution)/shard_map/all_to_all | solution.py:187
  23.9 39.3 %all-to-all-done = bf16[72,16,768]{2,0,1:T(8,128)(2,1)S(1)} async-done(((bf16[72,16,768]{2,0,1:T(8,128)(2,1)}), bf16[72,16,768]{2,0,1:T(8,128)(2,1)S(1)}, u32[]{:S(2)}, u32[]{:S(2)}) %all-to-all-start) | async-done | bytes 1769504 | tf_op jit(solution)/shard_map/all_to_all | solution.py:187
  65.7 1.2 fusion.37
  68.8 2.3 %maximum_select_fusion.1 = bf16[1024,1024]{1,0:T(8,128)(2,1)S(1)} fusion(bf16[1024,512]{1,0:T(8,128)(2,1)} %collective-permute-done.1, bf16[1024,512]{1,0:T(8,128)(2,1)S(1)} %slice.100, pred[]{:T(512)S(6)} %eq.86), kind=kLoop, calls=%fused_computation.13 | loop fusion | flops 9437184 | bytes 4194305 | tf_op jit(solution)/shard_map/jit(_where)/select_n | solution.py:172
  71.1 1.0 fusion.28
  72.1 1.0 fusion.12
  74.0 1.1 select_convert_fusion
  75.8 32.7 %all_to_all.35 = bf16[64,16,512]{2,0,1:T(8,128)(2,1)S(1)} all-to-all(bf16[64,16,512]{2,0,1:T(8,128)(2,1)S(1)} %bitcast.102), channel_id=1, replica_groups=mesh['sx'=4,'sy'=4,'tensor'=16] {'tensor'}, dimensions={1} | all-to-all | bytes 2097152 | tf_op jit(solution)/shard_map/all_to_all | solution.py:195
  108.5 2.8 %collective-permute-done = bf16[1024,512]{1,0:T(8,128)(2,1)} collective-permute-done((bf16[1024,512]{1,0:T(8,128)(2,1)S(1)}, bf16[1024,512]{1,0:T(8,128)(2,1)}, u32[]{:S(2)}, u32[]{:S(2)}) %collective-permute-start) | collective-permute-done | bytes 1048608 | tf_op jit(solution)/shard_map/ppermute | solution.py:171
  111.3 2.4 %maximum_select_fusion = bf16[1024,1024]{1,0:T(8,128)(2,1)S(1)} fusion(bf16[1024,512]{1,0:T(8,128)(2,1)} %collective-permute-done, bf16[1024,512]{1,0:T(8,128)(2,1)S(1)} %bitcast.100, pred[]{:T(512)S(6)} %eq.86), kind=kLoop, calls=%fused_computation.12 | loop fusion | flops 9437184 | bytes 4194305 | tf_op jit(solution)/shard_map/jit(_where)/select_n | solution.py:172
  113.8 2.9 %fusion.50 = (f32[1024]{0:T(1024)S(1)}, f32[1024,1024]{0,1:T(8,128)S(1)}) fusion(bf16[1024,1024]{1,0:T(8,128)(2,1)S(1)} %maximum_select_fusion, bf16[1024,1024]{1,0:T(8,128)(2,1)S(1)} %copy-done.1, f32[1024]{0:T(1024)S(1)} %bitcast.123, f32[1024]{0:T(1024)S(1)} %add_bitcast_fusion, s32[1024]{0:T(1024)S(1)} %copy-done.6), kind=kOutput, calls=%fused_computation.95 | convolution fusion | flops 2157968384 | bytes 8404992 | tf_op jit(solution)/shard_map/dot_general | solution.py:220
  116.7 0.7 fusion.5
  117.5 1.8 fusion.9
  119.3 28.5 %all-gather.2.cloned.1.call-done = bf16[16,1032,256]{2,1,0:T(8,128)(2,1)} async-done(((bf16[1,1032,256]{2,1,0:T(8,128)(2,1)}), bf16[16,1032,256]{2,1,0:T(8,128)(2,1)}) %all-gather.2.cloned.1.call-update) | async-done | bytes 8454160 | tf_op jit(solution)/shard_map/all_gather | solution.py:134
  147.9 0.8 slice.102
  149.3 5.2 %fusion = f32[1,1032,256]{2,0,1:T(1,128)S(1)} fusion(bf16[16,1032,256]{2,1,0:T(8,128)(2,1)} %all-gather.2.cloned.1.call-done, bf16[1]{0:T(256)(128)(2,1)} %constant.157, bf16[15]{0:T(256)(128)(2,1)S(1)} %slice.92, s32[]{:T(128)S(6)} %add.87), kind=kOutput, calls=%fused_computation | convolution fusion | flops 8454240 | bytes 9510948 | tf_op jit(solution)/shard_map/s,src->rc/dot_general | solution.py:139
  154.5 1.7 fusion.26
  159.5 2.3 %fusion.16 = bf16[1024,256]{1,0:T(8,128)(2,1)S(1)} fusion(f32[1024,256]{1,0:T(8,128)} %fusion.9, f32[1024,256]{1,0:T(8,128)} %fusion.26, bf16[1024,1024]{1,0:T(8,128)(2,1)S(1)} %maximum_select_fusion, f32[1032,256]{1,0:T(8,128)S(1)} %bitcast.111, f32[1024]{0:T(1024)S(1)} %get-tuple-element.5, f32[1024]{0:T(1024)S(1)} %get-tuple-element.6), kind=kOutput, calls=%fused_computation.32 | convolution fusion | flops 538705920 | bytes 5775360 | tf_op jit(solution)/shard_map/dot_general | solution.py:31
  161.8 24.9 %all_to_all.36 = bf16[16,64,256]{2,1,0:T(8,128)(2,1)S(1)} all-to-all(bf16[16,64,256]{2,1,0:T(8,128)(2,1)S(1)} %bitcast.113), channel_id=1, replica_groups=mesh['sx'=4,'sy'=4,'tensor'=16] {'tensor'}, dimensions={0} | all-to-all | bytes 1048576 | tf_op jit(solution)/shard_map/all_to_all | solution.py:239
  189.7 1.2 fusion.25
  (91 shorter events, 11.2 us)
Async XLA Ops:
  11.5 9.3 %copy-start.6 = (s32[1024]{0:T(1024)S(1)}, s32[1024]{0:T(1024)}, u32[]{:S(2)}) copy-start(s32[1024]{0:T(1024)} %param.13) | copy-start | bytes 12292
  11.5 51.8 %all-to-all-start = ((bf16[72,16,768]{2,0,1:T(8,128)(2,1)}), bf16[72,16,768]{2,0,1:T(8,128)(2,1)S(1)}, u32[]{:S(2)}, u32[]{:S(2)}) async-start(bf16[72,16,768]{2,0,1:T(8,128)(2,1)} %fusion.8), calls=%async_computation | async-start | bytes 3538944 | tf_op jit(solution)/shard_map/all_to_all | solution.py:187
  20.8 127.1 %all-gather.2.cloned.1.call-start = ((), (), s32[]{:S(2)}) async-start(), calls=%async_computation.3 | async-start | bytes 8982528 | tf_op jit(solution)/shard_map/all_gather | solution.py:134
  63.4 8.7 %copy-start.2 = (bf16[16,64,768]{2,1,0:T(8,128)(2,1)}, bf16[16,64,768]{2,1,0:T(8,128)(2,1)S(1)}, u32[]{:S(2)}) copy-start(bf16[16,64,768]{2,1,0:T(8,128)(2,1)S(1)} %slice.99) | copy-start | bytes 4718596
  63.5 5.2 %collective-permute-start.1 = (bf16[1024,512]{1,0:T(8,128)(2,1)S(1)}, bf16[1024,512]{1,0:T(8,128)(2,1)}, u32[]{:S(2)}, u32[]{:S(2)}) collective-permute-start(bf16[1024,512]{1,0:T(8,128)(2,1)S(1)} %slice.100), channel_id=1, source_target_pairs={{0,1},{1,0},{2,3},{3,2},{4,5},{5,4},{6,7},{7,6},{8,9},{9,8},{10,11... | collective-permute-start | bytes 3145736 | tf_op jit(solution)/shard_map/ppermute | solution.py:171
  71.1 2.4 %copy-start = (bf16[1024,1024]{1,0:T(8,128)(2,1)}, bf16[1024,1024]{1,0:T(8,128)(2,1)S(1)}, u32[]{:S(2)}) copy-start(bf16[1024,1024]{1,0:T(8,128)(2,1)S(1)} %maximum_select_fusion.1) | copy-start | bytes 6291460
  73.4 1.7 copy-start.4
  108.5 2.8 %collective-permute-start = (bf16[1024,512]{1,0:T(8,128)(2,1)S(1)}, bf16[1024,512]{1,0:T(8,128)(2,1)}, u32[]{:S(2)}, u32[]{:S(2)}) collective-permute-start(bf16[1024,512]{1,0:T(8,128)(2,1)S(1)} %bitcast.99), channel_id=1, source_target_pairs={{0,1},{1,0},{2,3},{3,2},{4,5},{5,4},{6,7},{7,6},{8,9},{9,8},{10,11... | collective-permute-start | bytes 3145736 | tf_op jit(solution)/shard_map/ppermute | solution.py:171
  108.5 5.2 %copy-start.1 = (bf16[1024,1024]{1,0:T(8,128)(2,1)S(1)}, bf16[1024,1024]{1,0:T(8,128)(2,1)}, u32[]{:S(2)}) copy-start(bf16[1024,1024]{1,0:T(8,128)(2,1)} %copy-done) | copy-start | bytes 6291460
  113.8 3.0 %copy-start.3 = (bf16[16,64,768]{2,1,0:T(8,128)(2,1)S(1)}, bf16[16,64,768]{2,1,0:T(8,128)(2,1)}, u32[]{:S(2)}) copy-start(bf16[16,64,768]{2,1,0:T(8,128)(2,1)} %copy-done.2) | copy-start | bytes 4718596
  188.6 1.0 copy-start.5
  188.6 1.0 copy-start.7
Sparse Core Ops, SparseCore 0:
  75.2 72.5 all-gather.1

commit v15 on v14

--- a/solution.py
+++ b/solution.py
@@ -63,7 +63,7 @@
     token_weight = key_scale * tail_weight
     weighted_values = value_all.astype(jnp.float32) * token_weight[:, None]
     state = split_dot_left(key_all, weighted_values, (((0,), (0,)), ((), ())))
-    norm = split_dot_left(key_all, token_weight[:, None], (((0,), (0,)), ((), ())))[:, 0]
+    norm = jnp.sum(key_all.astype(jnp.float32) * token_weight[:, None], axis=0)
     decay = jnp.exp(total_log) * (last_seg == first_seg).astype(jnp.float32)
     norm_rows = head_dim // column_count
     rows = meta_row(head_dim, column_count) + 1

time: 201 us -> 204 us (1.015)
  matrix products: 18.7 us -> 24 us
  waiting for transfers between devices: 70.7 us -> 68 us
    dot_general x8 -> x6, matrix products: 8.06 us -> 10.8 us  [one(): lax.dot_general(narrow.astype(jnp.bfloat16), part.astype(jnp.bfloat16), d...]
    all_gather x1, waiting for transfers between devices: 28.5 us -> 25.9 us  [prefix_from_all(): gathered = lax.all_gather(packed.astype(jnp.bfloat16), axes)]
    reduce_sum x0 -> x1, other arithmetic: none -> 2.64 us  [pack_summary(): norm = jnp.sum(key_all.astype(jnp.float32) * token_weight[:, None], axis=0)]
    dot_general x1, matrix products: 2.94 us -> 5.47 us  [on_device(): lax.dot_general(query_all, key_all, (((1,), (1,)), ((), ())), preferred_e...]
    select_n x2 -> x1, other arithmetic: 4.7 us -> 2.52 us  [joined(): jnp.where(is_even, jnp.concatenate([own, other], axis=1), jnp.concatenate...]
  transfers between devices with their start and end apart: 4 -> 4, of which waited for: 3 -> 3; matrix products, arithmetic and copies ran while one was open for 6% -> 7% of each run, Pallas kernels for 0% -> 0%
where the time goes in v15:
time: 204 us; the launch traced here: 201 us
  waiting for transfers between devices  68 us (33%)
  blocking collectives  57.6 us (28%)
  matrix products  24 us (12%)
  between operations  18.8 us (9%)
  other arithmetic  13.3 us (7%)
  local copies, waits for them, and re-layouts  9.55 us (5%)
  starting transfers between devices  9.42 us (5%)
    all_to_all x1, waiting for transfers between devices, on_device(): lax.all_to_all(first_send, 'tensor', split_axis=1, concat_axis=0, tiled=T...  39.3 us
    all_to_all x1, blocking collectives, on_device(): lax.all_to_all(halves_send(queries), 'tensor', split_axis=1, concat_axis=...  32.7 us
    all_gather x1, waiting for transfers between devices, prefix_from_all(): gathered = lax.all_gather(packed.astype(jnp.bfloat16), axes)  25.9 us
    all_to_all x1, blocking collectives, on_device(): lax.all_to_all(hidden.reshape(tensor_size, row_count, column_count), 'ten...  24.9 us
    dot_general x6, matrix products, one(): lax.dot_general(narrow.astype(jnp.bfloat16), part.astype(jnp.bfloat16), d...  10.8 us
    all_to_all x1, starting transfers between devices, on_device(): lax.all_to_all(first_send, 'tensor', split_axis=1, concat_axis=0, tiled=T...  9.28 us
    dot_general x1, matrix products, on_device(): lax.dot_general(query_all, key_all, (((1,), (1,)), ((), ())), preferred_e...  5.47 us
    dot_general x1, matrix products, prefix_from_all(): state = jnp.einsum('s,src->rc', weight, gathered.astype(jnp.float32))  5.18 us
  transfers between devices with their start and end apart: 4, of which 3 were waited for; matrix products, arithmetic and copies ran while one was open for 7% of the time, Pallas kernels for 0%

profile of v15, /device:TPU:23, one launch (start us, length us, event | category | flops | bytes accessed | tf_op | source)
XLA Modules:
  0.0 200.6 jit_solution(7901449364094395031)
XLA Ops:
  6.5 0.7 maximum_bitcast_fusion
  7.3 1.1 copy.68
  8.4 1.4 broadcast_in_dim.71
  10.1 1.4 fusion.8
  11.5 9.3 %all-to-all-start = ((bf16[72,16,768]{2,0,1:T(8,128)(2,1)}), bf16[72,16,768]{2,0,1:T(8,128)(2,1)S(1)}, u32[]{:S(2)}, u32[]{:S(2)}) async-start(bf16[72,16,768]{2,0,1:T(8,128)(2,1)} %fusion.8), calls=%async_computation | async-start | bytes 3538944 | tf_op jit(solution)/shard_map/all_to_all | solution.py:187
  23.9 39.3 %all-to-all-done = bf16[72,16,768]{2,0,1:T(8,128)(2,1)S(1)} async-done(((bf16[72,16,768]{2,0,1:T(8,128)(2,1)}), bf16[72,16,768]{2,0,1:T(8,128)(2,1)S(1)}, u32[]{:S(2)}, u32[]{:S(2)}) %all-to-all-start) | async-done | bytes 1769504 | tf_op jit(solution)/shard_map/all_to_all | solution.py:187
  67.5 1.2 select_multiply_fusion
  68.8 2.6 %multiply_reduce_fusion = bf16[1024]{0:T(1024)(128)(2,1)S(1)} fusion(f32[1024]{0:T(1024)S(1)} %select_multiply_fusion, bf16[1024,512]{1,0:T(8,128)(2,1)S(1)} %slice.100, bf16[1024,512]{1,0:T(8,128)(2,1)} %collective-permute-done.1, pred[]{:T(512)S(6)} %eq.86), kind=kLoop, calls=%fused_computation.5 | loop fusion | flops 12581888 | bytes 2103297 | tf_op jit(solution)/shard_map/reduce_sum | solution.py:66
  71.4 2.7 %fusion.28 = f32[1024,256]{1,0:T(8,128)S(1)} fusion(f32[1024]{0:T(1024)S(1)} %select_multiply_fusion, bf16[1024,768]{1,0:T(8,128)(2,1)S(1)} %bitcast.84, bf16[1024,512]{1,0:T(8,128)(2,1)} %collective-permute-done.1, bf16[1024,512]{1,0:T(8,128)(2,1)S(1)} %slice.100, pred[]{:T(512)S(6)} %eq.86), kind=kOutput, calls=%fused_computation.47 | convolution fusion | flops 547618816 | bytes 3674113 | tf_op jit(solution)/shard_map/dot_general | solution.py:31
  74.2 2.7 %fusion.12 = bf16[1,1024,256]{2,1,0:T(8,128)(2,1)S(1)} fusion(f32[1024,256]{1,0:T(8,128)S(1)} %fusion.28, f32[1024]{0:T(1024)S(1)} %select_multiply_fusion, bf16[1024,768]{1,0:T(8,128)(2,1)S(1)} %bitcast.85, bf16[1024,512]{1,0:T(8,128)(2,1)} %collective-permute-done.1, bf16[1024,512]{1,0:T(8,128)(2,1)S(1)} %slice.100, pred[]{:T(512)S(6)} %eq.86), kind=kOutput, calls=%fused_computation.25 | convolution fusion | flops 547880960 | bytes 4198401 | tf_op jit(solution)/shard_map/dot_general | solution.py:31
  77.1 1.1 select_convert_fusion
  78.8 32.7 %all_to_all.35 = bf16[64,16,512]{2,0,1:T(8,128)(2,1)S(1)} all-to-all(bf16[64,16,512]{2,0,1:T(8,128)(2,1)S(1)} %bitcast.93), channel_id=1, replica_groups=mesh['sx'=4,'sy'=4,'tensor'=16] {'tensor'}, dimensions={1} | all-to-all | bytes 2097152 | tf_op jit(solution)/shard_map/all_to_all | solution.py:195
  111.6 2.8 %collective-permute-done = bf16[1024,512]{1,0:T(8,128)(2,1)} collective-permute-done((bf16[1024,512]{1,0:T(8,128)(2,1)S(1)}, bf16[1024,512]{1,0:T(8,128)(2,1)}, u32[]{:S(2)}, u32[]{:S(2)}) %collective-permute-start) | collective-permute-done | bytes 1048608 | tf_op jit(solution)/shard_map/ppermute | solution.py:171
  114.4 2.5 %maximum_select_fusion = bf16[1024,1024]{1,0:T(8,128)(2,1)S(1)} fusion(bf16[1024,512]{1,0:T(8,128)(2,1)} %collective-permute-done, bf16[1024,512]{1,0:T(8,128)(2,1)S(1)} %bitcast.91, pred[]{:T(512)S(6)} %eq.86), kind=kLoop, calls=%fused_computation.13 | loop fusion | flops 9437184 | bytes 4194305 | tf_op jit(solution)/shard_map/jit(_where)/select_n | solution.py:172
  116.9 5.5 %fusion.49 = (f32[1024]{0:T(1024)S(1)}, f32[1024,1024]{0,1:T(8,128)S(1)}) fusion(bf16[1024,1024]{1,0:T(8,128)(2,1)S(1)} %maximum_select_fusion, bf16[1024,512]{1,0:T(8,128)(2,1)} %collective-permute-done.1, bf16[1024,512]{1,0:T(8,128)(2,1)S(1)} %copy-done.3, pred[]{:T(512)S(6)} %eq.86, f32[1024]{0:T(1024)S(1)} %bitcast.112, f32[1024]{0:T(1024)S(1)} %add_bitcast_fusion, ...), kind=kOutput, calls=%fused_computation.93 | convolution fusion | flops 2167405568 | bytes 8404993 | tf_op jit(solution)/shard_map/dot_general | solution.py:220
  122.4 0.7 fusion.5
  123.1 1.8 fusion.9
  124.9 25.9 %all-gather.2.cloned.1.call-done = bf16[16,1032,256]{2,1,0:T(8,128)(2,1)} async-done(((bf16[1,1032,256]{2,1,0:T(8,128)(2,1)}), bf16[16,1032,256]{2,1,0:T(8,128)(2,1)}) %all-gather.2.cloned.1.call-update) | async-done | bytes 8454160 | tf_op jit(solution)/shard_map/all_gather | solution.py:134
  150.8 0.8 slice.102
  152.2 5.2 %fusion = f32[1,1032,256]{2,0,1:T(1,128)S(1)} fusion(bf16[16,1032,256]{2,1,0:T(8,128)(2,1)} %all-gather.2.cloned.1.call-done, bf16[1]{0:T(256)(128)(2,1)} %constant.162, bf16[15]{0:T(256)(128)(2,1)S(1)} %slice.92, s32[]{:T(128)S(6)} %add.83), kind=kOutput, calls=%fused_computation | convolution fusion | flops 8454240 | bytes 9510948 | tf_op jit(solution)/shard_map/s,src->rc/dot_general | solution.py:139
  157.5 1.7 fusion.26
  162.5 2.3 %fusion.16 = bf16[1024,256]{1,0:T(8,128)(2,1)S(1)} fusion(f32[1024,256]{1,0:T(8,128)} %fusion.9, f32[1024,256]{1,0:T(8,128)} %fusion.26, bf16[1024,1024]{1,0:T(8,128)(2,1)S(1)} %maximum_select_fusion, f32[1032,256]{1,0:T(8,128)S(1)} %bitcast.102, f32[1024]{0:T(1024)S(1)} %get-tuple-element.5, f32[1024]{0:T(1024)S(1)} %get-tuple-element.6), kind=kOutput, calls=%fused_computation.33 | convolution fusion | flops 538705920 | bytes 5775360 | tf_op jit(solution)/shard_map/dot_general | solution.py:31
  164.8 24.9 %all_to_all.36 = bf16[16,64,256]{2,1,0:T(8,128)(2,1)S(1)} all-to-all(bf16[16,64,256]{2,1,0:T(8,128)(2,1)S(1)} %bitcast.104), channel_id=1, replica_groups=mesh['sx'=4,'sy'=4,'tensor'=16] {'tensor'}, dimensions={0} | all-to-all | bytes 1048576 | tf_op jit(solution)/shard_map/all_to_all | solution.py:239
  192.6 1.2 fusion.25
  (85 shorter events, 10.4 us)
Async XLA Ops:
  11.5 9.3 %copy-start.6 = (s32[1024]{0:T(1024)S(1)}, s32[1024]{0:T(1024)}, u32[]{:S(2)}) copy-start(s32[1024]{0:T(1024)} %param.13) | copy-start | bytes 12292
  11.5 51.8 %all-to-all-start = ((bf16[72,16,768]{2,0,1:T(8,128)(2,1)}), bf16[72,16,768]{2,0,1:T(8,128)(2,1)S(1)}, u32[]{:S(2)}, u32[]{:S(2)}) async-start(bf16[72,16,768]{2,0,1:T(8,128)(2,1)} %fusion.8), calls=%async_computation | async-start | bytes 3538944 | tf_op jit(solution)/shard_map/all_to_all | solution.py:187
  20.8 130.0 %all-gather.2.cloned.1.call-start = ((), (), s32[]{:S(2)}) async-start(), calls=%async_computation.3 | async-start | bytes 8982528 | tf_op jit(solution)/shard_map/all_gather | solution.py:134
  63.4 10.7 %copy-start = (bf16[16,64,768]{2,1,0:T(8,128)(2,1)}, bf16[16,64,768]{2,1,0:T(8,128)(2,1)S(1)}, u32[]{:S(2)}) copy-start(bf16[16,64,768]{2,1,0:T(8,128)(2,1)S(1)} %slice.99) | copy-start | bytes 4718596
  63.5 10.6 %copy-start.2 = (bf16[1024,512]{1,0:T(8,128)(2,1)}, bf16[1024,512]{1,0:T(8,128)(2,1)S(1)}, u32[]{:S(2)}) copy-start(bf16[1024,512]{1,0:T(8,128)(2,1)S(1)} %slice.100) | copy-start | bytes 3145732
  63.5 5.2 %collective-permute-start.1 = (bf16[1024,512]{1,0:T(8,128)(2,1)S(1)}, bf16[1024,512]{1,0:T(8,128)(2,1)}, u32[]{:S(2)}, u32[]{:S(2)}) collective-permute-start(bf16[1024,512]{1,0:T(8,128)(2,1)S(1)} %slice.100), channel_id=1, source_target_pairs={{0,1},{1,0},{2,3},{3,2},{4,5},{5,4},{6,7},{7,6},{8,9},{9,8},{10,11... | collective-permute-start | bytes 3145736 | tf_op jit(solution)/shard_map/ppermute | solution.py:171
  76.9 1.3 copy-start.4
  111.6 2.8 %collective-permute-start = (bf16[1024,512]{1,0:T(8,128)(2,1)S(1)}, bf16[1024,512]{1,0:T(8,128)(2,1)}, u32[]{:S(2)}, u32[]{:S(2)}) collective-permute-start(bf16[1024,512]{1,0:T(8,128)(2,1)S(1)} %bitcast.90), channel_id=1, source_target_pairs={{0,1},{1,0},{2,3},{3,2},{4,5},{5,4},{6,7},{7,6},{8,9},{9,8},{10,11... | collective-permute-start | bytes 3145736 | tf_op jit(solution)/shard_map/ppermute | solution.py:171
  111.6 5.3 %copy-start.3 = (bf16[1024,512]{1,0:T(8,128)(2,1)S(1)}, bf16[1024,512]{1,0:T(8,128)(2,1)}, u32[]{:S(2)}) copy-start(bf16[1024,512]{1,0:T(8,128)(2,1)} %copy-done.2) | copy-start | bytes 3145732
  116.9 5.5 %copy-start.1 = (bf16[16,64,768]{2,1,0:T(8,128)(2,1)S(1)}, bf16[16,64,768]{2,1,0:T(8,128)(2,1)}, u32[]{:S(2)}) copy-start(bf16[16,64,768]{2,1,0:T(8,128)(2,1)} %copy-done) | copy-start | bytes 4718596
  191.6 1.0 copy-start.5
  191.6 1.0 copy-start.7
Sparse Core Ops, SparseCore 0:
  78.3 72.4 all-gather.1
